TPU v7x, 512 devices: a whole 4x4x16 slice. The times are simulated.
512 devices in a mesh: rows: 64 (over x, z), batch: 8 (over y, core).
Axes of the slice: x: 4, y: 4, z: 16, core: 2. Of those that a mesh axis runs over, the one named last changes fastest.
Arguments:
- frames: bfloat16 [16384, 4096], P('rows', 'batch'), may hold values from -40 to 40
- tap_table: int32 [63], replicated, may hold values from -128 to 127
- sketch_matrix: bfloat16 [512, 256], replicated, may hold values from -0.25 to 0.25
- decay_rates: float32 [8, 256], P('batch'), may hold values from 0.5 to 1
Outputs:
- basis: float32 [8, 16384, 256], P('batch', 'rows')
- factor: float32 [8, 256, 256], P('batch')
- coeffs: float32 [8, 256, 512], P('batch')
All inputs are finite; a program needn't handle non-finite values.
Results may differ from a plain program's by a relative error of at most 0.0039.
The roundings to bfloat16 on the way count: a program that leaves them out, or rounds other values in their place, can miss the bound.
Values may be sent and summed in bfloat16 or wider, within the bound.
No kernel may reach another device: no remote copies, remote signals or barrier semaphores. Data moves between devices by JAX's collectives and lax.ppermute only.
A program may use at most 64 MiB of HBM per device.

v0:
```python
import math

import jax
import jax.numpy as jnp
from jax import lax
from jax.sharding import PartitionSpec as P

HIGH = lax.Precision.HIGHEST


def passed_along(x, axis, by):
    length = lax.axis_size(axis)
    pairs = [(i, i + by) for i in range(length) if 0 <= i + by < length]
    return lax.ppermute(x, axis, pairs)


def band_matrix(coefs, rows_count, cols_count, offset):
    row_ids = lax.broadcasted_iota(jnp.int32, (rows_count, cols_count), 0)
    col_ids = lax.broadcasted_iota(jnp.int32, (rows_count, cols_count), 1)
    lag_ids = col_ids - row_ids + offset
    valid = (lag_ids >= 0) & (lag_ids < coefs.shape[0])
    values = jnp.take(coefs, jnp.clip(lag_ids, 0, coefs.shape[0] - 1))
    return jnp.where(valid, values, jnp.zeros_like(values))


def gram_of(block):
    return lax.dot_general(
        block, block, (((0,), (0,)), ((), ())), precision=HIGH, preferred_element_type=jnp.float32
    )


def cross_of(left, right):
    return lax.dot_general(
        left, right, (((0,), (0,)), ((), ())), precision=HIGH, preferred_element_type=jnp.float32
    )


def shards(frames, tap_table, sketch_matrix, decay_rates):
    rows_here, frame_count = frames.shape
    tap_count = tap_table.shape[0]
    npoints = rows_here * lax.axis_size("rows")
    batch_count = lax.axis_size("batch")
    coefs = (tap_table.astype(jnp.float32) / 1024.0).astype(jnp.bfloat16)
    main_band = band_matrix(coefs, frame_count, frame_count, 0)
    hist_band = band_matrix(coefs, tap_count - 1, frame_count, tap_count - 1)
    history = passed_along(frames[:, frame_count - (tap_count - 1) :], "batch", 1)
    filtered = (
        jnp.dot(frames, main_band, preferred_element_type=jnp.float32)
        + jnp.dot(history, hist_band, preferred_element_type=jnp.float32)
    ).astype(jnp.bfloat16)
    sketched = jnp.dot(filtered, sketch_matrix, preferred_element_type=jnp.float32)
    rates = decay_rates[0]

    def one_turn(turn_index, carried):
        return rates[None, :] * passed_along(carried, "batch", 1) + sketched

    weighted = lax.fori_loop(0, batch_count - 1, one_turn, sketched)
    root_points = math.sqrt(npoints)
    rank_count = weighted.shape[1]
    filtered_wide = filtered.astype(jnp.float32)
    lower_one = jnp.linalg.cholesky(lax.psum(gram_of(weighted), "rows"))
    final_q = lax.linalg.triangular_solve(
        lower_one, weighted, left_side=False, lower=True, transpose_a=True
    )
    scaled = final_q * root_points
    partial_proj = cross_of(scaled, filtered_wide)
    projected = lax.psum(partial_proj, "rows") * (math.sqrt(rank_count) / npoints)
    upper = lower_one.T / root_points
    return (scaled[None], upper[None], projected[None])


def solution(mesh):
    placed = (P("rows", "batch"), P(), P(), P("batch", None))
    return jax.shard_map(
        shards,
        mesh=mesh,
        in_specs=placed,
        out_specs=(P("batch", "rows", None), P("batch", None, None), P("batch", None, None)),
        check_vma=False,
    )
```

profile of v0, /device:TPU:24, one launch (start us, length us, event | category | flops | bytes accessed | tf_op | source)
XLA Modules:
  0.0 904.4 jit_solution(605645552439976620)
XLA Ops:
  8.2 1.9 collective-permute-start.1
  14.0 41.2 %fusion.190 = f32[512,256]{1,0:T(8,128)S(1)} fusion(bf16[256,512]{1,0:T(8,128)(2,1)S(1)} %copy-done.3, bf16[]{:T(256)} %bitcast.113, bf16[]{:T(256)} %bitcast.114, bf16[]{:T(256)} %bitcast.115, bf16[]{:T(256)} %bitcast.116, bf16[]{:T(256)} %bitcast.117, bf16[]{:T(256)} %bitcast.119, bf16[]{:T(256)} %bitcast.118, bf16[]{:T(256)} %bitcast.2, bf16[]{:T(256)} %bitcast.4, ...), kind=kOutput, calls=%fused_computation.200 | convolution fusion | flops 171442176 | bytes 786558 | tf_op jit(solution)/shard_map/dot_general | solution.py:48
  55.2 185.6 %gather_fusion = bf16[31744]{0:T(1024)(128)(2,1)S(1)} fusion(bf16[63]{0:T(256)(128)(2,1)S(1)} %multiply_convert_fusion, s32[31744]{0:T(1024)S(1)} %broadcast_clamp_fusion), kind=kCustom, calls=%fused_computation | custom fusion | bytes 253952 | tf_op jit(solution)/shard_map/jit(_take)/gather | solution.py:22
  242.1 54.2 %while.11 = (s32[]{:T(128)}, f32[256,256]{1,0:T(8,128)S(1)}, f32[1,256]{1,0:T(1,128)S(1)}, f32[256,256]{1,0:T(8,128)S(1)}, s32[]{:T(128)}) while((s32[]{:T(128)}, f32[256,256]{1,0:T(8,128)S(1)}, f32[1,256]{1,0:T(1,128)S(1)}, f32[256,256]{1,0:T(8,128)S(1)}, s32[]{:T(128)}) %tuple.112), condition=%wide.region_1.2_spmd, body=%wide.region_0.1_spmd.sunk | while | flops 131074 | bytes 1836133 | solution.py:57
  244.1 5.8 collective-permute-done
  249.9 1.9 collective-permute-start
  251.8 5.8 collective-permute-done
  257.6 1.9 collective-permute-start
  259.5 5.8 collective-permute-done
  265.4 1.9 collective-permute-start
  267.3 5.8 collective-permute-done
  273.1 1.9 collective-permute-start
  275.0 5.8 collective-permute-done
  280.8 1.9 collective-permute-start
  282.8 5.8 collective-permute-done
  288.6 1.9 collective-permute-start
  290.5 5.8 collective-permute-done
  297.9 270.9 %all-reduce.4.cloned.1.call-done = f32[256,256]{0,1:T(8,128)} async-done(((f32[256,256]{0,1:T(8,128)}), f32[256,256]{0,1:T(8,128)}) %all-reduce.4.cloned.1.call-update) | async-done | bytes 262160 | tf_op jit(solution)/shard_map/psum | solution.py:61
  570.0 11.7 %cholesky.50 = f32[128,128]{1,0:T(8,128)S(1)} custom-call(f32[128,128]{1,0:T(8,128)S(1)} %cholesky.118), custom_call_target="Cholesky" | custom-call | tf_op jit(solution)/shard_map/jit(cholesky)/cholesky | solution.py:61
  581.8 9.8 %custom-call.14 = f32[1,128,128]{1,2,0:T(8,128)S(1)} custom-call(f32[1,128,128]{2,1,0:T(8,128)S(1)} %get-tuple-element.63), custom_call_target="InvertDiagBlocksLowerTriangular" | custom-call | tf_op jit(solution)/shard_map/jit(cholesky)/cholesky | solution.py:61
  592.0 11.7 %cholesky.105 = f32[128,128]{1,0:T(8,128)S(1)} custom-call(f32[128,128]{1,0:T(8,128)S(1)} %convolution_subtract_fusion.1), custom_call_target="Cholesky" | custom-call | tf_op jit(solution)/shard_map/jit(cholesky)/cholesky | solution.py:61
  605.9 4.2 while.12
  610.0 19.7 %custom-call.15 = f32[2,128,128]{1,2,0:T(8,128)S(1)} custom-call(f32[2,128,128]{2,1,0:T(8,128)S(1)} %get-tuple-element.33), custom_call_target="InvertDiagBlocksLowerTriangular" | custom-call | tf_op jit(solution)/shard_map/triangular_solve | solution.py:62
  633.7 262.0 %all-reduce.6.cloned.1.call-done = f32[256,512]{1,0:T(8,128)} async-done(((f32[256,512]{1,0:T(8,128)}), f32[256,512]{1,0:T(8,128)}) %all-reduce.6.cloned.1.call-update) | async-done | bytes 524304 | tf_op jit(solution)/shard_map/psum | solution.py:67
  (64 shorter events, 22.0 us)
Async XLA Ops:
  7.2 234.0 %copy-start = (bf16[512,256]{1,0:T(8,128)(2,1)S(1)}, bf16[512,256]{1,0:T(8,128)(2,1)}, u32[]{:S(2)}) copy-start(bf16[512,256]{1,0:T(8,128)(2,1)} %param.8) | copy-start | bytes 786436
  7.2 2.9 copy-start.4
  7.2 561.6 %all-reduce.4.cloned.1.call-start = ((), (), s32[]{:S(2)}) async-start(), calls=%async_computation | async-start | bytes 524288 | tf_op jit(solution)/shard_map/psum | solution.py:61
  8.2 232.7 %collective-permute-start.1 = (bf16[256,62]{1,0:T(8,128)(2,1)S(1)}, bf16[256,62]{1,0:T(8,128)(2,1)S(1)}, u32[]{:S(2)}, u32[]{:S(2)}) collective-permute-start(bf16[256,62]{1,0:T(8,128)(2,1)S(1)} %slice.45), channel_id=1, source_target_pairs={{0,1},{1,2},{2,3},{3,4},{4,5},{5,6},{6,7},{8,9},{9,10},{10,11},{11... | collective-permute-start | bytes 95240 | tf_op jit(solution)/shard_map/ppermute | solution.py:14
  13.0 1.0 copy-start.3
  241.5 0.7 copy-start.2
  242.1 7.7 collective-permute-start
  249.9 7.7 collective-permute-start
  257.6 7.7 collective-permute-start
  265.4 7.7 collective-permute-start
  273.1 7.7 collective-permute-start
  280.8 7.7 collective-permute-start
  288.6 7.7 collective-permute-start
  297.7 598.1 %all-reduce.6.cloned.1.call-start = ((), (), s32[]{:S(2)}) async-start(), calls=%async_computation.1 | async-start | bytes 1048576 | tf_op jit(solution)/shard_map/psum | solution.py:67
  568.8 1.2 copy-start.1
Sparse Core Ops, SparseCore 0:
  297.8 270.9 all-reduce.3
  632.1 263.5 all-reduce.5
where the time goes:
time: 906 us; the launch traced here: 904 us
  waiting for transfers between devices  573 us (63%)
  local copies, waits for them, and re-layouts  198 us (22%)
  other arithmetic  55.9 us (6%)
  matrix products  45.7 us (5%)
  starting transfers between devices  15.6 us (2%)
  between operations  15.6 us (2%)
    psum x1, waiting for transfers between devices, shards(): lower_one = jnp.linalg.cholesky(lax.psum(gram_of(weighted), 'rows'))  271 us
    psum x1, waiting for transfers between devices, shards(): lax.psum(partial_proj, 'rows') * (math.sqrt(rank_count) / npoints)  262 us
    gather x6, local copies, waits for them, and re-layouts, band_matrix(): values = jnp.take(coefs, jnp.clip(lag_ids, 0, coefs.shape[0] - 1))  189 us
    dot_general x1, matrix products, shards(): jnp.dot(frames, main_band, preferred_element_type=jnp.float32)  41.2 us
    ppermute x8, waiting for transfers between devices, passed_along(): return lax.ppermute(x, axis, pairs)  40.3 us
    another operation x6, other arithmetic, shards(): lower_one = jnp.linalg.cholesky(lax.psum(gram_of(weighted), 'rows'))  33.9 us
    another operation x2, other arithmetic, shards(): lax.linalg.triangular_solve(lower_one, weighted, left_side=False, lower=T...  19.7 us
  transfers between devices with their start and end apart: 10, of which 9 were waited for; matrix products, arithmetic and copies ran while one was open for 26% of the time, Pallas kernels for 0%

commit v1 on v0

v1 whole, which is shorter than its diff:
```python
import math

import jax
import jax.numpy as jnp
from jax import lax
from jax.sharding import Mesh
from jax.sharding import PartitionSpec as P

HIGH = lax.Precision.HIGHEST
ROWS = ("x", "z")
BATCH = ("y", "core")
BLOCK = 128


def shifted(x, axis, by):
    length = lax.axis_size(axis)
    pairs = [(i, i + by) for i in range(length) if 0 <= i + by < length]
    return lax.ppermute(x, axis, pairs)


def band_block(coefs, offset):
    row_ids = lax.broadcasted_iota(jnp.int32, (BLOCK, BLOCK), 0)
    col_ids = lax.broadcasted_iota(jnp.int32, (BLOCK, BLOCK), 1)
    lag_ids = col_ids - row_ids + offset
    block = jnp.zeros((BLOCK, BLOCK), jnp.float32)
    for k in range(coefs.shape[0]):
        block = jnp.where(lag_ids == k, coefs[k], block)
    return block.astype(jnp.bfloat16)


def halve(cur):
    if cur.shape[0] > 8:
        h = cur.shape[0] // 2
        return cur[:h], cur[h:], 0
    h = cur.shape[1] // 2
    return cur[:, :h], cur[:, h:], 1


def reduce_rows(x):
    sizes = {a: lax.axis_size(a) for a in ROWS}
    rounds = []
    d = 1
    while d < max(sizes.values()):
        for a in ROWS:
            if d < sizes[a]:
                rounds.append((a, d))
        d *= 2
    cur = x
    kept = []
    for a, d in rounds:
        bit = (lax.axis_index(a) // d) % 2 == 1
        lo, hi, dim = halve(cur)
        keep = jnp.where(bit, hi, lo)
        send = jnp.where(bit, lo, hi)
        pairs = [(i, i ^ d) for i in range(sizes[a])]
        cur = keep + lax.ppermute(send, a, pairs)
        kept.append(dim)
    for (a, d), dim in zip(reversed(rounds), reversed(kept)):
        bit = (lax.axis_index(a) // d) % 2 == 1
        pairs = [(i, i ^ d) for i in range(sizes[a])]
        other = lax.ppermute(cur, a, pairs)
        cur = jnp.where(
            bit,
            jnp.concatenate([other, cur], axis=dim),
            jnp.concatenate([cur, other], axis=dim),
        )
    return cur


def shards(frames, tap_table, sketch_matrix, decay_rates):
    rows_here, frame_count = frames.shape
    npoints = rows_here * math.prod(lax.axis_size(a) for a in ROWS)
    batch_count = lax.axis_size(BATCH)
    coefs = (tap_table.astype(jnp.float32) / 1024.0).astype(jnp.bfloat16).astype(jnp.float32)
    inner = band_block(coefs, 0)
    carry = band_block(coefs, BLOCK)
    nblocks = frame_count // BLOCK
    zero = jnp.zeros((BLOCK, BLOCK), jnp.bfloat16)
    main_band = jnp.block(
        [[inner if j == i else (carry if j == i + 1 else zero) for j in range(nblocks)] for i in range(nblocks)]
    )
    history = shifted(frames[:, frame_count - BLOCK :], BATCH, 1)
    main = jnp.dot(frames, main_band, preferred_element_type=jnp.float32)
    edge = jnp.dot(history, carry, preferred_element_type=jnp.float32)
    filtered = (main + jnp.pad(edge, ((0, 0), (0, frame_count - BLOCK)))).astype(jnp.bfloat16)
    sketched = jnp.dot(filtered, sketch_matrix, preferred_element_type=jnp.float32)

    weighted = sketched
    factor = decay_rates[0]
    d = 1
    while d < batch_count:
        got_w, got_f = shifted((weighted, factor), BATCH, d)
        weighted = weighted + factor[None, :] * got_w
        factor = factor * got_f
        d *= 2

    root_points = math.sqrt(npoints)
    rank_count = weighted.shape[1]
    both = jnp.concatenate([weighted, filtered.astype(jnp.float32)], axis=1)
    partial = lax.dot_general(
        weighted, both, (((0,), (0,)), ((), ())), precision=HIGH, preferred_element_type=jnp.float32
    )
    summed = reduce_rows(partial)
    gram = summed[:, :rank_count]
    cross = summed[:, rank_count:]
    lower_one = jnp.linalg.cholesky(gram)
    inverse = lax.linalg.triangular_solve(
        lower_one, jnp.eye(rank_count, dtype=jnp.float32), left_side=True, lower=True
    )
    scaled = jnp.dot(weighted, inverse.T, precision=HIGH) * root_points
    projected = jnp.dot(inverse, cross, precision=HIGH) * (math.sqrt(rank_count) / root_points)
    upper = lower_one.T / root_points
    return (scaled[None], upper[None], projected[None])


def solution(mesh):
    rows_n, batch_n = mesh.devices.shape
    along_x = len({d.coords[0] for d in mesh.devices.flat})
    along_y = len({d.coords[1] for d in mesh.devices.flat})
    devices = mesh.devices.reshape(along_x, rows_n // along_x, along_y, batch_n // along_y)
    fine = Mesh(devices, ("x", "z", "y", "core"))
    placed = (P(ROWS, BATCH), P(), P(), P(BATCH, None))
    return jax.shard_map(
        shards,
        mesh=fine,
        in_specs=placed,
        out_specs=(P(BATCH, ROWS, None), P(BATCH, None, None), P(BATCH, None, None)),
        check_vma=False,
    )
```

time: 906 us -> 307 us (0.34)
  waiting for transfers between devices: 573 us -> 70.8 us
  local copies, waits for them, and re-layouts: 198 us -> 9.14 us
  other arithmetic: 55.9 us -> 134 us
  starting transfers between devices: 15.6 us -> 82 us
  matrix products: 45.7 us -> 5.66 us
  between operations: 15.6 us -> 2.59 us
    psum x2 -> x0, waiting for transfers between devices: 533 us -> none  [the longest x1 271 us: shards(): lower_one = jnp.linalg.cholesky(lax.psum(gram_of(weighted), 'rows'))]
    gather x6 -> x0, local copies, waits for them, and re-layouts: 189 us -> none  [band_matrix(): values = jnp.take(coefs, jnp.clip(lag_ids, 0, coefs.shape[0] - 1))]
    convert_element_type x1 -> x3, other arithmetic: 0.01 us -> 79.1 us  [the longest x2 79.1 us: band_block(): return block.astype(jnp.bfloat16)]
    ppermute x8 -> x18, starting transfers between devices: 15.4 us -> 82 us  [the longest x6 42.5 us: reduce_rows(): cur = keep + lax.ppermute(send, a, pairs)]
    dot_general x4 -> x5, matrix products: 44 us -> 4.08 us  [the longest x1 1.42 us: shards(): jnp.dot(inverse, cross, precision=HIGH)]
    ppermute x8 -> x18, waiting for transfers between devices: 40.3 us -> 70.8 us  [the longest x6 34.4 us: reduce_rows(): other = lax.ppermute(cur, a, pairs)]
  transfers between devices with their start and end apart: 10 -> 18, of which waited for: 9 -> 17; matrix products, arithmetic and copies ran while one was open for 26% -> 27% of each run, Pallas kernels for 0% -> 0%
where the time goes in v1:
time: 307 us; the launch traced here: 304 us
  other arithmetic  134 us (44%)
  starting transfers between devices  82 us (27%)
  waiting for transfers between devices  70.8 us (23%)
  local copies, waits for them, and re-layouts  9.14 us (3%)
  matrix products  5.66 us (2%)
    convert_element_type x2, other arithmetic, band_block(): return block.astype(jnp.bfloat16)  79.1 us
    ppermute x6, starting transfers between devices, reduce_rows(): cur = keep + lax.ppermute(send, a, pairs)  42.5 us
    ppermute x6, waiting for transfers between devices, reduce_rows(): other = lax.ppermute(cur, a, pairs)  34.4 us
    another operation x6, other arithmetic, shards(): lower_one = jnp.linalg.cholesky(gram)  33.9 us
    ppermute x6, starting transfers between devices, reduce_rows(): other = lax.ppermute(cur, a, pairs)  29.9 us
    another operation x2, other arithmetic, shards(): lax.linalg.triangular_solve(lower_one, jnp.eye(rank_count, dtype=jnp.floa...  19.7 us
    ppermute x6, waiting for transfers between devices, reduce_rows(): cur = keep + lax.ppermute(send, a, pairs)  18.4 us
    ppermute x6, waiting for transfers between devices, shifted(): return lax.ppermute(x, axis, pairs)  18 us
  transfers between devices with their start and end apart: 18, of which 17 were waited for; matrix products, arithmetic and copies ran while one was open for 27% of the time, Pallas kernels for 0%

profile of v1, /device:TPU:24, one launch (start us, length us, event | category | flops | bytes accessed | tf_op | source)
XLA Modules:
  0.0 304.5 jit_solution(12940177982096644401)
XLA Ops:
  6.4 39.5 %select_convert_fusion = bf16[128,128]{1,0:T(8,128)(2,1)S(1)} fusion(bf16[]{:T(256)} %bitcast.62, bf16[]{:T(256)} %bitcast.61, bf16[]{:T(256)} %bitcast.60, bf16[]{:T(256)} %bitcast.59, bf16[]{:T(256)} %bitcast.58, bf16[]{:T(256)} %bitcast.57, bf16[]{:T(256)} %bitcast.56, bf16[]{:T(256)} %bitcast.55, bf16[]{:T(256)} %bitcast.54, bf16[]{:T(256)} %bitcast.53, ...), kind=kLoop, calls=%fused_computation.84 | loop fusion | flops 2097152 | bytes 32894 | tf_op jit(solution)/shard_map/convert_element_type | solution.py:28
  45.9 39.6 %select_convert_fusion.1 = bf16[128,128]{1,0:T(8,128)(2,1)S(1)} fusion(bf16[]{:T(256)} %bitcast.62, bf16[]{:T(256)} %bitcast.61, bf16[]{:T(256)} %bitcast.60, bf16[]{:T(256)} %bitcast.59, bf16[]{:T(256)} %bitcast.58, bf16[]{:T(256)} %bitcast.57, bf16[]{:T(256)} %bitcast.56, bf16[]{:T(256)} %bitcast.55, bf16[]{:T(256)} %bitcast.54, bf16[]{:T(256)} %bitcast.53, ...), kind=kLoop, calls=%fused_computation.85 | loop fusion | flops 2080768 | bytes 32894 | tf_op jit(solution)/shard_map/convert_element_type | solution.py:28
  88.3 5.8 %collective-permute-done.1 = f32[256,256]{0,1:T(8,128)S(1)} collective-permute-done((f32[256,256]{0,1:T(8,128)S(1)}, f32[256,256]{0,1:T(8,128)S(1)}, u32[]{:S(2)}, u32[]{:S(2)}) %collective-permute-start.1) | collective-permute-done | bytes 262176 | tf_op jit(solution)/shard_map/ppermute | solution.py:18
  105.1 4.2 %collective-permute-done.4 = f32[256]{0:T(256)S(1)} collective-permute-done((f32[256]{0:T(256)S(1)}, f32[256]{0:T(256)S(1)}, u32[]{:S(2)}, u32[]{:S(2)}) %collective-permute-start.4) | collective-permute-done | bytes 1056 | tf_op jit(solution)/shard_map/ppermute | solution.py:18
  116.7 6.2 %collective-permute-done.6 = f32[128,768]{1,0:T(8,128)S(1)} collective-permute-done((f32[128,768]{1,0:T(8,128)S(1)}, f32[128,768]{1,0:T(8,128)S(1)}, u32[]{:S(2)}, u32[]{:S(2)}) %collective-permute-start.6) | collective-permute-done | bytes 393248 | tf_op jit(solution)/shard_map/ppermute | solution.py:56
  123.0 3.8 %collective-permute-start.7 = (f32[64,768]{1,0:T(8,128)S(1)}, f32[64,768]{1,0:T(8,128)S(1)}, u32[]{:S(2)}, u32[]{:S(2)}) collective-permute-start(f32[64,768]{1,0:T(8,128)S(1)} %slice_select_fusion.1), channel_id=1, source_target_pairs={{0,8},{8,0},{16,24},{24,16},{32,40},{40,32},{48,56},{56,48},{64,72... | collective-permute-start | bytes 589832 | tf_op jit(solution)/shard_map/ppermute | solution.py:56
  126.9 3.7 %collective-permute-done.7 = f32[64,768]{1,0:T(8,128)S(1)} collective-permute-done((f32[64,768]{1,0:T(8,128)S(1)}, f32[64,768]{1,0:T(8,128)S(1)}, u32[]{:S(2)}, u32[]{:S(2)}) %collective-permute-start.7) | collective-permute-done | bytes 196640 | tf_op jit(solution)/shard_map/ppermute | solution.py:56
  130.7 4.9 %collective-permute-start.8 = (f32[32,768]{1,0:T(8,128)S(1)}, f32[32,768]{1,0:T(8,128)S(1)}, u32[]{:S(2)}, u32[]{:S(2)}) collective-permute-start(f32[32,768]{1,0:T(8,128)S(1)} %slice_select_fusion.2), channel_id=1, source_target_pairs={{0,256},{128,384},{256,0},{384,128},{1,257},{129,385},{257,1},{385... | collective-permute-start | bytes 294920 | tf_op jit(solution)/shard_map/ppermute | solution.py:56
  138.7 5.2 %collective-permute-start.9 = (f32[16,768]{1,0:T(8,128)S(1)}, f32[16,768]{1,0:T(8,128)S(1)}, u32[]{:S(2)}, u32[]{:S(2)}) collective-permute-start(f32[16,768]{1,0:T(8,128)S(1)} %slice_select_fusion.3), channel_id=1, source_target_pairs={{0,16},{8,24},{16,0},{24,8},{32,48},{40,56},{48,32},{56,40},{64,80... | collective-permute-start | bytes 147464 | tf_op jit(solution)/shard_map/ppermute | solution.py:56
  146.0 9.4 %collective-permute-start.10 = (f32[8,768]{1,0:T(8,128)S(1)}, f32[8,768]{1,0:T(8,128)S(1)}, u32[]{:S(2)}, u32[]{:S(2)}) collective-permute-start(f32[8,768]{1,0:T(8,128)S(1)} %slice_select_fusion.4), channel_id=1, source_target_pairs={{0,32},{8,40},{16,48},{24,56},{32,0},{40,8},{48,16},{56,24},{64,96... | collective-permute-start | bytes 73736 | tf_op jit(solution)/shard_map/ppermute | solution.py:56
  157.2 15.7 %collective-permute-start.11 = (f32[8,384]{1,0:T(8,128)S(1)}, f32[8,384]{1,0:T(8,128)S(1)}, u32[]{:S(2)}, u32[]{:S(2)}) collective-permute-start(f32[8,384]{1,0:T(8,128)S(1)} %slice_select_fusion.5), channel_id=1, source_target_pairs={{0,64},{8,72},{16,80},{24,88},{32,96},{40,104},{48,112},{56,120},{... | collective-permute-start | bytes 36872 | tf_op jit(solution)/shard_map/ppermute | solution.py:56
  174.6 12.6 %collective-permute-start.12 = (f32[8,384]{1,0:T(8,128)S(1)}, f32[8,384]{1,0:T(8,128)S(1)}, u32[]{:S(2)}, u32[]{:S(2)}) collective-permute-start(f32[8,384]{1,0:T(8,128)S(1)} %select_add_fusion.5), channel_id=1, source_target_pairs={{0,64},{8,72},{16,80},{24,88},{32,96},{40,104},{48,112},{56,120},{... | collective-permute-start | bytes 36872 | tf_op jit(solution)/shard_map/ppermute | solution.py:61
  188.9 4.8 %collective-permute-start.13 = (f32[8,768]{1,0:T(8,128)S(1)}, f32[8,768]{1,0:T(8,128)S(1)}, u32[]{:S(2)}, u32[]{:S(2)}) collective-permute-start(f32[8,768]{1,0:T(8,128)S(1)} %maximum_select_fusion.4), channel_id=1, source_target_pairs={{0,32},{8,40},{16,48},{24,56},{32,0},{40,8},{48,16},{56,24},{64,96... | collective-permute-start | bytes 73736 | tf_op jit(solution)/shard_map/ppermute | solution.py:61
  193.7 5.2 %collective-permute-done.13 = f32[8,768]{1,0:T(8,128)S(1)} collective-permute-done((f32[8,768]{1,0:T(8,128)S(1)}, f32[8,768]{1,0:T(8,128)S(1)}, u32[]{:S(2)}, u32[]{:S(2)}) %collective-permute-start.13) | collective-permute-done | bytes 24608 | tf_op jit(solution)/shard_map/ppermute | solution.py:61
  201.0 5.2 %collective-permute-done.14 = f32[16,768]{1,0:T(8,128)S(1)} collective-permute-done((f32[16,768]{1,0:T(8,128)S(1)}, f32[16,768]{1,0:T(8,128)S(1)}, u32[]{:S(2)}, u32[]{:S(2)}) %collective-permute-start.14) | collective-permute-done | bytes 49184 | tf_op jit(solution)/shard_map/ppermute | solution.py:61
  206.5 4.9 %collective-permute-start.15 = (f32[32,768]{0,1:T(8,128)S(1)}, f32[32,768]{0,1:T(8,128)S(1)}, u32[]{:S(2)}, u32[]{:S(2)}) collective-permute-start(f32[32,768]{0,1:T(8,128)S(1)} %broadcast_select_fusion), channel_id=1, source_target_pairs={{0,256},{128,384},{256,0},{384,128},{1,257},{129,385},{257,1},{385... | collective-permute-start | bytes 294920 | tf_op jit(solution)/shard_map/ppermute | solution.py:61
  211.5 8.7 %collective-permute-done.15 = f32[32,768]{0,1:T(8,128)S(1)} collective-permute-done((f32[32,768]{0,1:T(8,128)S(1)}, f32[32,768]{0,1:T(8,128)S(1)}, u32[]{:S(2)}, u32[]{:S(2)}) %collective-permute-start.15) | collective-permute-done | bytes 98336 | tf_op jit(solution)/shard_map/ppermute | solution.py:61
  222.3 7.7 %collective-permute-done.16 = f32[64,768]{0,1:T(8,128)S(1)} collective-permute-done((f32[64,768]{0,1:T(8,128)S(1)}, f32[64,768]{0,1:T(8,128)S(1)}, u32[]{:S(2)}, u32[]{:S(2)}) %collective-permute-start.16) | collective-permute-done | bytes 196640 | tf_op jit(solution)/shard_map/ppermute | solution.py:61
  234.0 6.0 %collective-permute-done.17 = f32[128,768]{0,1:T(8,128)S(1)} collective-permute-done((f32[128,768]{0,1:T(8,128)S(1)}, f32[128,768]{0,1:T(8,128)S(1)}, u32[]{:S(2)}, u32[]{:S(2)}) %collective-permute-start.17) | collective-permute-done | bytes 393248 | tf_op jit(solution)/shard_map/ppermute | solution.py:61
  240.3 11.7 %cholesky.45 = f32[128,128]{1,0:T(8,128)S(1)} custom-call(f32[128,128]{1,0:T(8,128)S(1)} %cholesky.107), custom_call_target="Cholesky" | custom-call | tf_op jit(solution)/shard_map/jit(cholesky)/cholesky | solution.py:106
  252.1 9.8 %custom-call.14 = f32[1,128,128]{1,2,0:T(8,128)S(1)} custom-call(f32[1,128,128]{2,1,0:T(8,128)S(1)} %get-tuple-element.34), custom_call_target="InvertDiagBlocksLowerTriangular" | custom-call | tf_op jit(solution)/shard_map/jit(cholesky)/cholesky | solution.py:106
  262.4 11.7 %cholesky.94 = f32[128,128]{1,0:T(8,128)S(1)} custom-call(f32[128,128]{1,0:T(8,128)S(1)} %convolution_subtract_fusion.1), custom_call_target="Cholesky" | custom-call | tf_op jit(solution)/shard_map/jit(cholesky)/cholesky | solution.py:106
  276.2 4.2 %while.1 = (s32[]{:T(128)}, f32[256,256]{1,0:T(8,128)S(1)}, s32[2,2]{1,0:T(2,128)S(1)}, f32[2,128,128]{2,1,0:T(8,128)S(1)}, s32[]{:T(128)}) while((s32[]{:T(128)}, f32[256,256]{1,0:T(8,128)S(1)}, s32[2,2]{1,0:T(2,128)S(1)}, f32[2,128,128]{2,1,0:T(8,128)S(1)}, s32[]{:T(128)}) %tuple.91), condition=%wide.while_cond, body=%wide.while_body.sunk | while | flops 2 | bytes 131189 | solution.py:107
  280.4 19.7 %custom-call.15 = f32[2,128,128]{1,2,0:T(8,128)S(1)} custom-call(f32[2,128,128]{2,1,0:T(8,128)S(1)} %get-tuple-element.10), custom_call_target="InvertDiagBlocksLowerTriangular" | custom-call | tf_op jit(solution)/shard_map/triangular_solve | solution.py:107
  (91 shorter events, 55.7 us)
Async XLA Ops:
  0.6 85.4 %copy-start = (bf16[512,256]{1,0:T(8,128)(2,1)S(1)}, bf16[512,256]{1,0:T(8,128)(2,1)}, u32[]{:S(2)}) copy-start(bf16[512,256]{1,0:T(8,128)(2,1)} %param.6) | copy-start | bytes 786436
  0.6 2.8 copy-start.3
  1.5 83.9 %collective-permute-start = (bf16[256,128]{1,0:T(8,128)(2,1)S(1)}, bf16[256,128]{1,0:T(8,128)(2,1)S(1)}, u32[]{:S(2)}, u32[]{:S(2)}) collective-permute-start(bf16[256,128]{1,0:T(8,128)(2,1)S(1)} %slice.403), channel_id=1, source_target_pairs={{0,1},{1,2},{2,3},{3,4},{4,5},{5,6},{6,7},{8,9},{9,10},{10,11},{11... | collective-permute-start | bytes 196616 | tf_op jit(solution)/shard_map/ppermute | solution.py:18
  6.3 79.3 %copy-start.1 = (bf16[256,512]{1,0:T(8,128)(2,1)S(1)}, bf16[256,512]{1,0:T(8,128)(2,1)}, u32[]{:S(2)}) copy-start(bf16[256,512]{1,0:T(8,128)(2,1)} %param.4) | copy-start | bytes 786436
  86.3 7.7 %copy-start.2 = (f32[1,256]{1,0:T(1,128)S(1)}, f32[1,256]{1,0:T(1,128)}, u32[]{:S(2)}) copy-start(f32[1,256]{1,0:T(1,128)} %param.7) | copy-start | bytes 3076
  86.3 7.7 %collective-permute-start.1 = (f32[256,256]{0,1:T(8,128)S(1)}, f32[256,256]{0,1:T(8,128)S(1)}, u32[]{:S(2)}, u32[]{:S(2)}) collective-permute-start(f32[256,256]{0,1:T(8,128)S(1)} %fusion.175), channel_id=1, source_target_pairs={{0,1},{1,2},{2,3},{3,4},{4,5},{5,6},{6,7},{8,9},{9,10},{10,11},{11... | collective-permute-start | bytes 786440 | tf_op jit(solution)/shard_map/ppermute | solution.py:18
  94.1 8.3 %collective-permute-start.3 = (f32[256,256]{0,1:T(8,128)S(1)}, f32[256,256]{0,1:T(8,128)S(1)}, u32[]{:S(2)}, u32[]{:S(2)}) collective-permute-start(f32[256,256]{0,1:T(8,128)S(1)} %multiply_add_fusion.2), channel_id=1, source_target_pairs={{0,2},{1,3},{2,4},{3,5},{4,6},{5,7},{8,10},{9,11},{10,12},{11,13},... | collective-permute-start | bytes 786440 | tf_op jit(solution)/shard_map/ppermute | solution.py:18
  95.4 4.9 %collective-permute-start.2 = (f32[256]{0:T(256)S(1)}, f32[256]{0:T(256)S(1)}, u32[]{:S(2)}, u32[]{:S(2)}) collective-permute-start(f32[256]{0:T(256)S(1)} %bitcast.114), channel_id=1, source_target_pairs={{0,1},{1,2},{2,3},{3,4},{4,5},{5,6},{6,7},{8,9},{9,10},{10,11},{11... | collective-permute-start | bytes 3080 | tf_op jit(solution)/shard_map/ppermute | solution.py:18
  102.5 9.8 %collective-permute-start.5 = (f32[256,256]{0,1:T(8,128)S(1)}, f32[256,256]{0,1:T(8,128)S(1)}, u32[]{:S(2)}, u32[]{:S(2)}) collective-permute-start(f32[256,256]{0,1:T(8,128)S(1)} %multiply_add_fusion.1), channel_id=1, source_target_pairs={{0,4},{1,5},{2,6},{3,7},{8,12},{9,13},{10,14},{11,15},{16,20},{17,... | collective-permute-start | bytes 786440 | tf_op jit(solution)/shard_map/ppermute | solution.py:18
  103.8 5.5 %collective-permute-start.4 = (f32[256]{0:T(256)S(1)}, f32[256]{0:T(256)S(1)}, u32[]{:S(2)}, u32[]{:S(2)}) collective-permute-start(f32[256]{0:T(256)S(1)} %mul.44), channel_id=1, source_target_pairs={{0,2},{1,3},{2,4},{3,5},{4,6},{5,7},{8,10},{9,11},{10,12},{11,13},... | collective-permute-start | bytes 3080 | tf_op jit(solution)/shard_map/ppermute | solution.py:18
  113.3 9.7 %collective-permute-start.6 = (f32[128,768]{1,0:T(8,128)S(1)}, f32[128,768]{1,0:T(8,128)S(1)}, u32[]{:S(2)}, u32[]{:S(2)}) collective-permute-start(f32[128,768]{1,0:T(8,128)S(1)} %slice_select_fusion), channel_id=1, source_target_pairs={{0,128},{128,0},{256,384},{384,256},{1,129},{129,1},{257,385},{385... | collective-permute-start | bytes 1179656 | tf_op jit(solution)/shard_map/ppermute | solution.py:56
  123.0 7.6 %collective-permute-start.7 = (f32[64,768]{1,0:T(8,128)S(1)}, f32[64,768]{1,0:T(8,128)S(1)}, u32[]{:S(2)}, u32[]{:S(2)}) collective-permute-start(f32[64,768]{1,0:T(8,128)S(1)} %slice_select_fusion.1), channel_id=1, source_target_pairs={{0,8},{8,0},{16,24},{24,16},{32,40},{40,32},{48,56},{56,48},{64,72... | collective-permute-start | bytes 589832 | tf_op jit(solution)/shard_map/ppermute | solution.py:56
  130.7 8.0 %collective-permute-start.8 = (f32[32,768]{1,0:T(8,128)S(1)}, f32[32,768]{1,0:T(8,128)S(1)}, u32[]{:S(2)}, u32[]{:S(2)}) collective-permute-start(f32[32,768]{1,0:T(8,128)S(1)} %slice_select_fusion.2), channel_id=1, source_target_pairs={{0,256},{128,384},{256,0},{384,128},{1,257},{129,385},{257,1},{385... | collective-permute-start | bytes 294920 | tf_op jit(solution)/shard_map/ppermute | solution.py:56
  138.7 7.2 %collective-permute-start.9 = (f32[16,768]{1,0:T(8,128)S(1)}, f32[16,768]{1,0:T(8,128)S(1)}, u32[]{:S(2)}, u32[]{:S(2)}) collective-permute-start(f32[16,768]{1,0:T(8,128)S(1)} %slice_select_fusion.3), channel_id=1, source_target_pairs={{0,16},{8,24},{16,0},{24,8},{32,48},{40,56},{48,32},{56,40},{64,80... | collective-permute-start | bytes 147464 | tf_op jit(solution)/shard_map/ppermute | solution.py:56
  146.0 11.2 %collective-permute-start.10 = (f32[8,768]{1,0:T(8,128)S(1)}, f32[8,768]{1,0:T(8,128)S(1)}, u32[]{:S(2)}, u32[]{:S(2)}) collective-permute-start(f32[8,768]{1,0:T(8,128)S(1)} %slice_select_fusion.4), channel_id=1, source_target_pairs={{0,32},{8,40},{16,48},{24,56},{32,0},{40,8},{48,16},{56,24},{64,96... | collective-permute-start | bytes 73736 | tf_op jit(solution)/shard_map/ppermute | solution.py:56
  157.2 17.3 %collective-permute-start.11 = (f32[8,384]{1,0:T(8,128)S(1)}, f32[8,384]{1,0:T(8,128)S(1)}, u32[]{:S(2)}, u32[]{:S(2)}) collective-permute-start(f32[8,384]{1,0:T(8,128)S(1)} %slice_select_fusion.5), channel_id=1, source_target_pairs={{0,64},{8,72},{16,80},{24,88},{32,96},{40,104},{48,112},{56,120},{... | collective-permute-start | bytes 36872 | tf_op jit(solution)/shard_map/ppermute | solution.py:56
  174.6 14.3 %collective-permute-start.12 = (f32[8,384]{1,0:T(8,128)S(1)}, f32[8,384]{1,0:T(8,128)S(1)}, u32[]{:S(2)}, u32[]{:S(2)}) collective-permute-start(f32[8,384]{1,0:T(8,128)S(1)} %select_add_fusion.5), channel_id=1, source_target_pairs={{0,64},{8,72},{16,80},{24,88},{32,96},{40,104},{48,112},{56,120},{... | collective-permute-start | bytes 36872 | tf_op jit(solution)/shard_map/ppermute | solution.py:61
  188.9 10.0 %collective-permute-start.13 = (f32[8,768]{1,0:T(8,128)S(1)}, f32[8,768]{1,0:T(8,128)S(1)}, u32[]{:S(2)}, u32[]{:S(2)}) collective-permute-start(f32[8,768]{1,0:T(8,128)S(1)} %maximum_select_fusion.4), channel_id=1, source_target_pairs={{0,32},{8,40},{16,48},{24,56},{32,0},{40,8},{48,16},{56,24},{64,96... | collective-permute-start | bytes 73736 | tf_op jit(solution)/shard_map/ppermute | solution.py:61
  198.8 7.3 %collective-permute-start.14 = (f32[16,768]{1,0:T(8,128)S(1)}, f32[16,768]{1,0:T(8,128)S(1)}, u32[]{:S(2)}, u32[]{:S(2)}) collective-permute-start(f32[16,768]{1,0:T(8,128)S(1)} %maximum_select_fusion.3), channel_id=1, source_target_pairs={{0,16},{8,24},{16,0},{24,8},{32,48},{40,56},{48,32},{56,40},{64,80... | collective-permute-start | bytes 147464 | tf_op jit(solution)/shard_map/ppermute | solution.py:61
  206.5 13.6 %collective-permute-start.15 = (f32[32,768]{0,1:T(8,128)S(1)}, f32[32,768]{0,1:T(8,128)S(1)}, u32[]{:S(2)}, u32[]{:S(2)}) collective-permute-start(f32[32,768]{0,1:T(8,128)S(1)} %broadcast_select_fusion), channel_id=1, source_target_pairs={{0,256},{128,384},{256,0},{384,128},{1,257},{129,385},{257,1},{385... | collective-permute-start | bytes 294920 | tf_op jit(solution)/shard_map/ppermute | solution.py:61
  220.4 9.7 %collective-permute-start.16 = (f32[64,768]{0,1:T(8,128)S(1)}, f32[64,768]{0,1:T(8,128)S(1)}, u32[]{:S(2)}, u32[]{:S(2)}) collective-permute-start(f32[64,768]{0,1:T(8,128)S(1)} %maximum_select_fusion.1), channel_id=1, source_target_pairs={{0,8},{8,0},{16,24},{24,16},{32,40},{40,32},{48,56},{56,48},{64,72... | collective-permute-start | bytes 589832 | tf_op jit(solution)/shard_map/ppermute | solution.py:61
  230.4 9.7 %collective-permute-start.17 = (f32[128,768]{0,1:T(8,128)S(1)}, f32[128,768]{0,1:T(8,128)S(1)}, u32[]{:S(2)}, u32[]{:S(2)}) collective-permute-start(f32[128,768]{0,1:T(8,128)S(1)} %maximum_select_fusion.2), channel_id=1, source_target_pairs={{0,128},{128,0},{256,384},{384,256},{1,129},{129,1},{257,385},{385... | collective-permute-start | bytes 1179656 | tf_op jit(solution)/shard_map/ppermute | solution.py:61

commit v2 on v1

--- a/solution.py
+++ b/solution.py
@@ -3,6 +3,8 @@
 import jax
 import jax.numpy as jnp
 from jax import lax
+from jax.experimental import pallas as pl
+from jax.experimental.pallas import tpu as pltpu
 from jax.sharding import Mesh
 from jax.sharding import PartitionSpec as P
 
@@ -18,53 +20,50 @@
     return lax.ppermute(x, axis, pairs)
 
 
-def band_block(coefs, offset):
+def band_kernel(coefs_ref, inner_ref, carry_ref):
     row_ids = lax.broadcasted_iota(jnp.int32, (BLOCK, BLOCK), 0)
     col_ids = lax.broadcasted_iota(jnp.int32, (BLOCK, BLOCK), 1)
-    lag_ids = col_ids - row_ids + offset
-    block = jnp.zeros((BLOCK, BLOCK), jnp.float32)
-    for k in range(coefs.shape[0]):
-        block = jnp.where(lag_ids == k, coefs[k], block)
-    return block.astype(jnp.bfloat16)
+    lag_ids = col_ids - row_ids
+    inner = jnp.zeros((BLOCK, BLOCK), jnp.float32)
+    carry = jnp.zeros((BLOCK, BLOCK), jnp.float32)
+    for k in range(coefs_ref.shape[0]):
+        tap = coefs_ref[k]
+        inner = jnp.where(lag_ids == k, tap, inner)
+        carry = jnp.where(lag_ids == k - BLOCK, tap, carry)
+    inner_ref[...] = inner.astype(inner_ref.dtype)
+    carry_ref[...] = carry.astype(carry_ref.dtype)
 
 
-def halve(cur):
-    if cur.shape[0] > 8:
-        h = cur.shape[0] // 2
-        return cur[:h], cur[h:], 0
-    h = cur.shape[1] // 2
-    return cur[:, :h], cur[:, h:], 1
+def band_blocks(coefs):
+    block = jax.ShapeDtypeStruct((BLOCK, BLOCK), jnp.bfloat16)
+    vmem = pl.BlockSpec(memory_space=pltpu.VMEM)
+    return pl.pallas_call(
+        band_kernel,
+        out_shape=(block, block),
+        in_specs=[pl.BlockSpec(memory_space=pltpu.SMEM)],
+        out_specs=(vmem, vmem),
+    )(coefs)
+
+
+def scatter_sum(flat, axis):
+    count = lax.axis_size(axis)
+    got = lax.all_to_all(flat.reshape(count, -1), axis, 0, 0, tiled=True)
+    return jnp.sum(got, axis=0)
+
+
+def gather_back(flat, axis):
+    count = lax.axis_size(axis)
+    spread = jnp.broadcast_to(flat[None], (count,) + flat.shape)
+    return lax.all_to_all(spread, axis, 0, 0, tiled=True).reshape(-1)
 
 
 def reduce_rows(x):
-    sizes = {a: lax.axis_size(a) for a in ROWS}
-    rounds = []
-    d = 1
-    while d < max(sizes.values()):
-        for a in ROWS:
-            if d < sizes[a]:
-                rounds.append((a, d))
-        d *= 2
-    cur = x
-    kept = []
-    for a, d in rounds:
-        bit = (lax.axis_index(a) // d) % 2 == 1
-        lo, hi, dim = halve(cur)
-        keep = jnp.where(bit, hi, lo)
-        send = jnp.where(bit, lo, hi)
-        pairs = [(i, i ^ d) for i in range(sizes[a])]
-        cur = keep + lax.ppermute(send, a, pairs)
-        kept.append(dim)
-    for (a, d), dim in zip(reversed(rounds), reversed(kept)):
-        bit = (lax.axis_index(a) // d) % 2 == 1
-        pairs = [(i, i ^ d) for i in range(sizes[a])]
-        other = lax.ppermute(cur, a, pairs)
-        cur = jnp.where(
-            bit,
-            jnp.concatenate([other, cur], axis=dim),
-            jnp.concatenate([cur, other], axis=dim),
-        )
-    return cur
+    flat = x.reshape(-1)
+    flat = scatter_sum(flat, "x")
+    flat = scatter_sum(flat, "z")
+    flat = gather_back(flat, "z")
+    flat = gather_back(flat, "x")
+    return flat.reshape(x.shape)
 
 
 def shards(frames, tap_table, sketch_matrix, decay_rates):
@@ -72,8 +71,7 @@
     npoints = rows_here * math.prod(lax.axis_size(a) for a in ROWS)
     batch_count = lax.axis_size(BATCH)
     coefs = (tap_table.astype(jnp.float32) / 1024.0).astype(jnp.bfloat16).astype(jnp.float32)
-    inner = band_block(coefs, 0)
-    carry = band_block(coefs, BLOCK)
+    inner, carry = band_blocks(coefs)
     nblocks = frame_count // BLOCK
     zero = jnp.zeros((BLOCK, BLOCK), jnp.bfloat16)
     main_band = jnp.block(

time: 307 us -> 182 us (0.59)
  other arithmetic: 134 us -> 58.5 us
  starting transfers between devices: 82 us -> 13.3 us
  blocking collectives: 0 us -> 60.4 us
  waiting for transfers between devices: 70.8 us -> 28.1 us
    convert_element_type x2 -> x0, other arithmetic: 79.1 us -> none  [band_block(): return block.astype(jnp.bfloat16)]
    ppermute x12 -> x0, starting transfers between devices: 72.4 us -> none  [the longest x6 42.5 us: reduce_rows(): cur = keep + lax.ppermute(send, a, pairs)]
    all_to_all x0 -> x3, blocking collectives: none -> 60.4 us  [the longest x2 42.2 us: scatter_sum(): got = lax.all_to_all(flat.reshape(count, -1), axis, 0, 0, tiled=True)]
    ppermute x12 -> x0, waiting for transfers between devices: 52.9 us -> none  [the longest x6 34.4 us: reduce_rows(): other = lax.ppermute(cur, a, pairs)]
    all_to_all x0 -> x1, waiting for transfers between devices: none -> 9.22 us  [gather_back(): return lax.all_to_all(spread, axis, 0, 0, tiled=True).reshape(-1)]
    all_to_all x0 -> x1, starting transfers between devices: none -> 3.67 us  [gather_back(): return lax.all_to_all(spread, axis, 0, 0, tiled=True).reshape(-1)]
  transfers between devices with their start and end apart: 18 -> 7, of which waited for: 17 -> 7; matrix products, arithmetic and copies ran while one was open for 27% -> 1% of each run, Pallas kernels for 0% -> 1%
where the time goes in v2:
time: 182 us; the launch traced here: 180 us
  blocking collectives  60.4 us (33%)
  other arithmetic  58.5 us (32%)
  waiting for transfers between devices  28.1 us (15%)
  starting transfers between devices  13.3 us (7%)
  local copies, waits for them, and re-layouts  9.43 us (5%)
  matrix products  6.42 us (4%)
  between operations  2.26 us (1%)
    all_to_all x2, blocking collectives, scatter_sum(): got = lax.all_to_all(flat.reshape(count, -1), axis, 0, 0, tiled=True)  42.2 us
    another operation x6, other arithmetic, shards(): lower_one = jnp.linalg.cholesky(gram)  34.1 us
    another operation x2, other arithmetic, shards(): lax.linalg.triangular_solve(lower_one, jnp.eye(rank_count, dtype=jnp.floa...  19.7 us
    ppermute x6, waiting for transfers between devices, shifted(): return lax.ppermute(x, axis, pairs)  18.9 us
    all_to_all x1, blocking collectives, gather_back(): return lax.all_to_all(spread, axis, 0, 0, tiled=True).reshape(-1)  18.2 us
    ppermute x6, starting transfers between devices, shifted(): return lax.ppermute(x, axis, pairs)  9.63 us
    all_to_all x1, waiting for transfers between devices, gather_back(): return lax.all_to_all(spread, axis, 0, 0, tiled=True).reshape(-1)  9.22 us
    another operation x6, local copies, waits for them, and re-layouts  3.95 us
  transfers between devices with their start and end apart: 7, of which 7 were waited for; matrix products, arithmetic and copies ran while one was open for 1% of the time, Pallas kernels for 1%

profile of v2, /device:TPU:24, one launch (start us, length us, event | category | flops | bytes accessed | tf_op | source)
XLA Modules:
  0.0 180.0 jit_solution(14938610914577928493)
XLA Ops:
  1.6 1.9 %collective-permute-start = (bf16[256,128]{1,0:T(8,128)(2,1)S(1)}, bf16[256,128]{1,0:T(8,128)(2,1)S(1)}, u32[]{:S(2)}, u32[]{:S(2)}) collective-permute-start(bf16[256,128]{1,0:T(8,128)(2,1)S(1)} %slice.52), channel_id=1, source_target_pairs={{0,1},{1,2},{2,3},{3,4},{4,5},{5,6},{6,7},{8,9},{9,10},{10,11},{11... | collective-permute-start | bytes 196616 | tf_op jit(solution)/shard_map/ppermute | solution.py:20
  4.7 1.6 shard_map.67
  9.5 1.9 %collective-permute-start.1 = (f32[256,256]{0,1:T(8,128)S(1)}, f32[256,256]{0,1:T(8,128)S(1)}, u32[]{:S(2)}, u32[]{:S(2)}) collective-permute-start(f32[256,256]{0,1:T(8,128)S(1)} %fusion.48), channel_id=1, source_target_pairs={{0,1},{1,2},{2,3},{3,4},{4,5},{5,6},{6,7},{8,9},{9,10},{10,11},{11... | collective-permute-start | bytes 786440 | tf_op jit(solution)/shard_map/ppermute | solution.py:20
  11.4 5.8 %collective-permute-done.1 = f32[256,256]{0,1:T(8,128)S(1)} collective-permute-done((f32[256,256]{0,1:T(8,128)S(1)}, f32[256,256]{0,1:T(8,128)S(1)}, u32[]{:S(2)}, u32[]{:S(2)}) %collective-permute-start.1) | collective-permute-done | bytes 262176 | tf_op jit(solution)/shard_map/ppermute | solution.py:20
  18.6 1.9 %collective-permute-start.2 = (f32[256]{0:T(256)S(1)}, f32[256]{0:T(256)S(1)}, u32[]{:S(2)}, u32[]{:S(2)}) collective-permute-start(f32[256]{0:T(256)S(1)} %bitcast.55), channel_id=1, source_target_pairs={{0,1},{1,2},{2,3},{3,4},{4,5},{5,6},{6,7},{8,9},{9,10},{10,11},{11... | collective-permute-start | bytes 3080 | tf_op jit(solution)/shard_map/ppermute | solution.py:20
  20.6 3.0 %collective-permute-done.2 = f32[256]{0:T(256)S(1)} collective-permute-done((f32[256]{0:T(256)S(1)}, f32[256]{0:T(256)S(1)}, u32[]{:S(2)}, u32[]{:S(2)}) %collective-permute-start.2) | collective-permute-done | bytes 1056 | tf_op jit(solution)/shard_map/ppermute | solution.py:20
  23.5 2.1 %collective-permute-done.3 = f32[256,256]{0,1:T(8,128)S(1)} collective-permute-done((f32[256,256]{0,1:T(8,128)S(1)}, f32[256,256]{0,1:T(8,128)S(1)}, u32[]{:S(2)}, u32[]{:S(2)}) %collective-permute-start.3) | collective-permute-done | bytes 262176 | tf_op jit(solution)/shard_map/ppermute | solution.py:20
  28.3 4.2 %collective-permute-done.4 = f32[256]{0:T(256)S(1)} collective-permute-done((f32[256]{0:T(256)S(1)}, f32[256]{0:T(256)S(1)}, u32[]{:S(2)}, u32[]{:S(2)}) %collective-permute-start.4) | collective-permute-done | bytes 1056 | tf_op jit(solution)/shard_map/ppermute | solution.py:20
  32.5 3.0 %collective-permute-done.5 = f32[256,256]{0,1:T(8,128)S(1)} collective-permute-done((f32[256,256]{0,1:T(8,128)S(1)}, f32[256,256]{0,1:T(8,128)S(1)}, u32[]{:S(2)}, u32[]{:S(2)}) %collective-permute-start.5) | collective-permute-done | bytes 262176 | tf_op jit(solution)/shard_map/ppermute | solution.py:20
  37.2 13.6 %all_to_all.31 = f32[4,1,49152]{2,1,0:T(1,128)S(1)} all-to-all(f32[4,1,49152]{2,1,0:T(1,128)S(1)} %all_to_all.26), channel_id=1, replica_groups=mesh['x'=4,'z'=16,'y'=4,'core'=2] {'x'}, dimensions={0} | all-to-all | bytes 1572864 | tf_op jit(solution)/shard_map/all_to_all | solution.py:50
  51.5 28.7 %all_to_all.32 = f32[16,1,3072]{2,1,0:T(1,128)S(1)} all-to-all(f32[16,1,3072]{2,1,0:T(1,128)S(1)} %bitcast.52), channel_id=1, replica_groups=mesh['x'=4,'z'=16,'y'=4,'core'=2] {'z'}, dimensions={0} | all-to-all | bytes 393216 | tf_op jit(solution)/shard_map/all_to_all | solution.py:50
  80.4 18.2 %all_to_all.33 = f32[16,1,3072]{2,1,0:T(1,128)S(1)} all-to-all(f32[16,1,3072]{2,1,0:T(1,128)S(1)} %broadcast_in_dim.30), channel_id=1, replica_groups=mesh['x'=4,'z'=16,'y'=4,'core'=2] {'z'}, dimensions={0} | all-to-all | bytes 393216 | tf_op jit(solution)/shard_map/all_to_all | solution.py:57
  99.9 3.7 %all-to-all-start.3 = ((f32[4,1,49152]{2,1,0:T(1,128)}), f32[4,1,49152]{2,1,0:T(1,128)S(1)}, u32[]{:S(2)}, u32[]{:S(2)}) async-start(f32[4,1,49152]{2,1,0:T(1,128)} %broadcast_in_dim.32), calls=%async_computation.3 | async-start | bytes 1572864 | tf_op jit(solution)/shard_map/all_to_all | solution.py:57
  103.6 9.2 %all-to-all-done.3 = f32[4,1,49152]{2,1,0:T(1,128)S(1)} async-done(((f32[4,1,49152]{2,1,0:T(1,128)}), f32[4,1,49152]{2,1,0:T(1,128)S(1)}, u32[]{:S(2)}, u32[]{:S(2)}) %all-to-all-start.3) | async-done | bytes 786464 | tf_op jit(solution)/shard_map/all_to_all | solution.py:57
  112.8 2.3 %reduce.14 = f32[4,49152]{1,0:T(4,128)S(1)} reduce(f32[4,1,49152]{2,1,0:T(1,128)S(1)} %all-to-all-done.3, f32[]{:T(128)} %constant.110), dimensions={1}, to_apply=%all_to_all.25.reduce_sub_computation | reduce | bytes 1572868 | tf_op jit(solution)/shard_map/all_to_all | solution.py:57
  115.9 11.7 %cholesky.50 = f32[128,128]{1,0:T(8,128)S(1)} custom-call(f32[128,128]{1,0:T(8,128)S(1)} %cholesky.118), custom_call_target="Cholesky" | custom-call | tf_op jit(solution)/shard_map/jit(cholesky)/cholesky | solution.py:104
  127.7 9.8 %custom-call.14 = f32[1,128,128]{1,2,0:T(8,128)S(1)} custom-call(f32[1,128,128]{2,1,0:T(8,128)S(1)} %get-tuple-element.45), custom_call_target="InvertDiagBlocksLowerTriangular" | custom-call | tf_op jit(solution)/shard_map/jit(cholesky)/cholesky | solution.py:104
  138.0 11.9 %cholesky.105 = f32[128,128]{1,0:T(8,128)S(1)} custom-call(f32[128,128]{1,0:T(8,128)S(1)} %convolution_subtract_fusion.1), custom_call_target="Cholesky" | custom-call | tf_op jit(solution)/shard_map/jit(cholesky)/cholesky | solution.py:104
  151.9 4.0 %while.1 = (s32[]{:T(128)}, f32[256,256]{1,0:T(8,128)S(1)}, s32[2,2]{1,0:T(2,128)S(1)}, f32[2,128,128]{2,1,0:T(8,128)S(1)}, s32[]{:T(128)}) while((s32[]{:T(128)}, f32[256,256]{1,0:T(8,128)S(1)}, s32[2,2]{1,0:T(2,128)S(1)}, f32[2,128,128]{2,1,0:T(8,128)S(1)}, s32[]{:T(128)}) %tuple.34), condition=%wide.while_cond, body=%wide.while_body.sunk | while | flops 2 | bytes 131189 | solution.py:105
  152.5 1.4 bitcast_dynamic-update-slice_fusion.2
  154.5 1.4 bitcast_dynamic-update-slice_fusion.2
  155.9 19.7 %custom-call.15 = f32[2,128,128]{1,2,0:T(8,128)S(1)} custom-call(f32[2,128,128]{2,1,0:T(8,128)S(1)} %get-tuple-element.14), custom_call_target="InvertDiagBlocksLowerTriangular" | custom-call | tf_op jit(solution)/shard_map/triangular_solve | solution.py:105
  176.5 1.3 fusion.1
  177.8 1.4 fusion
  (55 shorter events, 18.3 us)
Async XLA Ops:
  0.6 8.6 %copy-start = (bf16[512,256]{1,0:T(8,128)(2,1)S(1)}, bf16[512,256]{1,0:T(8,128)(2,1)}, u32[]{:S(2)}) copy-start(bf16[512,256]{1,0:T(8,128)(2,1)} %param.6) | copy-start | bytes 786436
  0.6 7.5 %copy-start.2 = (bf16[256,512]{1,0:T(8,128)(2,1)S(1)}, bf16[256,512]{1,0:T(8,128)(2,1)}, u32[]{:S(2)}) copy-start(bf16[256,512]{1,0:T(8,128)(2,1)} %param.4) | copy-start | bytes 786436
  1.6 5.6 %collective-permute-start = (bf16[256,128]{1,0:T(8,128)(2,1)S(1)}, bf16[256,128]{1,0:T(8,128)(2,1)S(1)}, u32[]{:S(2)}, u32[]{:S(2)}) collective-permute-start(bf16[256,128]{1,0:T(8,128)(2,1)S(1)} %slice.52), channel_id=1, source_target_pairs={{0,1},{1,2},{2,3},{3,4},{4,5},{5,6},{6,7},{8,9},{9,10},{10,11},{11... | collective-permute-start | bytes 196616 | tf_op jit(solution)/shard_map/ppermute | solution.py:20
  7.1 1.0 copy-start.4
  8.1 0.8 copy-start.1
  9.5 7.7 %copy-start.3 = (f32[1,256]{1,0:T(1,128)S(1)}, f32[1,256]{1,0:T(1,128)}, u32[]{:S(2)}) copy-start(f32[1,256]{1,0:T(1,128)} %param.7) | copy-start | bytes 3076
  9.5 7.7 %collective-permute-start.1 = (f32[256,256]{0,1:T(8,128)S(1)}, f32[256,256]{0,1:T(8,128)S(1)}, u32[]{:S(2)}, u32[]{:S(2)}) collective-permute-start(f32[256,256]{0,1:T(8,128)S(1)} %fusion.48), channel_id=1, source_target_pairs={{0,1},{1,2},{2,3},{3,4},{4,5},{5,6},{6,7},{8,9},{9,10},{10,11},{11... | collective-permute-start | bytes 786440 | tf_op jit(solution)/shard_map/ppermute | solution.py:20
  17.3 8.3 %collective-permute-start.3 = (f32[256,256]{0,1:T(8,128)S(1)}, f32[256,256]{0,1:T(8,128)S(1)}, u32[]{:S(2)}, u32[]{:S(2)}) collective-permute-start(f32[256,256]{0,1:T(8,128)S(1)} %multiply_add_fusion.2), channel_id=1, source_target_pairs={{0,2},{1,3},{2,4},{3,5},{4,6},{5,7},{8,10},{9,11},{10,12},{11,13},... | collective-permute-start | bytes 786440 | tf_op jit(solution)/shard_map/ppermute | solution.py:20
  18.6 4.9 %collective-permute-start.2 = (f32[256]{0:T(256)S(1)}, f32[256]{0:T(256)S(1)}, u32[]{:S(2)}, u32[]{:S(2)}) collective-permute-start(f32[256]{0:T(256)S(1)} %bitcast.55), channel_id=1, source_target_pairs={{0,1},{1,2},{2,3},{3,4},{4,5},{5,6},{6,7},{8,9},{9,10},{10,11},{11... | collective-permute-start | bytes 3080 | tf_op jit(solution)/shard_map/ppermute | solution.py:20
  25.7 9.8 %collective-permute-start.5 = (f32[256,256]{0,1:T(8,128)S(1)}, f32[256,256]{0,1:T(8,128)S(1)}, u32[]{:S(2)}, u32[]{:S(2)}) collective-permute-start(f32[256,256]{0,1:T(8,128)S(1)} %multiply_add_fusion.1), channel_id=1, source_target_pairs={{0,4},{1,5},{2,6},{3,7},{8,12},{9,13},{10,14},{11,15},{16,20},{17,... | collective-permute-start | bytes 786440 | tf_op jit(solution)/shard_map/ppermute | solution.py:20
  27.0 5.5 %collective-permute-start.4 = (f32[256]{0:T(256)S(1)}, f32[256]{0:T(256)S(1)}, u32[]{:S(2)}, u32[]{:S(2)}) collective-permute-start(f32[256]{0:T(256)S(1)} %mul.44), channel_id=1, source_target_pairs={{0,2},{1,3},{2,4},{3,5},{4,6},{5,7},{8,10},{9,11},{10,12},{11,13},... | collective-permute-start | bytes 3080 | tf_op jit(solution)/shard_map/ppermute | solution.py:20
  99.9 13.0 %all-to-all-start.3 = ((f32[4,1,49152]{2,1,0:T(1,128)}), f32[4,1,49152]{2,1,0:T(1,128)S(1)}, u32[]{:S(2)}, u32[]{:S(2)}) async-start(f32[4,1,49152]{2,1,0:T(1,128)} %broadcast_in_dim.32), calls=%async_computation.3 | async-start | bytes 1572864 | tf_op jit(solution)/shard_map/all_to_all | solution.py:57

commit v3 on v2

--- a/solution.py
+++ b/solution.py
@@ -94,13 +94,20 @@
 
     root_points = math.sqrt(npoints)
     rank_count = weighted.shape[1]
-    both = jnp.concatenate([weighted, filtered.astype(jnp.float32)], axis=1)
-    partial = lax.dot_general(
-        weighted, both, (((0,), (0,)), ((), ())), precision=HIGH, preferred_element_type=jnp.float32
+    gram = reduce_rows(
+        lax.dot_general(
+            weighted, weighted, (((0,), (0,)), ((), ())), precision=HIGH, preferred_element_type=jnp.float32
+        )
     )
-    summed = reduce_rows(partial)
-    gram = summed[:, :rank_count]
-    cross = summed[:, rank_count:]
+    cross = reduce_rows(
+        lax.dot_general(
+            weighted,
+            filtered.astype(jnp.float32),
+            (((0,), (0,)), ((), ())),
+            precision=HIGH,
+            preferred_element_type=jnp.float32,
+        )
+    )
     lower_one = jnp.linalg.cholesky(gram)
     inverse = lax.linalg.triangular_solve(
         lower_one, jnp.eye(rank_count, dtype=jnp.float32), left_side=True, lower=True

time: 182 us -> 207 us (1.14)
  starting transfers between devices: 13.3 us -> 50.8 us
  blocking collectives: 60.4 us -> 26.3 us
  waiting for transfers between devices: 28.1 us -> 47.5 us
    all_to_all x2 -> x1, blocking collectives: 42.2 us -> 10.8 us  [scatter_sum(): got = lax.all_to_all(flat.reshape(count, -1), axis, 0, 0, tiled=True)]
    all_to_all x0 -> x3, starting transfers between devices: none -> 22.2 us  [scatter_sum(): got = lax.all_to_all(flat.reshape(count, -1), axis, 0, 0, tiled=True)]
    all_to_all x0 -> x3, waiting for transfers between devices: none -> 18.9 us  [scatter_sum(): got = lax.all_to_all(flat.reshape(count, -1), axis, 0, 0, tiled=True)]
    all_to_all x1 -> x3, starting transfers between devices: 3.67 us -> 18.9 us  [gather_back(): return lax.all_to_all(spread, axis, 0, 0, tiled=True).reshape(-1)]
    all_to_all x1, blocking collectives: 18.2 us -> 15.5 us  [gather_back(): return lax.all_to_all(spread, axis, 0, 0, tiled=True).reshape(-1)]
    all_to_all x1 -> x3, waiting for transfers between devices: 9.22 us -> 10.7 us  [gather_back(): return lax.all_to_all(spread, axis, 0, 0, tiled=True).reshape(-1)]
  transfers between devices with their start and end apart: 7 -> 12, of which waited for: 7 -> 10; matrix products, arithmetic and copies ran while one was open for 1% -> 32% of each run, Pallas kernels for 1% -> 1%
where the time goes in v3:
time: 207 us; the launch traced here: 206 us
  other arithmetic  58.9 us (28%)
  starting transfers between devices  50.8 us (25%)
  waiting for transfers between devices  47.5 us (23%)
  blocking collectives  26.3 us (13%)
  local copies, waits for them, and re-layouts  11.4 us (6%)
  matrix products  6.89 us (3%)
  between operations  2.21 us (1%)
    another operation x6, other arithmetic, shards(): lower_one = jnp.linalg.cholesky(gram)  33.9 us
    all_to_all x3, starting transfers between devices, scatter_sum(): got = lax.all_to_all(flat.reshape(count, -1), axis, 0, 0, tiled=True)  22.2 us
    another operation x2, other arithmetic, shards(): lax.linalg.triangular_solve(lower_one, jnp.eye(rank_count, dtype=jnp.floa...  19.7 us
    all_to_all x3, starting transfers between devices, gather_back(): return lax.all_to_all(spread, axis, 0, 0, tiled=True).reshape(-1)  18.9 us
    all_to_all x3, waiting for transfers between devices, scatter_sum(): got = lax.all_to_all(flat.reshape(count, -1), axis, 0, 0, tiled=True)  18.9 us
    ppermute x6, waiting for transfers between devices, shifted(): return lax.ppermute(x, axis, pairs)  18 us
    all_to_all x1, blocking collectives, gather_back(): return lax.all_to_all(spread, axis, 0, 0, tiled=True).reshape(-1)  15.5 us
    all_to_all x1, blocking collectives, scatter_sum(): got = lax.all_to_all(flat.reshape(count, -1), axis, 0, 0, tiled=True)  10.8 us
  transfers between devices with their start and end apart: 12, of which 10 were waited for; matrix products, arithmetic and copies ran while one was open for 32% of the time, Pallas kernels for 1%

profile of v3, /device:TPU:24, one launch (start us, length us, event | category | flops | bytes accessed | tf_op | source)
XLA Modules:
  0.0 205.6 jit_solution(11494049753418061588)
XLA Ops:
  8.2 1.9 collective-permute-start.1
  10.1 5.8 %collective-permute-done.1 = f32[256,256]{1,0:T(8,128)S(1)} collective-permute-done((f32[256,256]{1,0:T(8,128)S(1)}, f32[256,256]{1,0:T(8,128)S(1)}, u32[]{:S(2)}, u32[]{:S(2)}) %collective-permute-start.1) | collective-permute-done | bytes 262176 | tf_op jit(solution)/shard_map/ppermute | solution.py:20
  17.2 1.9 collective-permute-start.2
  19.2 3.0 %collective-permute-done.2 = f32[256]{0:T(256)S(1)} collective-permute-done((f32[256]{0:T(256)S(1)}, f32[256]{0:T(256)S(1)}, u32[]{:S(2)}, u32[]{:S(2)}) %collective-permute-start.2) | collective-permute-done | bytes 1056 | tf_op jit(solution)/shard_map/ppermute | solution.py:20
  22.1 2.1 %collective-permute-done.3 = f32[256,256]{1,0:T(8,128)S(1)} collective-permute-done((f32[256,256]{1,0:T(8,128)S(1)}, f32[256,256]{1,0:T(8,128)S(1)}, u32[]{:S(2)}, u32[]{:S(2)}) %collective-permute-start.3) | collective-permute-done | bytes 262176 | tf_op jit(solution)/shard_map/ppermute | solution.py:20
  26.8 4.2 %collective-permute-done.4 = f32[256]{0:T(256)S(1)} collective-permute-done((f32[256]{0:T(256)S(1)}, f32[256]{0:T(256)S(1)}, u32[]{:S(2)}, u32[]{:S(2)}) %collective-permute-start.4) | collective-permute-done | bytes 1056 | tf_op jit(solution)/shard_map/ppermute | solution.py:20
  31.0 3.0 %collective-permute-done.5 = f32[256,256]{1,0:T(8,128)S(1)} collective-permute-done((f32[256,256]{1,0:T(8,128)S(1)}, f32[256,256]{1,0:T(8,128)S(1)}, u32[]{:S(2)}, u32[]{:S(2)}) %collective-permute-start.5) | collective-permute-done | bytes 262176 | tf_op jit(solution)/shard_map/ppermute | solution.py:20
  34.9 10.8 %all_to_all.62 = f32[4,1,16384]{2,1,0:T(1,128)S(1)} all-to-all(f32[4,1,16384]{2,1,0:T(1,128)S(1)} %all_to_all.52), channel_id=1, replica_groups=mesh['x'=4,'z'=16,'y'=4,'core'=2] {'x'}, dimensions={0} | all-to-all | bytes 524288 | tf_op jit(solution)/shard_map/all_to_all | solution.py:50
  46.6 15.2 %all-to-all-start.1 = ((f32[16,1,1024]{2,1,0:T(1,128)}), f32[16,1,1024]{2,1,0:T(1,128)S(1)}, u32[]{:S(2)}, u32[]{:S(2)}) async-start(f32[16,1,1024]{2,1,0:T(1,128)} %bitcast.3), calls=%async_computation.1 | async-start | bytes 131072 | tf_op jit(solution)/shard_map/all_to_all | solution.py:50
  63.9 10.8 %all-to-all-done.1 = f32[16,1,1024]{2,1,0:T(1,128)S(1)} async-done(((f32[16,1,1024]{2,1,0:T(1,128)}), f32[16,1,1024]{2,1,0:T(1,128)S(1)}, u32[]{:S(2)}, u32[]{:S(2)}) %all-to-all-start.1) | async-done | bytes 65568 | tf_op jit(solution)/shard_map/all_to_all | solution.py:50
  74.6 3.5 %all-to-all-start.4 = ((f32[4,1,32768]{2,1,0:T(1,128)}), f32[4,1,32768]{2,1,0:T(1,128)S(1)}, u32[]{:S(2)}, u32[]{:S(2)}) async-start(f32[4,1,32768]{2,1,0:T(1,128)} %all_to_all.53), calls=%async_computation.4 | async-start | bytes 1048576 | tf_op jit(solution)/shard_map/all_to_all | solution.py:50
  78.2 8.0 %all-to-all-done.4 = f32[4,1,32768]{2,1,0:T(1,128)S(1)} async-done(((f32[4,1,32768]{2,1,0:T(1,128)}), f32[4,1,32768]{2,1,0:T(1,128)S(1)}, u32[]{:S(2)}, u32[]{:S(2)}) %all-to-all-start.4) | async-done | bytes 524320 | tf_op jit(solution)/shard_map/all_to_all | solution.py:50
  86.2 15.5 %all_to_all.63 = f32[16,1,1024]{2,1,0:T(1,128)S(1)} all-to-all(f32[16,1,1024]{2,1,0:T(1,128)S(1)} %broadcast_in_dim.43), channel_id=1, replica_groups=mesh['x'=4,'z'=16,'y'=4,'core'=2] {'z'}, dimensions={0} | all-to-all | bytes 131072 | tf_op jit(solution)/shard_map/all_to_all | solution.py:57
  102.6 3.4 %all-to-all-start.3 = ((f32[4,1,16384]{2,1,0:T(1,128)}), f32[4,1,16384]{2,1,0:T(1,128)S(1)}, u32[]{:S(2)}, u32[]{:S(2)}) async-start(f32[4,1,16384]{2,1,0:T(1,128)} %broadcast_in_dim.45), calls=%async_computation.3 | async-start | bytes 524288 | tf_op jit(solution)/shard_map/all_to_all | solution.py:57
  107.3 5.4 %all-to-all-done.3 = f32[4,1,16384]{2,1,0:T(1,128)S(1)} async-done(((f32[4,1,16384]{2,1,0:T(1,128)}), f32[4,1,16384]{2,1,0:T(1,128)S(1)}, u32[]{:S(2)}, u32[]{:S(2)}) %all-to-all-start.3) | async-done | bytes 262176 | tf_op jit(solution)/shard_map/all_to_all | solution.py:57
  112.6 3.5 %all-to-all-start.5 = ((f32[16,1,2048]{2,1,0:T(1,128)}), f32[16,1,2048]{2,1,0:T(1,128)S(1)}, u32[]{:S(2)}, u32[]{:S(2)}) async-start(f32[16,1,2048]{2,1,0:T(1,128)} %bitcast.13), calls=%async_computation.5 | async-start | bytes 262144 | tf_op jit(solution)/shard_map/all_to_all | solution.py:50
  117.3 11.7 %cholesky.50 = f32[128,128]{1,0:T(8,128)S(1)} custom-call(f32[128,128]{1,0:T(8,128)S(1)} %cholesky.118), custom_call_target="Cholesky" | custom-call | tf_op jit(solution)/shard_map/jit(cholesky)/cholesky | solution.py:111
  130.0 11.8 %all-to-all-start.6 = ((f32[16,1,2048]{2,1,0:T(1,128)}), f32[16,1,2048]{2,1,0:T(1,128)S(1)}, u32[]{:S(2)}, u32[]{:S(2)}) async-start(f32[16,1,2048]{2,1,0:T(1,128)} %broadcast_in_dim.48), calls=%async_computation.6 | async-start | bytes 262144 | tf_op jit(solution)/shard_map/all_to_all | solution.py:57
  141.9 9.8 %custom-call.14 = f32[1,128,128]{1,2,0:T(8,128)S(1)} custom-call(f32[1,128,128]{2,1,0:T(8,128)S(1)} %get-tuple-element.45), custom_call_target="InvertDiagBlocksLowerTriangular" | custom-call | tf_op jit(solution)/shard_map/jit(cholesky)/cholesky | solution.py:111
  152.2 11.7 %cholesky.105 = f32[128,128]{1,0:T(8,128)S(1)} custom-call(f32[128,128]{1,0:T(8,128)S(1)} %convolution_subtract_fusion.1), custom_call_target="Cholesky" | custom-call | tf_op jit(solution)/shard_map/jit(cholesky)/cholesky | solution.py:111
  165.9 3.8 %while.1 = (s32[]{:T(128)}, f32[256,256]{1,0:T(8,128)S(1)}, s32[2,2]{1,0:T(2,128)S(1)}, f32[2,128,128]{2,1,0:T(8,128)S(1)}, s32[]{:T(128)}) while((s32[]{:T(128)}, f32[256,256]{1,0:T(8,128)S(1)}, s32[2,2]{1,0:T(2,128)S(1)}, f32[2,128,128]{2,1,0:T(8,128)S(1)}, s32[]{:T(128)}) %tuple.33), condition=%wide.while_cond, body=%wide.while_body.sunk | while | flops 2 | bytes 131189 | solution.py:112
  169.7 19.7 %custom-call.15 = f32[2,128,128]{1,2,0:T(8,128)S(1)} custom-call(f32[2,128,128]{2,1,0:T(8,128)S(1)} %get-tuple-element.14), custom_call_target="InvertDiagBlocksLowerTriangular" | custom-call | tf_op jit(solution)/shard_map/triangular_solve | solution.py:112
  190.8 3.7 %all-to-all-start.7 = ((f32[4,1,32768]{2,1,0:T(1,128)}), f32[4,1,32768]{2,1,0:T(1,128)S(1)}, u32[]{:S(2)}, u32[]{:S(2)}) async-start(f32[4,1,32768]{2,1,0:T(1,128)} %broadcast_in_dim.50), calls=%async_computation.7 | async-start | bytes 1048576 | tf_op jit(solution)/shard_map/all_to_all | solution.py:57
  197.0 5.3 %all-to-all-done.7 = f32[4,1,32768]{2,1,0:T(1,128)S(1)} async-done(((f32[4,1,32768]{2,1,0:T(1,128)}), f32[4,1,32768]{2,1,0:T(1,128)S(1)}, u32[]{:S(2)}, u32[]{:S(2)}) %all-to-all-start.7) | async-done | bytes 524320 | tf_op jit(solution)/shard_map/all_to_all | solution.py:57
  (69 shorter events, 31.7 us)
Async XLA Ops:
  0.6 7.3 %copy-start = (bf16[512,256]{1,0:T(8,128)(2,1)S(1)}, bf16[512,256]{1,0:T(8,128)(2,1)}, u32[]{:S(2)}) copy-start(bf16[512,256]{1,0:T(8,128)(2,1)} %param.6) | copy-start | bytes 786436
  0.6 2.8 %copy-start.3 = (s32[63]{0:T(128)S(1)}, s32[63]{0:T(128)}, u32[]{:S(2)}) copy-start(s32[63]{0:T(128)} %param.5) | copy-start | bytes 760
  1.5 6.2 %collective-permute-start = (bf16[256,128]{1,0:T(8,128)(2,1)S(1)}, bf16[256,128]{1,0:T(8,128)(2,1)S(1)}, u32[]{:S(2)}, u32[]{:S(2)}) collective-permute-start(bf16[256,128]{1,0:T(8,128)(2,1)S(1)} %slice.46), channel_id=1, source_target_pairs={{0,1},{1,2},{2,3},{3,4},{4,5},{5,6},{6,7},{8,9},{9,10},{10,11},{11... | collective-permute-start | bytes 196616 | tf_op jit(solution)/shard_map/ppermute | solution.py:20
  5.6 0.8 copy-start.1
  8.2 7.7 %copy-start.2 = (f32[1,256]{1,0:T(1,128)S(1)}, f32[1,256]{1,0:T(1,128)}, u32[]{:S(2)}) copy-start(f32[1,256]{1,0:T(1,128)} %param.7) | copy-start | bytes 3076
  8.2 7.7 %collective-permute-start.1 = (f32[256,256]{1,0:T(8,128)S(1)}, f32[256,256]{1,0:T(8,128)S(1)}, u32[]{:S(2)}, u32[]{:S(2)}) collective-permute-start(f32[256,256]{1,0:T(8,128)S(1)} %fusion.43), channel_id=1, source_target_pairs={{0,1},{1,2},{2,3},{3,4},{4,5},{5,6},{6,7},{8,9},{9,10},{10,11},{11... | collective-permute-start | bytes 786440 | tf_op jit(solution)/shard_map/ppermute | solution.py:20
  15.9 8.3 %collective-permute-start.3 = (f32[256,256]{1,0:T(8,128)S(1)}, f32[256,256]{1,0:T(8,128)S(1)}, u32[]{:S(2)}, u32[]{:S(2)}) collective-permute-start(f32[256,256]{1,0:T(8,128)S(1)} %multiply_add_fusion.2), channel_id=1, source_target_pairs={{0,2},{1,3},{2,4},{3,5},{4,6},{5,7},{8,10},{9,11},{10,12},{11,13},... | collective-permute-start | bytes 786440 | tf_op jit(solution)/shard_map/ppermute | solution.py:20
  17.2 4.9 %collective-permute-start.2 = (f32[256]{0:T(256)S(1)}, f32[256]{0:T(256)S(1)}, u32[]{:S(2)}, u32[]{:S(2)}) collective-permute-start(f32[256]{0:T(256)S(1)} %bitcast.60), channel_id=1, source_target_pairs={{0,1},{1,2},{2,3},{3,4},{4,5},{5,6},{6,7},{8,9},{9,10},{10,11},{11... | collective-permute-start | bytes 3080 | tf_op jit(solution)/shard_map/ppermute | solution.py:20
  24.2 9.8 %collective-permute-start.5 = (f32[256,256]{1,0:T(8,128)S(1)}, f32[256,256]{1,0:T(8,128)S(1)}, u32[]{:S(2)}, u32[]{:S(2)}) collective-permute-start(f32[256,256]{1,0:T(8,128)S(1)} %multiply_add_fusion.1), channel_id=1, source_target_pairs={{0,4},{1,5},{2,6},{3,7},{8,12},{9,13},{10,14},{11,15},{16,20},{17,... | collective-permute-start | bytes 786440 | tf_op jit(solution)/shard_map/ppermute | solution.py:20
  25.5 5.5 %collective-permute-start.4 = (f32[256]{0:T(256)S(1)}, f32[256]{0:T(256)S(1)}, u32[]{:S(2)}, u32[]{:S(2)}) collective-permute-start(f32[256]{0:T(256)S(1)} %mul.44), channel_id=1, source_target_pairs={{0,2},{1,3},{2,4},{3,5},{4,6},{5,7},{8,10},{9,11},{10,12},{11,13},... | collective-permute-start | bytes 3080 | tf_op jit(solution)/shard_map/ppermute | solution.py:20
  46.6 28.0 %all-to-all-start.1 = ((f32[16,1,1024]{2,1,0:T(1,128)}), f32[16,1,1024]{2,1,0:T(1,128)S(1)}, u32[]{:S(2)}, u32[]{:S(2)}) async-start(f32[16,1,1024]{2,1,0:T(1,128)} %bitcast.3), calls=%async_computation.1 | async-start | bytes 131072 | tf_op jit(solution)/shard_map/all_to_all | solution.py:50
  74.6 11.5 %all-to-all-start.4 = ((f32[4,1,32768]{2,1,0:T(1,128)}), f32[4,1,32768]{2,1,0:T(1,128)S(1)}, u32[]{:S(2)}, u32[]{:S(2)}) async-start(f32[4,1,32768]{2,1,0:T(1,128)} %all_to_all.53), calls=%async_computation.4 | async-start | bytes 1048576 | tf_op jit(solution)/shard_map/all_to_all | solution.py:50
  102.6 10.1 %all-to-all-start.3 = ((f32[4,1,16384]{2,1,0:T(1,128)}), f32[4,1,16384]{2,1,0:T(1,128)S(1)}, u32[]{:S(2)}, u32[]{:S(2)}) async-start(f32[4,1,16384]{2,1,0:T(1,128)} %broadcast_in_dim.45), calls=%async_computation.3 | async-start | bytes 524288 | tf_op jit(solution)/shard_map/all_to_all | solution.py:57
  112.6 16.6 %all-to-all-start.5 = ((f32[16,1,2048]{2,1,0:T(1,128)}), f32[16,1,2048]{2,1,0:T(1,128)S(1)}, u32[]{:S(2)}, u32[]{:S(2)}) async-start(f32[16,1,2048]{2,1,0:T(1,128)} %bitcast.13), calls=%async_computation.5 | async-start | bytes 262144 | tf_op jit(solution)/shard_map/all_to_all | solution.py:50
  130.0 59.7 %all-to-all-start.6 = ((f32[16,1,2048]{2,1,0:T(1,128)}), f32[16,1,2048]{2,1,0:T(1,128)S(1)}, u32[]{:S(2)}, u32[]{:S(2)}) async-start(f32[16,1,2048]{2,1,0:T(1,128)} %broadcast_in_dim.48), calls=%async_computation.6 | async-start | bytes 262144 | tf_op jit(solution)/shard_map/all_to_all | solution.py:57
  190.8 11.5 %all-to-all-start.7 = ((f32[4,1,32768]{2,1,0:T(1,128)}), f32[4,1,32768]{2,1,0:T(1,128)S(1)}, u32[]{:S(2)}, u32[]{:S(2)}) async-start(f32[4,1,32768]{2,1,0:T(1,128)} %broadcast_in_dim.50), calls=%async_computation.7 | async-start | bytes 1048576 | tf_op jit(solution)/shard_map/all_to_all | solution.py:57

commit v4 on v2

--- a/solution.py
+++ b/solution.py
@@ -66,6 +66,19 @@
     return flat.reshape(x.shape)
 
 
+def factor_and_invert(gram):
+    h = gram.shape[0] // 2
+    eye = jnp.eye(h, dtype=jnp.float32)
+    l11 = lax.linalg.cholesky(gram[:h, :h])
+    i11 = lax.linalg.triangular_solve(l11, eye, left_side=True, lower=True)
+    l21 = jnp.dot(gram[h:, :h], i11.T, precision=HIGH)
+    l22 = lax.linalg.cholesky(gram[h:, h:] - jnp.dot(l21, l21.T, precision=HIGH))
+    i22 = lax.linalg.triangular_solve(l22, eye, left_side=True, lower=True)
+    x21 = -jnp.dot(i22, jnp.dot(l21, i11, precision=HIGH), precision=HIGH)
+    zero = jnp.zeros((h, h), jnp.float32)
+    return jnp.block([[l11, zero], [l21, l22]]), jnp.block([[i11, zero], [x21, i22]])
+
+
 def shards(frames, tap_table, sketch_matrix, decay_rates):
     rows_here, frame_count = frames.shape
     npoints = rows_here * math.prod(lax.axis_size(a) for a in ROWS)
@@ -83,13 +96,17 @@
     filtered = (main + jnp.pad(edge, ((0, 0), (0, frame_count - BLOCK)))).astype(jnp.bfloat16)
     sketched = jnp.dot(filtered, sketch_matrix, preferred_element_type=jnp.float32)
 
-    weighted = sketched
+    factors = []
     factor = decay_rates[0]
     d = 1
     while d < batch_count:
-        got_w, got_f = shifted((weighted, factor), BATCH, d)
-        weighted = weighted + factor[None, :] * got_w
-        factor = factor * got_f
+        factors.append(factor)
+        factor = factor * shifted(factor, BATCH, d)
+        d *= 2
+    weighted = sketched
+    d = 1
+    for factor in factors:
+        weighted = weighted + factor[None, :] * shifted(weighted, BATCH, d)
         d *= 2
 
     root_points = math.sqrt(npoints)
@@ -101,10 +118,7 @@
     summed = reduce_rows(partial)
     gram = summed[:, :rank_count]
     cross = summed[:, rank_count:]
-    lower_one = jnp.linalg.cholesky(gram)
-    inverse = lax.linalg.triangular_solve(
-        lower_one, jnp.eye(rank_count, dtype=jnp.float32), left_side=True, lower=True
-    )
+    lower_one, inverse = factor_and_invert(gram)
     scaled = jnp.dot(weighted, inverse.T, precision=HIGH) * root_points
     projected = jnp.dot(inverse, cross, precision=HIGH) * (math.sqrt(rank_count) / root_points)
     upper = lower_one.T / root_points

time: 182 us -> 167 us (0.918)
  blocking collectives: 60.4 us -> 72.3 us
  waiting for transfers between devices: 28.1 us -> 18.9 us
  other arithmetic: 58.5 us -> 50.6 us
  local copies, waits for them, and re-layouts: 9.43 us -> 4.8 us
  starting transfers between devices: 13.3 us -> 9.63 us
    all_to_all x1 -> x2, blocking collectives: 18.2 us -> 30.1 us  [gather_back(): return lax.all_to_all(spread, axis, 0, 0, tiled=True).reshape(-1)]
    all_to_all x1 -> x0, waiting for transfers between devices: 9.22 us -> none  [gather_back(): return lax.all_to_all(spread, axis, 0, 0, tiled=True).reshape(-1)]
    another operation x8 -> x10, other arithmetic: 53.8 us -> 45.9 us  [the longest x3 12.6 us: factor_and_invert(): lax.linalg.cholesky(gram[h:, h:] - jnp.dot(l21, l21.T, precision=HIGH))]
    another operation x9 -> x1, local copies, waits for them, and re-layouts: 4.05 us -> 0.09 us  [factor_and_invert(): i22 = lax.linalg.triangular_solve(l22, eye, left_side=True, lower=True)]
    all_to_all x1 -> x0, starting transfers between devices: 3.67 us -> none  [gather_back(): return lax.all_to_all(spread, axis, 0, 0, tiled=True).reshape(-1)]
  transfers between devices with their start and end apart: 7 -> 6, of which waited for: 7 -> 6; matrix products, arithmetic and copies ran while one was open for 1% -> 1% of each run, Pallas kernels for 1% -> 1%
where the time goes in v4:
time: 167 us; the launch traced here: 166 us
  blocking collectives  72.3 us (43%)
  other arithmetic  50.6 us (30%)
  waiting for transfers between devices  18.9 us (11%)
  starting transfers between devices  9.63 us (6%)
  matrix products  6.79 us (4%)
  local copies, waits for them, and re-layouts  4.8 us (3%)
    all_to_all x2, blocking collectives, scatter_sum(): got = lax.all_to_all(flat.reshape(count, -1), axis, 0, 0, tiled=True)  42.2 us
    all_to_all x2, blocking collectives, gather_back(): return lax.all_to_all(spread, axis, 0, 0, tiled=True).reshape(-1)  30.1 us
    ppermute x6, waiting for transfers between devices, shifted(): return lax.ppermute(x, axis, pairs)  18.9 us
    another operation x3, other arithmetic, factor_and_invert(): lax.linalg.cholesky(gram[h:, h:] - jnp.dot(l21, l21.T, precision=HIGH))  12.6 us
    another operation x3, other arithmetic, factor_and_invert(): l11 = lax.linalg.cholesky(gram[:h, :h])  12.4 us
    another operation x2, other arithmetic, factor_and_invert(): i11 = lax.linalg.triangular_solve(l11, eye, left_side=True, lower=True)  10.5 us
    another operation x2, other arithmetic, factor_and_invert(): i22 = lax.linalg.triangular_solve(l22, eye, left_side=True, lower=True)  10.5 us
    ppermute x6, starting transfers between devices, shifted(): return lax.ppermute(x, axis, pairs)  9.63 us
  transfers between devices with their start and end apart: 6, of which 6 were waited for; matrix products, arithmetic and copies ran while one was open for 1% of the time, Pallas kernels for 1%

profile of v4, /device:TPU:24, one launch (start us, length us, event | category | flops | bytes accessed | tf_op | source)
XLA Modules:
  0.0 165.5 jit_solution(2393212336042153468)
XLA Ops:
  1.6 1.9 %collective-permute-start = (bf16[256,128]{1,0:T(8,128)(2,1)S(1)}, bf16[256,128]{1,0:T(8,128)(2,1)S(1)}, u32[]{:S(2)}, u32[]{:S(2)}) collective-permute-start(bf16[256,128]{1,0:T(8,128)(2,1)S(1)} %slice.23), channel_id=1, source_target_pairs={{0,1},{1,2},{2,3},{3,4},{4,5},{5,6},{6,7},{8,9},{9,10},{10,11},{11... | collective-permute-start | bytes 196616 | tf_op jit(solution)/shard_map/ppermute | solution.py:20
  3.5 1.2 convert_convert_fusion.coefs_ref
  4.7 1.6 shard_map.67
  9.5 1.9 %collective-permute-start.1 = (f32[256,256]{0,1:T(8,128)S(1)}, f32[256,256]{0,1:T(8,128)S(1)}, u32[]{:S(2)}, u32[]{:S(2)}) collective-permute-start(f32[256,256]{0,1:T(8,128)S(1)} %fusion.56), channel_id=1, source_target_pairs={{0,1},{1,2},{2,3},{3,4},{4,5},{5,6},{6,7},{8,9},{9,10},{10,11},{11... | collective-permute-start | bytes 786440 | tf_op jit(solution)/shard_map/ppermute | solution.py:20
  11.4 5.8 %collective-permute-done.1 = f32[256,256]{0,1:T(8,128)S(1)} collective-permute-done((f32[256,256]{0,1:T(8,128)S(1)}, f32[256,256]{0,1:T(8,128)S(1)}, u32[]{:S(2)}, u32[]{:S(2)}) %collective-permute-start.1) | collective-permute-done | bytes 262176 | tf_op jit(solution)/shard_map/ppermute | solution.py:20
  17.3 1.3 collective-permute-start.3
  18.6 1.9 %collective-permute-start.2 = (f32[256]{0:T(256)S(1)}, f32[256]{0:T(256)S(1)}, u32[]{:S(2)}, u32[]{:S(2)}) collective-permute-start(f32[256]{0:T(256)S(1)} %bitcast.49), channel_id=1, source_target_pairs={{0,1},{1,2},{2,3},{3,4},{4,5},{5,6},{6,7},{8,9},{9,10},{10,11},{11... | collective-permute-start | bytes 3080 | tf_op jit(solution)/shard_map/ppermute | solution.py:20
  20.6 3.0 %collective-permute-done.2 = f32[256]{0:T(256)S(1)} collective-permute-done((f32[256]{0:T(256)S(1)}, f32[256]{0:T(256)S(1)}, u32[]{:S(2)}, u32[]{:S(2)}) %collective-permute-start.2) | collective-permute-done | bytes 1056 | tf_op jit(solution)/shard_map/ppermute | solution.py:20
  23.5 2.1 %collective-permute-done.3 = f32[256,256]{0,1:T(8,128)S(1)} collective-permute-done((f32[256,256]{0,1:T(8,128)S(1)}, f32[256,256]{0,1:T(8,128)S(1)}, u32[]{:S(2)}, u32[]{:S(2)}) %collective-permute-start.3) | collective-permute-done | bytes 262176 | tf_op jit(solution)/shard_map/ppermute | solution.py:20
  25.7 1.3 collective-permute-start.5
  27.0 1.3 collective-permute-start.4
  28.3 4.2 %collective-permute-done.4 = f32[256]{0:T(256)S(1)} collective-permute-done((f32[256]{0:T(256)S(1)}, f32[256]{0:T(256)S(1)}, u32[]{:S(2)}, u32[]{:S(2)}) %collective-permute-start.4) | collective-permute-done | bytes 1056 | tf_op jit(solution)/shard_map/ppermute | solution.py:20
  32.5 3.0 %collective-permute-done.5 = f32[256,256]{0,1:T(8,128)S(1)} collective-permute-done((f32[256,256]{0,1:T(8,128)S(1)}, f32[256,256]{0,1:T(8,128)S(1)}, u32[]{:S(2)}, u32[]{:S(2)}) %collective-permute-start.5) | collective-permute-done | bytes 262176 | tf_op jit(solution)/shard_map/ppermute | solution.py:20
  37.2 13.6 %all_to_all.31 = f32[4,1,49152]{2,1,0:T(1,128)S(1)} all-to-all(f32[4,1,49152]{2,1,0:T(1,128)S(1)} %all_to_all.26), channel_id=1, replica_groups=mesh['x'=4,'z'=16,'y'=4,'core'=2] {'x'}, dimensions={0} | all-to-all | bytes 1572864 | tf_op jit(solution)/shard_map/all_to_all | solution.py:50
  51.5 28.7 %all_to_all.32 = f32[16,1,3072]{2,1,0:T(1,128)S(1)} all-to-all(f32[16,1,3072]{2,1,0:T(1,128)S(1)} %bitcast.46), channel_id=1, replica_groups=mesh['x'=4,'z'=16,'y'=4,'core'=2] {'z'}, dimensions={0} | all-to-all | bytes 393216 | tf_op jit(solution)/shard_map/all_to_all | solution.py:50
  80.4 18.2 %all_to_all.33 = f32[16,1,3072]{2,1,0:T(1,128)S(1)} all-to-all(f32[16,1,3072]{2,1,0:T(1,128)S(1)} %broadcast_in_dim.28), channel_id=1, replica_groups=mesh['x'=4,'z'=16,'y'=4,'core'=2] {'z'}, dimensions={0} | all-to-all | bytes 393216 | tf_op jit(solution)/shard_map/all_to_all | solution.py:57
  99.0 11.9 %all_to_all.34 = f32[4,1,49152]{2,1,0:T(1,128)S(1)} all-to-all(f32[4,1,49152]{2,1,0:T(1,128)S(1)} %broadcast_in_dim.30), channel_id=1, replica_groups=mesh['x'=4,'z'=16,'y'=4,'core'=2] {'x'}, dimensions={0} | all-to-all | bytes 1572864 | tf_op jit(solution)/shard_map/all_to_all | solution.py:57
  110.9 2.3 %reduce.22 = f32[4,49152]{1,0:T(4,128)S(1)} reduce(f32[4,1,49152]{2,1,0:T(1,128)S(1)} %all_to_all.34, f32[]{:T(128)} %constant.43), dimensions={1}, to_apply=%all_to_all.25.reduce_sub_computation | reduce | bytes 1572868 | tf_op jit(solution)/shard_map/all_to_all | solution.py:57
  113.9 11.7 %custom-call.8 = f32[128,128]{1,0:T(8,128)S(1)} custom-call(f32[128,128]{1,0:T(8,128)S(1)} %get-tuple-element.29), custom_call_target="Cholesky" | custom-call | tf_op jit(solution)/shard_map/cholesky/custom-call.1 | solution.py:72
  126.9 9.8 %custom-call.9 = f32[1,128,128]{1,2,0:T(8,128)S(1)} custom-call(f32[1,128,128]{2,1,0:T(8,128)S(1)} %get-tuple-element.26), custom_call_target="InvertDiagBlocksLowerTriangular" | custom-call | tf_op jit(solution)/shard_map/triangular_solve/custom-call.0 | solution.py:73
  138.2 11.9 %custom-call.10 = f32[128,128]{1,0:T(8,128)S(1)} custom-call(f32[128,128]{1,0:T(8,128)S(1)} %fusion.51), custom_call_target="Cholesky" | custom-call | tf_op jit(solution)/shard_map/cholesky/custom-call.1 | solution.py:75
  151.5 9.8 %custom-call.11 = f32[1,128,128]{1,2,0:T(8,128)S(1)} custom-call(f32[1,128,128]{2,1,0:T(8,128)S(1)} %get-tuple-element.24), custom_call_target="InvertDiagBlocksLowerTriangular" | custom-call | tf_op jit(solution)/shard_map/triangular_solve/custom-call.0 | solution.py:76
  161.9 1.4 fusion
  163.4 1.3 fusion.1
  (50 shorter events, 13.7 us)
Async XLA Ops:
  0.6 8.6 %copy-start = (bf16[512,256]{1,0:T(8,128)(2,1)S(1)}, bf16[512,256]{1,0:T(8,128)(2,1)}, u32[]{:S(2)}) copy-start(bf16[512,256]{1,0:T(8,128)(2,1)} %param.9) | copy-start | bytes 786436
  0.6 7.5 %copy-start.2 = (bf16[256,512]{1,0:T(8,128)(2,1)S(1)}, bf16[256,512]{1,0:T(8,128)(2,1)}, u32[]{:S(2)}) copy-start(bf16[256,512]{1,0:T(8,128)(2,1)} %param.7) | copy-start | bytes 786436
  1.6 5.6 %collective-permute-start = (bf16[256,128]{1,0:T(8,128)(2,1)S(1)}, bf16[256,128]{1,0:T(8,128)(2,1)S(1)}, u32[]{:S(2)}, u32[]{:S(2)}) collective-permute-start(bf16[256,128]{1,0:T(8,128)(2,1)S(1)} %slice.23), channel_id=1, source_target_pairs={{0,1},{1,2},{2,3},{3,4},{4,5},{5,6},{6,7},{8,9},{9,10},{10,11},{11... | collective-permute-start | bytes 196616 | tf_op jit(solution)/shard_map/ppermute | solution.py:20
  7.1 1.0 copy-start.4
  8.1 0.8 copy-start.1
  9.5 7.7 %copy-start.3 = (f32[1,256]{1,0:T(1,128)S(1)}, f32[1,256]{1,0:T(1,128)}, u32[]{:S(2)}) copy-start(f32[1,256]{1,0:T(1,128)} %param.10) | copy-start | bytes 3076
  9.5 7.7 %collective-permute-start.1 = (f32[256,256]{0,1:T(8,128)S(1)}, f32[256,256]{0,1:T(8,128)S(1)}, u32[]{:S(2)}, u32[]{:S(2)}) collective-permute-start(f32[256,256]{0,1:T(8,128)S(1)} %fusion.56), channel_id=1, source_target_pairs={{0,1},{1,2},{2,3},{3,4},{4,5},{5,6},{6,7},{8,9},{9,10},{10,11},{11... | collective-permute-start | bytes 786440 | tf_op jit(solution)/shard_map/ppermute | solution.py:20
  17.3 8.3 %collective-permute-start.3 = (f32[256,256]{0,1:T(8,128)S(1)}, f32[256,256]{0,1:T(8,128)S(1)}, u32[]{:S(2)}, u32[]{:S(2)}) collective-permute-start(f32[256,256]{0,1:T(8,128)S(1)} %multiply_add_fusion.2), channel_id=1, source_target_pairs={{0,2},{1,3},{2,4},{3,5},{4,6},{5,7},{8,10},{9,11},{10,12},{11,13},... | collective-permute-start | bytes 786440 | tf_op jit(solution)/shard_map/ppermute | solution.py:20
  18.6 4.9 %collective-permute-start.2 = (f32[256]{0:T(256)S(1)}, f32[256]{0:T(256)S(1)}, u32[]{:S(2)}, u32[]{:S(2)}) collective-permute-start(f32[256]{0:T(256)S(1)} %bitcast.49), channel_id=1, source_target_pairs={{0,1},{1,2},{2,3},{3,4},{4,5},{5,6},{6,7},{8,9},{9,10},{10,11},{11... | collective-permute-start | bytes 3080 | tf_op jit(solution)/shard_map/ppermute | solution.py:20
  25.7 9.8 %collective-permute-start.5 = (f32[256,256]{0,1:T(8,128)S(1)}, f32[256,256]{0,1:T(8,128)S(1)}, u32[]{:S(2)}, u32[]{:S(2)}) collective-permute-start(f32[256,256]{0,1:T(8,128)S(1)} %multiply_add_fusion.1), channel_id=1, source_target_pairs={{0,4},{1,5},{2,6},{3,7},{8,12},{9,13},{10,14},{11,15},{16,20},{17,... | collective-permute-start | bytes 786440 | tf_op jit(solution)/shard_map/ppermute | solution.py:20
  27.0 5.5 %collective-permute-start.4 = (f32[256]{0:T(256)S(1)}, f32[256]{0:T(256)S(1)}, u32[]{:S(2)}, u32[]{:S(2)}) collective-permute-start(f32[256]{0:T(256)S(1)} %mul.44), channel_id=1, source_target_pairs={{0,2},{1,3},{2,4},{3,5},{4,6},{5,7},{8,10},{9,11},{10,12},{11,13},... | collective-permute-start | bytes 3080 | tf_op jit(solution)/shard_map/ppermute | solution.py:20

commit v5 on v4

--- a/solution.py
+++ b/solution.py
@@ -96,17 +96,18 @@
     filtered = (main + jnp.pad(edge, ((0, 0), (0, frame_count - BLOCK)))).astype(jnp.bfloat16)
     sketched = jnp.dot(filtered, sketch_matrix, preferred_element_type=jnp.float32)
 
-    factors = []
-    factor = decay_rates[0]
+    weighted = sketched
+    factor = jnp.broadcast_to(decay_rates[0][None, :], (8, weighted.shape[1]))
     d = 1
     while d < batch_count:
-        factors.append(factor)
-        factor = factor * shifted(factor, BATCH, d)
-        d *= 2
-    weighted = sketched
-    d = 1
-    for factor in factors:
-        weighted = weighted + factor[None, :] * shifted(weighted, BATCH, d)
+        if 2 * d < batch_count:
+            got = shifted(jnp.concatenate([weighted, factor], axis=0), BATCH, d)
+            got_w, got_f = got[: weighted.shape[0]], got[weighted.shape[0] :]
+        else:
+            got_w, got_f = shifted(weighted, BATCH, d), None
+        weighted = weighted + factor[:1] * got_w
+        if got_f is not None:
+            factor = factor * got_f
         d *= 2
 
     root_points = math.sqrt(npoints)

time: 167 us -> 172 us (1.030)
  waiting for transfers between devices: 18.9 us -> 26.1 us
  starting transfers between devices: 9.63 us -> 6.41 us
    ppermute x6 -> x4, waiting for transfers between devices: 18.9 us -> 26.1 us  [shifted(): return lax.ppermute(x, axis, pairs)]
    ppermute x6 -> x4, starting transfers between devices: 9.63 us -> 6.41 us  [shifted(): return lax.ppermute(x, axis, pairs)]
  transfers between devices with their start and end apart: 6 -> 4, of which waited for: 6 -> 4; matrix products, arithmetic and copies ran while one was open for 1% -> 1% of each run, Pallas kernels for 1% -> 1%
where the time goes in v5:
time: 172 us; the launch traced here: 171 us
  blocking collectives  72.4 us (42%)
  other arithmetic  50.9 us (30%)
  waiting for transfers between devices  26.1 us (15%)
  matrix products  6.79 us (4%)
  starting transfers between devices  6.41 us (4%)
  local copies, waits for them, and re-layouts  5.57 us (3%)
    all_to_all x2, blocking collectives, scatter_sum(): got = lax.all_to_all(flat.reshape(count, -1), axis, 0, 0, tiled=True)  42.3 us
    all_to_all x2, blocking collectives, gather_back(): return lax.all_to_all(spread, axis, 0, 0, tiled=True).reshape(-1)  30.1 us
    ppermute x4, waiting for transfers between devices, shifted(): return lax.ppermute(x, axis, pairs)  26.1 us
    another operation x3, other arithmetic, factor_and_invert(): lax.linalg.cholesky(gram[h:, h:] - jnp.dot(l21, l21.T, precision=HIGH))  12.6 us
    another operation x3, other arithmetic, factor_and_invert(): l11 = lax.linalg.cholesky(gram[:h, :h])  12.4 us
    another operation x2, other arithmetic, factor_and_invert(): i11 = lax.linalg.triangular_solve(l11, eye, left_side=True, lower=True)  10.5 us
    another operation x2, other arithmetic, factor_and_invert(): i22 = lax.linalg.triangular_solve(l22, eye, left_side=True, lower=True)  10.5 us
    ppermute x4, starting transfers between devices, shifted(): return lax.ppermute(x, axis, pairs)  6.41 us
  transfers between devices with their start and end apart: 4, of which 4 were waited for; matrix products, arithmetic and copies ran while one was open for 1% of the time, Pallas kernels for 1%

profile of v5, /device:TPU:24, one launch (start us, length us, event | category | flops | bytes accessed | tf_op | source)
XLA Modules:
  0.0 170.7 jit_solution(854840720767834999)
XLA Ops:
  0.7 0.9 slice.42
  1.6 1.9 %collective-permute-start = (bf16[256,128]{1,0:T(8,128)(2,1)S(1)}, bf16[256,128]{1,0:T(8,128)(2,1)S(1)}, u32[]{:S(2)}, u32[]{:S(2)}) collective-permute-start(bf16[256,128]{1,0:T(8,128)(2,1)S(1)} %slice.42), channel_id=1, source_target_pairs={{0,1},{1,2},{2,3},{3,4},{4,5},{5,6},{6,7},{8,9},{9,10},{10,11},{11... | collective-permute-start | bytes 196616 | tf_op jit(solution)/shard_map/ppermute | solution.py:20
  3.5 1.2 convert_convert_fusion.coefs_ref
  4.7 1.6 shard_map.67
  6.2 0.9 collective-permute-done
  7.1 1.0 convolution_bitcast_fusion.1
  10.3 1.9 %collective-permute-start.1 = (f32[264,256]{0,1:T(8,128)S(1)}, f32[264,256]{0,1:T(8,128)S(1)}, u32[]{:S(2)}, u32[]{:S(2)}) collective-permute-start(f32[264,256]{0,1:T(8,128)S(1)} %pad_maximum_fusion), channel_id=1, source_target_pairs={{0,1},{1,2},{2,3},{3,4},{4,5},{5,6},{6,7},{8,9},{9,10},{10,11},{11... | collective-permute-start | bytes 811016 | tf_op jit(solution)/shard_map/ppermute | solution.py:20
  12.3 7.2 %collective-permute-done.1 = f32[264,256]{0,1:T(8,128)S(1)} collective-permute-done((f32[264,256]{0,1:T(8,128)S(1)}, f32[264,256]{0,1:T(8,128)S(1)}, u32[]{:S(2)}, u32[]{:S(2)}) %collective-permute-start.1) | collective-permute-done | bytes 270368 | tf_op jit(solution)/shard_map/ppermute | solution.py:20
  19.7 1.3 collective-permute-start.2
  21.0 9.5 %collective-permute-done.2 = f32[264,256]{0,1:T(8,128)S(1)} collective-permute-done((f32[264,256]{0,1:T(8,128)S(1)}, f32[264,256]{0,1:T(8,128)S(1)}, u32[]{:S(2)}, u32[]{:S(2)}) %collective-permute-start.2) | collective-permute-done | bytes 270368 | tf_op jit(solution)/shard_map/ppermute | solution.py:20
  30.8 1.3 collective-permute-start.3
  32.1 8.5 %collective-permute-done.3 = f32[256,256]{0,1:T(8,128)S(1)} collective-permute-done((f32[256,256]{0,1:T(8,128)S(1)}, f32[256,256]{0,1:T(8,128)S(1)}, u32[]{:S(2)}, u32[]{:S(2)}) %collective-permute-start.3) | collective-permute-done | bytes 262176 | tf_op jit(solution)/shard_map/ppermute | solution.py:20
  42.3 13.6 %all_to_all.31 = f32[4,1,49152]{2,1,0:T(1,128)S(1)} all-to-all(f32[4,1,49152]{2,1,0:T(1,128)S(1)} %all_to_all.26), channel_id=1, replica_groups=mesh['x'=4,'z'=16,'y'=4,'core'=2] {'x'}, dimensions={0} | all-to-all | bytes 1572864 | tf_op jit(solution)/shard_map/all_to_all | solution.py:50
  56.6 28.7 %all_to_all.32 = f32[16,1,3072]{2,1,0:T(1,128)S(1)} all-to-all(f32[16,1,3072]{2,1,0:T(1,128)S(1)} %bitcast.46), channel_id=1, replica_groups=mesh['x'=4,'z'=16,'y'=4,'core'=2] {'z'}, dimensions={0} | all-to-all | bytes 393216 | tf_op jit(solution)/shard_map/all_to_all | solution.py:50
  85.5 18.2 %all_to_all.33 = f32[16,1,3072]{2,1,0:T(1,128)S(1)} all-to-all(f32[16,1,3072]{2,1,0:T(1,128)S(1)} %broadcast_in_dim.35), channel_id=1, replica_groups=mesh['x'=4,'z'=16,'y'=4,'core'=2] {'z'}, dimensions={0} | all-to-all | bytes 393216 | tf_op jit(solution)/shard_map/all_to_all | solution.py:57
  104.2 11.9 %all_to_all.34 = f32[4,1,49152]{2,1,0:T(1,128)S(1)} all-to-all(f32[4,1,49152]{2,1,0:T(1,128)S(1)} %broadcast_in_dim.37), channel_id=1, replica_groups=mesh['x'=4,'z'=16,'y'=4,'core'=2] {'x'}, dimensions={0} | all-to-all | bytes 1572864 | tf_op jit(solution)/shard_map/all_to_all | solution.py:57
  116.1 2.3 %reduce.24 = f32[4,49152]{1,0:T(4,128)S(1)} reduce(f32[4,1,49152]{2,1,0:T(1,128)S(1)} %all_to_all.34, f32[]{:T(128)} %constant.43), dimensions={1}, to_apply=%all_to_all.25.reduce_sub_computation | reduce | bytes 1572868 | tf_op jit(solution)/shard_map/all_to_all | solution.py:57
  119.0 11.7 %custom-call.8 = f32[128,128]{1,0:T(8,128)S(1)} custom-call(f32[128,128]{1,0:T(8,128)S(1)} %get-tuple-element.31), custom_call_target="Cholesky" | custom-call | tf_op jit(solution)/shard_map/cholesky/custom-call.1 | solution.py:72
  132.1 9.8 %custom-call.9 = f32[1,128,128]{1,2,0:T(8,128)S(1)} custom-call(f32[1,128,128]{2,1,0:T(8,128)S(1)} %get-tuple-element.28), custom_call_target="InvertDiagBlocksLowerTriangular" | custom-call | tf_op jit(solution)/shard_map/triangular_solve/custom-call.0 | solution.py:73
  143.4 11.9 %custom-call.10 = f32[128,128]{1,0:T(8,128)S(1)} custom-call(f32[128,128]{1,0:T(8,128)S(1)} %fusion.54), custom_call_target="Cholesky" | custom-call | tf_op jit(solution)/shard_map/cholesky/custom-call.1 | solution.py:75
  156.6 9.8 %custom-call.11 = f32[1,128,128]{1,2,0:T(8,128)S(1)} custom-call(f32[1,128,128]{2,1,0:T(8,128)S(1)} %get-tuple-element.26), custom_call_target="InvertDiagBlocksLowerTriangular" | custom-call | tf_op jit(solution)/shard_map/triangular_solve/custom-call.0 | solution.py:76
  167.1 1.4 fusion
  168.5 1.3 fusion.1
  169.8 0.8 copy.64
  (50 shorter events, 11.1 us)
Async XLA Ops:
  0.6 8.6 %copy-start = (bf16[512,256]{1,0:T(8,128)(2,1)S(1)}, bf16[512,256]{1,0:T(8,128)(2,1)}, u32[]{:S(2)}) copy-start(bf16[512,256]{1,0:T(8,128)(2,1)} %param.9) | copy-start | bytes 786436
  0.6 7.5 %copy-start.2 = (bf16[256,512]{1,0:T(8,128)(2,1)S(1)}, bf16[256,512]{1,0:T(8,128)(2,1)}, u32[]{:S(2)}) copy-start(bf16[256,512]{1,0:T(8,128)(2,1)} %param.7) | copy-start | bytes 786436
  1.6 5.6 %collective-permute-start = (bf16[256,128]{1,0:T(8,128)(2,1)S(1)}, bf16[256,128]{1,0:T(8,128)(2,1)S(1)}, u32[]{:S(2)}, u32[]{:S(2)}) collective-permute-start(bf16[256,128]{1,0:T(8,128)(2,1)S(1)} %slice.42), channel_id=1, source_target_pairs={{0,1},{1,2},{2,3},{3,4},{4,5},{5,6},{6,7},{8,9},{9,10},{10,11},{11... | collective-permute-start | bytes 196616 | tf_op jit(solution)/shard_map/ppermute | solution.py:20
  7.1 1.0 copy-start.4
  8.1 0.8 copy-start.1
  9.5 0.7 copy-start.3
  10.3 9.1 %collective-permute-start.1 = (f32[264,256]{0,1:T(8,128)S(1)}, f32[264,256]{0,1:T(8,128)S(1)}, u32[]{:S(2)}, u32[]{:S(2)}) collective-permute-start(f32[264,256]{0,1:T(8,128)S(1)} %pad_maximum_fusion), channel_id=1, source_target_pairs={{0,1},{1,2},{2,3},{3,4},{4,5},{5,6},{6,7},{8,9},{9,10},{10,11},{11... | collective-permute-start | bytes 811016 | tf_op jit(solution)/shard_map/ppermute | solution.py:20
  19.7 10.8 %collective-permute-start.2 = (f32[264,256]{0,1:T(8,128)S(1)}, f32[264,256]{0,1:T(8,128)S(1)}, u32[]{:S(2)}, u32[]{:S(2)}) collective-permute-start(f32[264,256]{0,1:T(8,128)S(1)} %pad_maximum_fusion.1), channel_id=1, source_target_pairs={{0,2},{1,3},{2,4},{3,5},{4,6},{5,7},{8,10},{9,11},{10,12},{11,13},... | collective-permute-start | bytes 811016 | tf_op jit(solution)/shard_map/ppermute | solution.py:20
  30.8 9.8 %collective-permute-start.3 = (f32[256,256]{0,1:T(8,128)S(1)}, f32[256,256]{0,1:T(8,128)S(1)}, u32[]{:S(2)}, u32[]{:S(2)}) collective-permute-start(f32[256,256]{0,1:T(8,128)S(1)} %fusion.40), channel_id=1, source_target_pairs={{0,4},{1,5},{2,6},{3,7},{8,12},{9,13},{10,14},{11,15},{16,20},{17,... | collective-permute-start | bytes 786440 | tf_op jit(solution)/shard_map/ppermute | solution.py:20

commit v6 on v4

--- a/solution.py
+++ b/solution.py
@@ -66,14 +66,42 @@
     return flat.reshape(x.shape)
 
 
+def chol_kernel(g_ref, out_ref, a_ref):
+    n = g_ref.shape[0]
+    rows = lax.broadcasted_iota(jnp.int32, (n, n), 0)
+    cols = lax.broadcasted_iota(jnp.int32, (n, n), 1)
+    a_ref[:, :n] = g_ref[...]
+    a_ref[:, n:] = jnp.where(rows == cols, 1.0, 0.0).astype(jnp.float32)
+    sub = lax.broadcasted_iota(jnp.int32, (n, 2 * n), 0)
+    lane = lax.broadcasted_iota(jnp.int32, (n, 2 * n), 1)
+    lane_row = lax.broadcasted_iota(jnp.int32, (1, 2 * n), 1)
+
+    def step(j, carry):
+        row = a_ref[pl.ds(j, 1), :]
+        pivot = jnp.sum(jnp.where(lane_row == j, row, 0.0), axis=1, keepdims=True)
+        scale = 1.0 / jnp.sqrt(pivot)
+        top = jnp.where(lane_row >= j, row * scale, 0.0)
+        whole = a_ref[...]
+        column = jnp.sum(jnp.where(lane == j, whole, 0.0), axis=1, keepdims=True) * scale
+        a_ref[...] = jnp.where(sub > j, whole - column * top, jnp.where(sub == j, top, whole))
+        return carry
+
+    lax.fori_loop(0, n, step, 0)
+    out_ref[...] = a_ref[...]
+
+def factor_block(g):
+    n = g.shape[0]
+    vmem = pl.BlockSpec(memory_space=pltpu.VMEM)
+    out = pl.pallas_call(chol_kernel, out_shape=jax.ShapeDtypeStruct((n, 2 * n), jnp.float32),
+        in_specs=[vmem], out_specs=vmem, scratch_shapes=[pltpu.VMEM((n, 2 * n), jnp.float32)])(g)
+    return out[:, :n].T, out[:, n:]
+
+
 def factor_and_invert(gram):
     h = gram.shape[0] // 2
-    eye = jnp.eye(h, dtype=jnp.float32)
-    l11 = lax.linalg.cholesky(gram[:h, :h])
-    i11 = lax.linalg.triangular_solve(l11, eye, left_side=True, lower=True)
+    l11, i11 = factor_block(gram[:h, :h])
     l21 = jnp.dot(gram[h:, :h], i11.T, precision=HIGH)
-    l22 = lax.linalg.cholesky(gram[h:, h:] - jnp.dot(l21, l21.T, precision=HIGH))
-    i22 = lax.linalg.triangular_solve(l22, eye, left_side=True, lower=True)
+    l22, i22 = factor_block(gram[h:, h:] - jnp.dot(l21, l21.T, precision=HIGH))
     x21 = -jnp.dot(i22, jnp.dot(l21, i11, precision=HIGH), precision=HIGH)
     zero = jnp.zeros((h, h), jnp.float32)
     return jnp.block([[l11, zero], [l21, l22]]), jnp.block([[i11, zero], [x21, i22]])

time: 167 us -> 158 us (0.946)
  other arithmetic: 50.6 us -> 5.32 us
  Pallas kernels: 1.58 us -> 36.2 us
    another operation x10 -> x0, other arithmetic: 45.9 us -> none  [the longest x3 12.6 us: factor_and_invert(): lax.linalg.cholesky(gram[h:, h:] - jnp.dot(l21, l21.T, precision=HIGH))]
    pallas_call x0 -> x2, Pallas kernels: none -> 34.7 us  [factor_block(): pl.pallas_call(chol_kernel, out_shape=jax.ShapeDtypeStruct((n, 2 * n), jn...]
where the time goes in v6:
time: 158 us; the launch traced here: 156 us
  blocking collectives  72.3 us (46%)
  Pallas kernels  36.2 us (23%)
  waiting for transfers between devices  18.9 us (12%)
  starting transfers between devices  9.63 us (6%)
  matrix products  7.69 us (5%)
  other arithmetic  5.32 us (3%)
  local copies, waits for them, and re-layouts  5.11 us (3%)
    all_to_all x2, blocking collectives, scatter_sum(): got = lax.all_to_all(flat.reshape(count, -1), axis, 0, 0, tiled=True)  42.3 us
    pallas_call x2, Pallas kernels, factor_block(): pl.pallas_call(chol_kernel, out_shape=jax.ShapeDtypeStruct((n, 2 * n), jn...  34.7 us
    all_to_all x2, blocking collectives, gather_back(): return lax.all_to_all(spread, axis, 0, 0, tiled=True).reshape(-1)  30.1 us
    ppermute x6, waiting for transfers between devices, shifted(): return lax.ppermute(x, axis, pairs)  18.9 us
    ppermute x6, starting transfers between devices, shifted(): return lax.ppermute(x, axis, pairs)  9.63 us
  transfers between devices with their start and end apart: 6, of which 6 were waited for; matrix products, arithmetic and copies ran while one was open for 1% of the time, Pallas kernels for 1%

profile of v6, /device:TPU:24, one launch (start us, length us, event | category | flops | bytes accessed | tf_op | source)
XLA Modules:
  0.0 156.0 jit_solution(13974544696526043097)
XLA Ops:
  1.6 1.9 %collective-permute-start = (bf16[256,128]{1,0:T(8,128)(2,1)S(1)}, bf16[256,128]{1,0:T(8,128)(2,1)S(1)}, u32[]{:S(2)}, u32[]{:S(2)}) collective-permute-start(bf16[256,128]{1,0:T(8,128)(2,1)S(1)} %slice.31), channel_id=1, source_target_pairs={{0,1},{1,2},{2,3},{3,4},{4,5},{5,6},{6,7},{8,9},{9,10},{10,11},{11... | collective-permute-start | bytes 196616 | tf_op jit(solution)/shard_map/ppermute | solution.py:20
  3.5 1.2 convert_convert_fusion.coefs_ref
  4.7 1.6 %shard_map.67 = (bf16[128,128]{1,0:T(8,128)(2,1)}, bf16[128,128]{1,0:T(8,128)(2,1)}) custom-call(f32[63]{0:T(128)} %convert_convert_fusion.coefs_ref), custom_call_target="tpu_custom_call" | custom-call | tf_op jit(solution)/shard_map/pallas_call | solution.py:40
  7.1 1.0 convolution_bitcast_fusion.1
  9.5 1.9 %collective-permute-start.1 = (f32[256,256]{0,1:T(8,128)S(1)}, f32[256,256]{0,1:T(8,128)S(1)}, u32[]{:S(2)}, u32[]{:S(2)}) collective-permute-start(f32[256,256]{0,1:T(8,128)S(1)} %fusion.47), channel_id=1, source_target_pairs={{0,1},{1,2},{2,3},{3,4},{4,5},{5,6},{6,7},{8,9},{9,10},{10,11},{11... | collective-permute-start | bytes 786440 | tf_op jit(solution)/shard_map/ppermute | solution.py:20
  11.4 5.8 %collective-permute-done.1 = f32[256,256]{0,1:T(8,128)S(1)} collective-permute-done((f32[256,256]{0,1:T(8,128)S(1)}, f32[256,256]{0,1:T(8,128)S(1)}, u32[]{:S(2)}, u32[]{:S(2)}) %collective-permute-start.1) | collective-permute-done | bytes 262176 | tf_op jit(solution)/shard_map/ppermute | solution.py:20
  17.3 1.3 collective-permute-start.3
  18.6 1.9 %collective-permute-start.2 = (f32[256]{0:T(256)S(1)}, f32[256]{0:T(256)S(1)}, u32[]{:S(2)}, u32[]{:S(2)}) collective-permute-start(f32[256]{0:T(256)S(1)} %bitcast.32), channel_id=1, source_target_pairs={{0,1},{1,2},{2,3},{3,4},{4,5},{5,6},{6,7},{8,9},{9,10},{10,11},{11... | collective-permute-start | bytes 3080 | tf_op jit(solution)/shard_map/ppermute | solution.py:20
  20.5 3.0 %collective-permute-done.2 = f32[256]{0:T(256)S(1)} collective-permute-done((f32[256]{0:T(256)S(1)}, f32[256]{0:T(256)S(1)}, u32[]{:S(2)}, u32[]{:S(2)}) %collective-permute-start.2) | collective-permute-done | bytes 1056 | tf_op jit(solution)/shard_map/ppermute | solution.py:20
  23.5 2.1 %collective-permute-done.3 = f32[256,256]{0,1:T(8,128)S(1)} collective-permute-done((f32[256,256]{0,1:T(8,128)S(1)}, f32[256,256]{0,1:T(8,128)S(1)}, u32[]{:S(2)}, u32[]{:S(2)}) %collective-permute-start.3) | collective-permute-done | bytes 262176 | tf_op jit(solution)/shard_map/ppermute | solution.py:20
  25.7 1.3 collective-permute-start.5
  27.0 1.3 collective-permute-start.4
  28.3 4.2 %collective-permute-done.4 = f32[256]{0:T(256)S(1)} collective-permute-done((f32[256]{0:T(256)S(1)}, f32[256]{0:T(256)S(1)}, u32[]{:S(2)}, u32[]{:S(2)}) %collective-permute-start.4) | collective-permute-done | bytes 1056 | tf_op jit(solution)/shard_map/ppermute | solution.py:20
  32.5 3.0 %collective-permute-done.5 = f32[256,256]{0,1:T(8,128)S(1)} collective-permute-done((f32[256,256]{0,1:T(8,128)S(1)}, f32[256,256]{0,1:T(8,128)S(1)}, u32[]{:S(2)}, u32[]{:S(2)}) %collective-permute-start.5) | collective-permute-done | bytes 262176 | tf_op jit(solution)/shard_map/ppermute | solution.py:20
  37.2 13.6 %all_to_all.31 = f32[4,1,49152]{2,1,0:T(1,128)S(1)} all-to-all(f32[4,1,49152]{2,1,0:T(1,128)S(1)} %all_to_all.26), channel_id=1, replica_groups=mesh['x'=4,'z'=16,'y'=4,'core'=2] {'x'}, dimensions={0} | all-to-all | bytes 1572864 | tf_op jit(solution)/shard_map/all_to_all | solution.py:50
  51.5 28.7 %all_to_all.32 = f32[16,1,3072]{2,1,0:T(1,128)S(1)} all-to-all(f32[16,1,3072]{2,1,0:T(1,128)S(1)} %bitcast.29), channel_id=1, replica_groups=mesh['x'=4,'z'=16,'y'=4,'core'=2] {'z'}, dimensions={0} | all-to-all | bytes 393216 | tf_op jit(solution)/shard_map/all_to_all | solution.py:50
  80.4 18.2 %all_to_all.33 = f32[16,1,3072]{2,1,0:T(1,128)S(1)} all-to-all(f32[16,1,3072]{2,1,0:T(1,128)S(1)} %broadcast_in_dim.29), channel_id=1, replica_groups=mesh['x'=4,'z'=16,'y'=4,'core'=2] {'z'}, dimensions={0} | all-to-all | bytes 393216 | tf_op jit(solution)/shard_map/all_to_all | solution.py:57
  99.0 11.9 %all_to_all.34 = f32[4,1,49152]{2,1,0:T(1,128)S(1)} all-to-all(f32[4,1,49152]{2,1,0:T(1,128)S(1)} %broadcast_in_dim.31), channel_id=1, replica_groups=mesh['x'=4,'z'=16,'y'=4,'core'=2] {'x'}, dimensions={0} | all-to-all | bytes 1572864 | tf_op jit(solution)/shard_map/all_to_all | solution.py:57
  110.9 2.3 %reduce.2 = f32[4,49152]{1,0:T(4,128)S(1)} reduce(f32[4,1,49152]{2,1,0:T(1,128)S(1)} %all_to_all.34, f32[]{:T(128)} %constant.23), dimensions={1}, to_apply=%all_to_all.25.reduce_sub_computation | reduce | bytes 1572868 | tf_op jit(solution)/shard_map/all_to_all | solution.py:57
  114.4 17.3 %shard_map.68 = f32[128,256]{1,0:T(8,128)} custom-call(f32[128,128]{1,0:T(8,128)} %slice.40.g_ref), custom_call_target="tpu_custom_call" | custom-call | tf_op jit(solution)/shard_map/pallas_call | solution.py:95
  131.7 1.2 fusion.44
  134.1 17.3 %shard_map.69 = f32[128,256]{1,0:T(8,128)} custom-call(f32[128,128]{1,0:T(8,128)} %convolution_subtract_fusion.g_ref), custom_call_target="tpu_custom_call" | custom-call | tf_op jit(solution)/shard_map/pallas_call | solution.py:95
  152.6 1.4 fusion
  154.0 1.3 fusion.1
  (37 shorter events, 10.8 us)
Async XLA Ops:
  0.6 8.6 %copy-start = (bf16[512,256]{1,0:T(8,128)(2,1)S(1)}, bf16[512,256]{1,0:T(8,128)(2,1)}, u32[]{:S(2)}) copy-start(bf16[512,256]{1,0:T(8,128)(2,1)} %param.6) | copy-start | bytes 786436
  0.6 7.5 %copy-start.4 = (bf16[256,512]{1,0:T(8,128)(2,1)S(1)}, bf16[256,512]{1,0:T(8,128)(2,1)}, u32[]{:S(2)}) copy-start(bf16[256,512]{1,0:T(8,128)(2,1)} %param.4) | copy-start | bytes 786436
  1.6 5.6 %collective-permute-start = (bf16[256,128]{1,0:T(8,128)(2,1)S(1)}, bf16[256,128]{1,0:T(8,128)(2,1)S(1)}, u32[]{:S(2)}, u32[]{:S(2)}) collective-permute-start(bf16[256,128]{1,0:T(8,128)(2,1)S(1)} %slice.31), channel_id=1, source_target_pairs={{0,1},{1,2},{2,3},{3,4},{4,5},{5,6},{6,7},{8,9},{9,10},{10,11},{11... | collective-permute-start | bytes 196616 | tf_op jit(solution)/shard_map/ppermute | solution.py:20
  7.1 1.0 copy-start.6
  8.1 0.8 copy-start.3
  9.5 7.7 %copy-start.5 = (f32[1,256]{1,0:T(1,128)S(1)}, f32[1,256]{1,0:T(1,128)}, u32[]{:S(2)}) copy-start(f32[1,256]{1,0:T(1,128)} %param.7) | copy-start | bytes 3076
  9.5 7.7 %collective-permute-start.1 = (f32[256,256]{0,1:T(8,128)S(1)}, f32[256,256]{0,1:T(8,128)S(1)}, u32[]{:S(2)}, u32[]{:S(2)}) collective-permute-start(f32[256,256]{0,1:T(8,128)S(1)} %fusion.47), channel_id=1, source_target_pairs={{0,1},{1,2},{2,3},{3,4},{4,5},{5,6},{6,7},{8,9},{9,10},{10,11},{11... | collective-permute-start | bytes 786440 | tf_op jit(solution)/shard_map/ppermute | solution.py:20
  17.3 8.3 %collective-permute-start.3 = (f32[256,256]{0,1:T(8,128)S(1)}, f32[256,256]{0,1:T(8,128)S(1)}, u32[]{:S(2)}, u32[]{:S(2)}) collective-permute-start(f32[256,256]{0,1:T(8,128)S(1)} %multiply_add_fusion.2), channel_id=1, source_target_pairs={{0,2},{1,3},{2,4},{3,5},{4,6},{5,7},{8,10},{9,11},{10,12},{11,13},... | collective-permute-start | bytes 786440 | tf_op jit(solution)/shard_map/ppermute | solution.py:20
  18.6 4.9 %collective-permute-start.2 = (f32[256]{0:T(256)S(1)}, f32[256]{0:T(256)S(1)}, u32[]{:S(2)}, u32[]{:S(2)}) collective-permute-start(f32[256]{0:T(256)S(1)} %bitcast.32), channel_id=1, source_target_pairs={{0,1},{1,2},{2,3},{3,4},{4,5},{5,6},{6,7},{8,9},{9,10},{10,11},{11... | collective-permute-start | bytes 3080 | tf_op jit(solution)/shard_map/ppermute | solution.py:20
  25.7 9.8 %collective-permute-start.5 = (f32[256,256]{0,1:T(8,128)S(1)}, f32[256,256]{0,1:T(8,128)S(1)}, u32[]{:S(2)}, u32[]{:S(2)}) collective-permute-start(f32[256,256]{0,1:T(8,128)S(1)} %multiply_add_fusion.1), channel_id=1, source_target_pairs={{0,4},{1,5},{2,6},{3,7},{8,12},{9,13},{10,14},{11,15},{16,20},{17,... | collective-permute-start | bytes 786440 | tf_op jit(solution)/shard_map/ppermute | solution.py:20
  27.0 5.5 %collective-permute-start.4 = (f32[256]{0:T(256)S(1)}, f32[256]{0:T(256)S(1)}, u32[]{:S(2)}, u32[]{:S(2)}) collective-permute-start(f32[256]{0:T(256)S(1)} %mul.44), channel_id=1, source_target_pairs={{0,2},{1,3},{2,4},{3,5},{4,6},{5,7},{8,10},{9,11},{10,12},{11,13},... | collective-permute-start | bytes 3080 | tf_op jit(solution)/shard_map/ppermute | solution.py:20
  131.7 1.2 copy-start.1
  151.4 1.0 copy-start.2

commit v7 on v6

--- a/solution.py
+++ b/solution.py
@@ -72,22 +72,25 @@
     cols = lax.broadcasted_iota(jnp.int32, (n, n), 1)
     a_ref[:, :n] = g_ref[...]
     a_ref[:, n:] = jnp.where(rows == cols, 1.0, 0.0).astype(jnp.float32)
-    sub = lax.broadcasted_iota(jnp.int32, (n, 2 * n), 0)
-    lane = lax.broadcasted_iota(jnp.int32, (n, 2 * n), 1)
     lane_row = lax.broadcasted_iota(jnp.int32, (1, 2 * n), 1)
+    for lo in range(0, n, 8):
+        count = n - lo
+        sub = lax.broadcasted_iota(jnp.int32, (count, 2 * n), 0) + lo
+        lane = lax.broadcasted_iota(jnp.int32, (count, n), 1)
 
-    def step(j, carry):
-        row = a_ref[pl.ds(j, 1), :]
-        pivot = jnp.sum(jnp.where(lane_row == j, row, 0.0), axis=1, keepdims=True)
-        scale = 1.0 / jnp.sqrt(pivot)
-        top = jnp.where(lane_row >= j, row * scale, 0.0)
-        whole = a_ref[...]
-        column = jnp.sum(jnp.where(lane == j, whole, 0.0), axis=1, keepdims=True) * scale
-        a_ref[...] = jnp.where(sub > j, whole - column * top, jnp.where(sub == j, top, whole))
-        return carry
+        def step(j, carry, lo=lo, sub=sub, lane=lane):
+            row = a_ref[pl.ds(j, 1), :]
+            pivot = jnp.sum(jnp.where(lane_row == j, row, 0.0), axis=1, keepdims=True)
+            scale = 1.0 / jnp.sqrt(pivot)
+            top = jnp.where(lane_row >= j, row * scale, 0.0)
+            whole = a_ref[lo:, :]
+            column = jnp.sum(jnp.where(lane == j, whole[:, :n], 0.0), axis=1, keepdims=True) * scale
+            a_ref[lo:, :] = jnp.where(sub > j, whole - column * top, jnp.where(sub == j, top, whole))
+            return carry
 
-    lax.fori_loop(0, n, step, 0)
+        lax.fori_loop(lo, lo + 8, step, 0, unroll=True)
     out_ref[...] = a_ref[...]
+
 
 def factor_block(g):
     n = g.shape[0]

time: 158 us -> 154 us (0.975)
  Pallas kernels: 36.2 us -> 32.9 us
    pallas_call x2, Pallas kernels: 34.7 us -> 31.3 us  [factor_block(): pl.pallas_call(chol_kernel, out_shape=jax.ShapeDtypeStruct((n, 2 * n), jn...]
where the time goes in v7:
time: 154 us; the launch traced here: 153 us
  blocking collectives  72.3 us (47%)
  Pallas kernels  32.9 us (21%)
  waiting for transfers between devices  18.9 us (12%)
  starting transfers between devices  9.63 us (6%)
  matrix products  7.69 us (5%)
  other arithmetic  5.32 us (3%)
  local copies, waits for them, and re-layouts  5.11 us (3%)
    all_to_all x2, blocking collectives, scatter_sum(): got = lax.all_to_all(flat.reshape(count, -1), axis, 0, 0, tiled=True)  42.2 us
    pallas_call x2, Pallas kernels, factor_block(): pl.pallas_call(chol_kernel, out_shape=jax.ShapeDtypeStruct((n, 2 * n), jn...  31.3 us
    all_to_all x2, blocking collectives, gather_back(): return lax.all_to_all(spread, axis, 0, 0, tiled=True).reshape(-1)  30.1 us
    ppermute x6, waiting for transfers between devices, shifted(): return lax.ppermute(x, axis, pairs)  18.9 us
    ppermute x6, starting transfers between devices, shifted(): return lax.ppermute(x, axis, pairs)  9.63 us
  transfers between devices with their start and end apart: 6, of which 6 were waited for; matrix products, arithmetic and copies ran while one was open for 1% of the time, Pallas kernels for 1%

profile of v7, /device:TPU:24, one launch (start us, length us, event | category | flops | bytes accessed | tf_op | source)
XLA Modules:
  0.0 152.7 jit_solution(5097761325979779057)
XLA Ops:
  1.6 1.9 %collective-permute-start = (bf16[256,128]{1,0:T(8,128)(2,1)S(1)}, bf16[256,128]{1,0:T(8,128)(2,1)S(1)}, u32[]{:S(2)}, u32[]{:S(2)}) collective-permute-start(bf16[256,128]{1,0:T(8,128)(2,1)S(1)} %slice.31), channel_id=1, source_target_pairs={{0,1},{1,2},{2,3},{3,4},{4,5},{5,6},{6,7},{8,9},{9,10},{10,11},{11... | collective-permute-start | bytes 196616 | tf_op jit(solution)/shard_map/ppermute | solution.py:20
  3.5 1.2 convert_convert_fusion.coefs_ref
  4.7 1.6 %shard_map.67 = (bf16[128,128]{1,0:T(8,128)(2,1)}, bf16[128,128]{1,0:T(8,128)(2,1)}) custom-call(f32[63]{0:T(128)} %convert_convert_fusion.coefs_ref), custom_call_target="tpu_custom_call" | custom-call | tf_op jit(solution)/shard_map/pallas_call | solution.py:40
  7.1 1.0 convolution_bitcast_fusion.1
  9.5 1.9 %collective-permute-start.1 = (f32[256,256]{0,1:T(8,128)S(1)}, f32[256,256]{0,1:T(8,128)S(1)}, u32[]{:S(2)}, u32[]{:S(2)}) collective-permute-start(f32[256,256]{0,1:T(8,128)S(1)} %fusion.47), channel_id=1, source_target_pairs={{0,1},{1,2},{2,3},{3,4},{4,5},{5,6},{6,7},{8,9},{9,10},{10,11},{11... | collective-permute-start | bytes 786440 | tf_op jit(solution)/shard_map/ppermute | solution.py:20
  11.4 5.8 %collective-permute-done.1 = f32[256,256]{0,1:T(8,128)S(1)} collective-permute-done((f32[256,256]{0,1:T(8,128)S(1)}, f32[256,256]{0,1:T(8,128)S(1)}, u32[]{:S(2)}, u32[]{:S(2)}) %collective-permute-start.1) | collective-permute-done | bytes 262176 | tf_op jit(solution)/shard_map/ppermute | solution.py:20
  17.3 1.3 collective-permute-start.3
  18.6 1.9 %collective-permute-start.2 = (f32[256]{0:T(256)S(1)}, f32[256]{0:T(256)S(1)}, u32[]{:S(2)}, u32[]{:S(2)}) collective-permute-start(f32[256]{0:T(256)S(1)} %bitcast.32), channel_id=1, source_target_pairs={{0,1},{1,2},{2,3},{3,4},{4,5},{5,6},{6,7},{8,9},{9,10},{10,11},{11... | collective-permute-start | bytes 3080 | tf_op jit(solution)/shard_map/ppermute | solution.py:20
  20.5 3.0 %collective-permute-done.2 = f32[256]{0:T(256)S(1)} collective-permute-done((f32[256]{0:T(256)S(1)}, f32[256]{0:T(256)S(1)}, u32[]{:S(2)}, u32[]{:S(2)}) %collective-permute-start.2) | collective-permute-done | bytes 1056 | tf_op jit(solution)/shard_map/ppermute | solution.py:20
  23.5 2.1 %collective-permute-done.3 = f32[256,256]{0,1:T(8,128)S(1)} collective-permute-done((f32[256,256]{0,1:T(8,128)S(1)}, f32[256,256]{0,1:T(8,128)S(1)}, u32[]{:S(2)}, u32[]{:S(2)}) %collective-permute-start.3) | collective-permute-done | bytes 262176 | tf_op jit(solution)/shard_map/ppermute | solution.py:20
  25.7 1.3 collective-permute-start.5
  27.0 1.3 collective-permute-start.4
  28.3 4.2 %collective-permute-done.4 = f32[256]{0:T(256)S(1)} collective-permute-done((f32[256]{0:T(256)S(1)}, f32[256]{0:T(256)S(1)}, u32[]{:S(2)}, u32[]{:S(2)}) %collective-permute-start.4) | collective-permute-done | bytes 1056 | tf_op jit(solution)/shard_map/ppermute | solution.py:20
  32.5 3.0 %collective-permute-done.5 = f32[256,256]{0,1:T(8,128)S(1)} collective-permute-done((f32[256,256]{0,1:T(8,128)S(1)}, f32[256,256]{0,1:T(8,128)S(1)}, u32[]{:S(2)}, u32[]{:S(2)}) %collective-permute-start.5) | collective-permute-done | bytes 262176 | tf_op jit(solution)/shard_map/ppermute | solution.py:20
  37.2 13.6 %all_to_all.31 = f32[4,1,49152]{2,1,0:T(1,128)S(1)} all-to-all(f32[4,1,49152]{2,1,0:T(1,128)S(1)} %all_to_all.26), channel_id=1, replica_groups=mesh['x'=4,'z'=16,'y'=4,'core'=2] {'x'}, dimensions={0} | all-to-all | bytes 1572864 | tf_op jit(solution)/shard_map/all_to_all | solution.py:50
  51.5 28.7 %all_to_all.32 = f32[16,1,3072]{2,1,0:T(1,128)S(1)} all-to-all(f32[16,1,3072]{2,1,0:T(1,128)S(1)} %bitcast.29), channel_id=1, replica_groups=mesh['x'=4,'z'=16,'y'=4,'core'=2] {'z'}, dimensions={0} | all-to-all | bytes 393216 | tf_op jit(solution)/shard_map/all_to_all | solution.py:50
  80.4 18.2 %all_to_all.33 = f32[16,1,3072]{2,1,0:T(1,128)S(1)} all-to-all(f32[16,1,3072]{2,1,0:T(1,128)S(1)} %broadcast_in_dim.29), channel_id=1, replica_groups=mesh['x'=4,'z'=16,'y'=4,'core'=2] {'z'}, dimensions={0} | all-to-all | bytes 393216 | tf_op jit(solution)/shard_map/all_to_all | solution.py:57
  99.0 11.9 %all_to_all.34 = f32[4,1,49152]{2,1,0:T(1,128)S(1)} all-to-all(f32[4,1,49152]{2,1,0:T(1,128)S(1)} %broadcast_in_dim.31), channel_id=1, replica_groups=mesh['x'=4,'z'=16,'y'=4,'core'=2] {'x'}, dimensions={0} | all-to-all | bytes 1572864 | tf_op jit(solution)/shard_map/all_to_all | solution.py:57
  110.9 2.3 %reduce.2 = f32[4,49152]{1,0:T(4,128)S(1)} reduce(f32[4,1,49152]{2,1,0:T(1,128)S(1)} %all_to_all.34, f32[]{:T(128)} %constant.23), dimensions={1}, to_apply=%all_to_all.25.reduce_sub_computation | reduce | bytes 1572868 | tf_op jit(solution)/shard_map/all_to_all | solution.py:57
  114.4 15.7 %shard_map.68 = f32[128,256]{1,0:T(8,128)} custom-call(f32[128,128]{1,0:T(8,128)} %slice.40.g_ref), custom_call_target="tpu_custom_call" | custom-call | tf_op jit(solution)/shard_map/pallas_call | solution.py:98
  130.0 1.2 fusion.44
  132.4 15.7 %shard_map.69 = f32[128,256]{1,0:T(8,128)} custom-call(f32[128,128]{1,0:T(8,128)} %convolution_subtract_fusion.g_ref), custom_call_target="tpu_custom_call" | custom-call | tf_op jit(solution)/shard_map/pallas_call | solution.py:98
  149.3 1.4 fusion
  150.7 1.3 fusion.1
  (37 shorter events, 10.7 us)
Async XLA Ops:
  0.6 8.6 %copy-start = (bf16[512,256]{1,0:T(8,128)(2,1)S(1)}, bf16[512,256]{1,0:T(8,128)(2,1)}, u32[]{:S(2)}) copy-start(bf16[512,256]{1,0:T(8,128)(2,1)} %param.6) | copy-start | bytes 786436
  0.6 7.5 %copy-start.4 = (bf16[256,512]{1,0:T(8,128)(2,1)S(1)}, bf16[256,512]{1,0:T(8,128)(2,1)}, u32[]{:S(2)}) copy-start(bf16[256,512]{1,0:T(8,128)(2,1)} %param.4) | copy-start | bytes 786436
  1.6 5.6 %collective-permute-start = (bf16[256,128]{1,0:T(8,128)(2,1)S(1)}, bf16[256,128]{1,0:T(8,128)(2,1)S(1)}, u32[]{:S(2)}, u32[]{:S(2)}) collective-permute-start(bf16[256,128]{1,0:T(8,128)(2,1)S(1)} %slice.31), channel_id=1, source_target_pairs={{0,1},{1,2},{2,3},{3,4},{4,5},{5,6},{6,7},{8,9},{9,10},{10,11},{11... | collective-permute-start | bytes 196616 | tf_op jit(solution)/shard_map/ppermute | solution.py:20
  7.1 1.0 copy-start.6
  8.1 0.8 copy-start.3
  9.5 7.7 %copy-start.5 = (f32[1,256]{1,0:T(1,128)S(1)}, f32[1,256]{1,0:T(1,128)}, u32[]{:S(2)}) copy-start(f32[1,256]{1,0:T(1,128)} %param.7) | copy-start | bytes 3076
  9.5 7.7 %collective-permute-start.1 = (f32[256,256]{0,1:T(8,128)S(1)}, f32[256,256]{0,1:T(8,128)S(1)}, u32[]{:S(2)}, u32[]{:S(2)}) collective-permute-start(f32[256,256]{0,1:T(8,128)S(1)} %fusion.47), channel_id=1, source_target_pairs={{0,1},{1,2},{2,3},{3,4},{4,5},{5,6},{6,7},{8,9},{9,10},{10,11},{11... | collective-permute-start | bytes 786440 | tf_op jit(solution)/shard_map/ppermute | solution.py:20
  17.3 8.3 %collective-permute-start.3 = (f32[256,256]{0,1:T(8,128)S(1)}, f32[256,256]{0,1:T(8,128)S(1)}, u32[]{:S(2)}, u32[]{:S(2)}) collective-permute-start(f32[256,256]{0,1:T(8,128)S(1)} %multiply_add_fusion.2), channel_id=1, source_target_pairs={{0,2},{1,3},{2,4},{3,5},{4,6},{5,7},{8,10},{9,11},{10,12},{11,13},... | collective-permute-start | bytes 786440 | tf_op jit(solution)/shard_map/ppermute | solution.py:20
  18.6 4.9 %collective-permute-start.2 = (f32[256]{0:T(256)S(1)}, f32[256]{0:T(256)S(1)}, u32[]{:S(2)}, u32[]{:S(2)}) collective-permute-start(f32[256]{0:T(256)S(1)} %bitcast.32), channel_id=1, source_target_pairs={{0,1},{1,2},{2,3},{3,4},{4,5},{5,6},{6,7},{8,9},{9,10},{10,11},{11... | collective-permute-start | bytes 3080 | tf_op jit(solution)/shard_map/ppermute | solution.py:20
  25.7 9.8 %collective-permute-start.5 = (f32[256,256]{0,1:T(8,128)S(1)}, f32[256,256]{0,1:T(8,128)S(1)}, u32[]{:S(2)}, u32[]{:S(2)}) collective-permute-start(f32[256,256]{0,1:T(8,128)S(1)} %multiply_add_fusion.1), channel_id=1, source_target_pairs={{0,4},{1,5},{2,6},{3,7},{8,12},{9,13},{10,14},{11,15},{16,20},{17,... | collective-permute-start | bytes 786440 | tf_op jit(solution)/shard_map/ppermute | solution.py:20
  27.0 5.5 %collective-permute-start.4 = (f32[256]{0:T(256)S(1)}, f32[256]{0:T(256)S(1)}, u32[]{:S(2)}, u32[]{:S(2)}) collective-permute-start(f32[256]{0:T(256)S(1)} %mul.44), channel_id=1, source_target_pairs={{0,2},{1,3},{2,4},{3,5},{4,6},{5,7},{8,10},{9,11},{10,12},{11,13},... | collective-permute-start | bytes 3080 | tf_op jit(solution)/shard_map/ppermute | solution.py:20
  130.0 1.2 copy-start.1
  148.1 1.0 copy-start.2

commit v8 on v4

--- a/solution.py
+++ b/solution.py
@@ -66,14 +66,40 @@
     return flat.reshape(x.shape)
 
 
+def chol_kernel(g_ref, out_ref):
+    n = g_ref.shape[0]
+    rows = lax.broadcasted_iota(jnp.int32, (n, n), 0)
+    cols = lax.broadcasted_iota(jnp.int32, (n, n), 1)
+    whole = jnp.concatenate([g_ref[...], jnp.where(rows == cols, 1.0, 0.0).astype(jnp.float32)], axis=1)
+    lane_row = lax.broadcasted_iota(jnp.int32, (1, 2 * n), 1)
+    for j in range(n):
+        lo = j - j % 8
+        if j % 8 == 0 and j > 0:
+            out_ref[lo - 8 : lo, :] = whole[:8]
+            whole = whole[8:]
+        r = j - lo
+        row = whole[r : r + 1]
+        scale = 1.0 / jnp.sqrt(row[:, j : j + 1])
+        top = jnp.where(lane_row >= j, row * scale, 0.0)
+        column = whole[:, j : j + 1] * scale
+        sub = lax.broadcasted_iota(jnp.int32, whole.shape, 0)
+        whole = jnp.where(sub > r, whole - column * top, jnp.where(sub == r, top, whole))
+    out_ref[n - 8 :, :] = whole
+
+
+def factor_block(g):
+    n = g.shape[0]
+    vmem = pl.BlockSpec(memory_space=pltpu.VMEM)
+    out = pl.pallas_call(chol_kernel, out_shape=jax.ShapeDtypeStruct((n, 2 * n), jnp.float32),
+        in_specs=[vmem], out_specs=vmem)(g)
+    return out[:, :n].T, out[:, n:]
+
+
 def factor_and_invert(gram):
     h = gram.shape[0] // 2
-    eye = jnp.eye(h, dtype=jnp.float32)
-    l11 = lax.linalg.cholesky(gram[:h, :h])
-    i11 = lax.linalg.triangular_solve(l11, eye, left_side=True, lower=True)
+    l11, i11 = factor_block(gram[:h, :h])
     l21 = jnp.dot(gram[h:, :h], i11.T, precision=HIGH)
-    l22 = lax.linalg.cholesky(gram[h:, h:] - jnp.dot(l21, l21.T, precision=HIGH))
-    i22 = lax.linalg.triangular_solve(l22, eye, left_side=True, lower=True)
+    l22, i22 = factor_block(gram[h:, h:] - jnp.dot(l21, l21.T, precision=HIGH))
     x21 = -jnp.dot(i22, jnp.dot(l21, i11, precision=HIGH), precision=HIGH)
     zero = jnp.zeros((h, h), jnp.float32)
     return jnp.block([[l11, zero], [l21, l22]]), jnp.block([[i11, zero], [x21, i22]])

time: 167 us -> 151 us (0.904)
  other arithmetic: 50.6 us -> 5.32 us
  Pallas kernels: 1.58 us -> 29.8 us
    another operation x10 -> x0, other arithmetic: 45.9 us -> none  [the longest x3 12.6 us: factor_and_invert(): lax.linalg.cholesky(gram[h:, h:] - jnp.dot(l21, l21.T, precision=HIGH))]
    pallas_call x0 -> x2, Pallas kernels: none -> 28.2 us  [factor_block(): pl.pallas_call(chol_kernel, out_shape=jax.ShapeDtypeStruct((n, 2 * n), jn...]
where the time goes in v8:
time: 151 us; the launch traced here: 150 us
  blocking collectives  72.3 us (48%)
  Pallas kernels  29.8 us (20%)
  waiting for transfers between devices  18.9 us (13%)
  starting transfers between devices  9.63 us (6%)
  matrix products  7.69 us (5%)
  other arithmetic  5.32 us (4%)
  local copies, waits for them, and re-layouts  5.11 us (3%)
    all_to_all x2, blocking collectives, scatter_sum(): got = lax.all_to_all(flat.reshape(count, -1), axis, 0, 0, tiled=True)  42.2 us
    all_to_all x2, blocking collectives, gather_back(): return lax.all_to_all(spread, axis, 0, 0, tiled=True).reshape(-1)  30.1 us
    pallas_call x2, Pallas kernels, factor_block(): pl.pallas_call(chol_kernel, out_shape=jax.ShapeDtypeStruct((n, 2 * n), jn...  28.2 us
    ppermute x6, waiting for transfers between devices, shifted(): return lax.ppermute(x, axis, pairs)  18.9 us
    ppermute x6, starting transfers between devices, shifted(): return lax.ppermute(x, axis, pairs)  9.63 us
  transfers between devices with their start and end apart: 6, of which 6 were waited for; matrix products, arithmetic and copies ran while one was open for 1% of the time, Pallas kernels for 1%

profile of v8, /device:TPU:24, one launch (start us, length us, event | category | flops | bytes accessed | tf_op | source)
XLA Modules:
  0.0 149.6 jit_solution(10960375622201832257)
XLA Ops:
  1.6 1.9 %collective-permute-start = (bf16[256,128]{1,0:T(8,128)(2,1)S(1)}, bf16[256,128]{1,0:T(8,128)(2,1)S(1)}, u32[]{:S(2)}, u32[]{:S(2)}) collective-permute-start(bf16[256,128]{1,0:T(8,128)(2,1)S(1)} %slice.31), channel_id=1, source_target_pairs={{0,1},{1,2},{2,3},{3,4},{4,5},{5,6},{6,7},{8,9},{9,10},{10,11},{11... | collective-permute-start | bytes 196616 | tf_op jit(solution)/shard_map/ppermute | solution.py:20
  3.5 1.2 convert_convert_fusion.coefs_ref
  4.7 1.6 %shard_map.67 = (bf16[128,128]{1,0:T(8,128)(2,1)}, bf16[128,128]{1,0:T(8,128)(2,1)}) custom-call(f32[63]{0:T(128)} %convert_convert_fusion.coefs_ref), custom_call_target="tpu_custom_call" | custom-call | tf_op jit(solution)/shard_map/pallas_call | solution.py:40
  7.1 1.0 convolution_bitcast_fusion.1
  9.5 1.9 %collective-permute-start.1 = (f32[256,256]{0,1:T(8,128)S(1)}, f32[256,256]{0,1:T(8,128)S(1)}, u32[]{:S(2)}, u32[]{:S(2)}) collective-permute-start(f32[256,256]{0,1:T(8,128)S(1)} %fusion.47), channel_id=1, source_target_pairs={{0,1},{1,2},{2,3},{3,4},{4,5},{5,6},{6,7},{8,9},{9,10},{10,11},{11... | collective-permute-start | bytes 786440 | tf_op jit(solution)/shard_map/ppermute | solution.py:20
  11.4 5.8 %collective-permute-done.1 = f32[256,256]{0,1:T(8,128)S(1)} collective-permute-done((f32[256,256]{0,1:T(8,128)S(1)}, f32[256,256]{0,1:T(8,128)S(1)}, u32[]{:S(2)}, u32[]{:S(2)}) %collective-permute-start.1) | collective-permute-done | bytes 262176 | tf_op jit(solution)/shard_map/ppermute | solution.py:20
  17.3 1.3 collective-permute-start.3
  18.6 1.9 %collective-permute-start.2 = (f32[256]{0:T(256)S(1)}, f32[256]{0:T(256)S(1)}, u32[]{:S(2)}, u32[]{:S(2)}) collective-permute-start(f32[256]{0:T(256)S(1)} %bitcast.32), channel_id=1, source_target_pairs={{0,1},{1,2},{2,3},{3,4},{4,5},{5,6},{6,7},{8,9},{9,10},{10,11},{11... | collective-permute-start | bytes 3080 | tf_op jit(solution)/shard_map/ppermute | solution.py:20
  20.5 3.0 %collective-permute-done.2 = f32[256]{0:T(256)S(1)} collective-permute-done((f32[256]{0:T(256)S(1)}, f32[256]{0:T(256)S(1)}, u32[]{:S(2)}, u32[]{:S(2)}) %collective-permute-start.2) | collective-permute-done | bytes 1056 | tf_op jit(solution)/shard_map/ppermute | solution.py:20
  23.5 2.1 %collective-permute-done.3 = f32[256,256]{0,1:T(8,128)S(1)} collective-permute-done((f32[256,256]{0,1:T(8,128)S(1)}, f32[256,256]{0,1:T(8,128)S(1)}, u32[]{:S(2)}, u32[]{:S(2)}) %collective-permute-start.3) | collective-permute-done | bytes 262176 | tf_op jit(solution)/shard_map/ppermute | solution.py:20
  25.7 1.3 collective-permute-start.5
  27.0 1.3 collective-permute-start.4
  28.3 4.2 %collective-permute-done.4 = f32[256]{0:T(256)S(1)} collective-permute-done((f32[256]{0:T(256)S(1)}, f32[256]{0:T(256)S(1)}, u32[]{:S(2)}, u32[]{:S(2)}) %collective-permute-start.4) | collective-permute-done | bytes 1056 | tf_op jit(solution)/shard_map/ppermute | solution.py:20
  32.5 3.0 %collective-permute-done.5 = f32[256,256]{0,1:T(8,128)S(1)} collective-permute-done((f32[256,256]{0,1:T(8,128)S(1)}, f32[256,256]{0,1:T(8,128)S(1)}, u32[]{:S(2)}, u32[]{:S(2)}) %collective-permute-start.5) | collective-permute-done | bytes 262176 | tf_op jit(solution)/shard_map/ppermute | solution.py:20
  37.2 13.6 %all_to_all.31 = f32[4,1,49152]{2,1,0:T(1,128)S(1)} all-to-all(f32[4,1,49152]{2,1,0:T(1,128)S(1)} %all_to_all.26), channel_id=1, replica_groups=mesh['x'=4,'z'=16,'y'=4,'core'=2] {'x'}, dimensions={0} | all-to-all | bytes 1572864 | tf_op jit(solution)/shard_map/all_to_all | solution.py:50
  51.5 28.7 %all_to_all.32 = f32[16,1,3072]{2,1,0:T(1,128)S(1)} all-to-all(f32[16,1,3072]{2,1,0:T(1,128)S(1)} %bitcast.29), channel_id=1, replica_groups=mesh['x'=4,'z'=16,'y'=4,'core'=2] {'z'}, dimensions={0} | all-to-all | bytes 393216 | tf_op jit(solution)/shard_map/all_to_all | solution.py:50
  80.4 18.2 %all_to_all.33 = f32[16,1,3072]{2,1,0:T(1,128)S(1)} all-to-all(f32[16,1,3072]{2,1,0:T(1,128)S(1)} %broadcast_in_dim.29), channel_id=1, replica_groups=mesh['x'=4,'z'=16,'y'=4,'core'=2] {'z'}, dimensions={0} | all-to-all | bytes 393216 | tf_op jit(solution)/shard_map/all_to_all | solution.py:57
  99.0 11.9 %all_to_all.34 = f32[4,1,49152]{2,1,0:T(1,128)S(1)} all-to-all(f32[4,1,49152]{2,1,0:T(1,128)S(1)} %broadcast_in_dim.31), channel_id=1, replica_groups=mesh['x'=4,'z'=16,'y'=4,'core'=2] {'x'}, dimensions={0} | all-to-all | bytes 1572864 | tf_op jit(solution)/shard_map/all_to_all | solution.py:57
  110.9 2.3 %reduce.2 = f32[4,49152]{1,0:T(4,128)S(1)} reduce(f32[4,1,49152]{2,1,0:T(1,128)S(1)} %all_to_all.34, f32[]{:T(128)} %constant.23), dimensions={1}, to_apply=%all_to_all.25.reduce_sub_computation | reduce | bytes 1572868 | tf_op jit(solution)/shard_map/all_to_all | solution.py:57
  114.4 14.1 %shard_map.68 = f32[128,256]{1,0:T(8,128)} custom-call(f32[128,128]{1,0:T(8,128)} %slice.40.g_ref), custom_call_target="tpu_custom_call" | custom-call | tf_op jit(solution)/shard_map/pallas_call | solution.py:93
  128.5 1.2 fusion.44
  130.9 14.1 %shard_map.69 = f32[128,256]{1,0:T(8,128)} custom-call(f32[128,128]{1,0:T(8,128)} %convolution_subtract_fusion.g_ref), custom_call_target="tpu_custom_call" | custom-call | tf_op jit(solution)/shard_map/pallas_call | solution.py:93
  146.2 1.4 fusion
  147.6 1.3 fusion.1
  (37 shorter events, 10.7 us)
Async XLA Ops:
  0.6 8.6 %copy-start = (bf16[512,256]{1,0:T(8,128)(2,1)S(1)}, bf16[512,256]{1,0:T(8,128)(2,1)}, u32[]{:S(2)}) copy-start(bf16[512,256]{1,0:T(8,128)(2,1)} %param.6) | copy-start | bytes 786436
  0.6 7.5 %copy-start.4 = (bf16[256,512]{1,0:T(8,128)(2,1)S(1)}, bf16[256,512]{1,0:T(8,128)(2,1)}, u32[]{:S(2)}) copy-start(bf16[256,512]{1,0:T(8,128)(2,1)} %param.4) | copy-start | bytes 786436
  1.6 5.6 %collective-permute-start = (bf16[256,128]{1,0:T(8,128)(2,1)S(1)}, bf16[256,128]{1,0:T(8,128)(2,1)S(1)}, u32[]{:S(2)}, u32[]{:S(2)}) collective-permute-start(bf16[256,128]{1,0:T(8,128)(2,1)S(1)} %slice.31), channel_id=1, source_target_pairs={{0,1},{1,2},{2,3},{3,4},{4,5},{5,6},{6,7},{8,9},{9,10},{10,11},{11... | collective-permute-start | bytes 196616 | tf_op jit(solution)/shard_map/ppermute | solution.py:20
  7.1 1.0 copy-start.6
  8.1 0.8 copy-start.3
  9.5 7.7 %copy-start.5 = (f32[1,256]{1,0:T(1,128)S(1)}, f32[1,256]{1,0:T(1,128)}, u32[]{:S(2)}) copy-start(f32[1,256]{1,0:T(1,128)} %param.7) | copy-start | bytes 3076
  9.5 7.7 %collective-permute-start.1 = (f32[256,256]{0,1:T(8,128)S(1)}, f32[256,256]{0,1:T(8,128)S(1)}, u32[]{:S(2)}, u32[]{:S(2)}) collective-permute-start(f32[256,256]{0,1:T(8,128)S(1)} %fusion.47), channel_id=1, source_target_pairs={{0,1},{1,2},{2,3},{3,4},{4,5},{5,6},{6,7},{8,9},{9,10},{10,11},{11... | collective-permute-start | bytes 786440 | tf_op jit(solution)/shard_map/ppermute | solution.py:20
  17.3 8.3 %collective-permute-start.3 = (f32[256,256]{0,1:T(8,128)S(1)}, f32[256,256]{0,1:T(8,128)S(1)}, u32[]{:S(2)}, u32[]{:S(2)}) collective-permute-start(f32[256,256]{0,1:T(8,128)S(1)} %multiply_add_fusion.2), channel_id=1, source_target_pairs={{0,2},{1,3},{2,4},{3,5},{4,6},{5,7},{8,10},{9,11},{10,12},{11,13},... | collective-permute-start | bytes 786440 | tf_op jit(solution)/shard_map/ppermute | solution.py:20
  18.6 4.9 %collective-permute-start.2 = (f32[256]{0:T(256)S(1)}, f32[256]{0:T(256)S(1)}, u32[]{:S(2)}, u32[]{:S(2)}) collective-permute-start(f32[256]{0:T(256)S(1)} %bitcast.32), channel_id=1, source_target_pairs={{0,1},{1,2},{2,3},{3,4},{4,5},{5,6},{6,7},{8,9},{9,10},{10,11},{11... | collective-permute-start | bytes 3080 | tf_op jit(solution)/shard_map/ppermute | solution.py:20
  25.7 9.8 %collective-permute-start.5 = (f32[256,256]{0,1:T(8,128)S(1)}, f32[256,256]{0,1:T(8,128)S(1)}, u32[]{:S(2)}, u32[]{:S(2)}) collective-permute-start(f32[256,256]{0,1:T(8,128)S(1)} %multiply_add_fusion.1), channel_id=1, source_target_pairs={{0,4},{1,5},{2,6},{3,7},{8,12},{9,13},{10,14},{11,15},{16,20},{17,... | collective-permute-start | bytes 786440 | tf_op jit(solution)/shard_map/ppermute | solution.py:20
  27.0 5.5 %collective-permute-start.4 = (f32[256]{0:T(256)S(1)}, f32[256]{0:T(256)S(1)}, u32[]{:S(2)}, u32[]{:S(2)}) collective-permute-start(f32[256]{0:T(256)S(1)} %mul.44), channel_id=1, source_target_pairs={{0,2},{1,3},{2,4},{3,5},{4,6},{5,7},{8,10},{9,11},{10,12},{11,13},... | collective-permute-start | bytes 3080 | tf_op jit(solution)/shard_map/ppermute | solution.py:20
  128.5 1.2 copy-start.1
  145.0 1.0 copy-start.2

commit v9 on v8

--- a/solution.py
+++ b/solution.py
@@ -79,11 +79,13 @@
             whole = whole[8:]
         r = j - lo
         row = whole[r : r + 1]
-        scale = 1.0 / jnp.sqrt(row[:, j : j + 1])
-        top = jnp.where(lane_row >= j, row * scale, 0.0)
-        column = whole[:, j : j + 1] * scale
+        inverse = 1.0 / row[:, j : j + 1]
+        kept = jnp.where(lane_row >= j, row, 0.0)
+        top = kept * jnp.sqrt(inverse)
         sub = lax.broadcasted_iota(jnp.int32, whole.shape, 0)
-        whole = jnp.where(sub > r, whole - column * top, jnp.where(sub == r, top, whole))
+        whole = jnp.where(
+            sub > r, whole - whole[:, j : j + 1] * (kept * inverse), jnp.where(sub == r, top, whole)
+        )
     out_ref[n - 8 :, :] = whole
 
 

time: 151 us -> 150 us (level)
  no operation moved by 1% of the time
where the time goes in v9:
time: 150 us; the launch traced here: 149 us
  blocking collectives  72.3 us (48%)
  Pallas kernels  28.8 us (19%)
  waiting for transfers between devices  18.9 us (13%)
  starting transfers between devices  9.63 us (6%)
  matrix products  7.69 us (5%)
  other arithmetic  5.32 us (4%)
  local copies, waits for them, and re-layouts  5.11 us (3%)
    all_to_all x2, blocking collectives, scatter_sum(): got = lax.all_to_all(flat.reshape(count, -1), axis, 0, 0, tiled=True)  42.2 us
    all_to_all x2, blocking collectives, gather_back(): return lax.all_to_all(spread, axis, 0, 0, tiled=True).reshape(-1)  30.1 us
    pallas_call x2, Pallas kernels, factor_block(): pl.pallas_call(chol_kernel, out_shape=jax.ShapeDtypeStruct((n, 2 * n), jn...  27.3 us
    ppermute x6, waiting for transfers between devices, shifted(): return lax.ppermute(x, axis, pairs)  18.9 us
    ppermute x6, starting transfers between devices, shifted(): return lax.ppermute(x, axis, pairs)  9.63 us
  transfers between devices with their start and end apart: 6, of which 6 were waited for; matrix products, arithmetic and copies ran while one was open for 1% of the time, Pallas kernels for 1%

profile of v9, /device:TPU:24, one launch (start us, length us, event | category | flops | bytes accessed | tf_op | source)
XLA Modules:
  0.0 148.6 jit_solution(14425498326951081180)
XLA Ops:
  1.6 1.9 %collective-permute-start = (bf16[256,128]{1,0:T(8,128)(2,1)S(1)}, bf16[256,128]{1,0:T(8,128)(2,1)S(1)}, u32[]{:S(2)}, u32[]{:S(2)}) collective-permute-start(bf16[256,128]{1,0:T(8,128)(2,1)S(1)} %slice.31), channel_id=1, source_target_pairs={{0,1},{1,2},{2,3},{3,4},{4,5},{5,6},{6,7},{8,9},{9,10},{10,11},{11... | collective-permute-start | bytes 196616 | tf_op jit(solution)/shard_map/ppermute | solution.py:20
  3.5 1.2 convert_convert_fusion.coefs_ref
  4.7 1.6 %shard_map.67 = (bf16[128,128]{1,0:T(8,128)(2,1)}, bf16[128,128]{1,0:T(8,128)(2,1)}) custom-call(f32[63]{0:T(128)} %convert_convert_fusion.coefs_ref), custom_call_target="tpu_custom_call" | custom-call | tf_op jit(solution)/shard_map/pallas_call | solution.py:40
  7.1 1.0 convolution_bitcast_fusion.1
  9.5 1.9 %collective-permute-start.1 = (f32[256,256]{0,1:T(8,128)S(1)}, f32[256,256]{0,1:T(8,128)S(1)}, u32[]{:S(2)}, u32[]{:S(2)}) collective-permute-start(f32[256,256]{0,1:T(8,128)S(1)} %fusion.47), channel_id=1, source_target_pairs={{0,1},{1,2},{2,3},{3,4},{4,5},{5,6},{6,7},{8,9},{9,10},{10,11},{11... | collective-permute-start | bytes 786440 | tf_op jit(solution)/shard_map/ppermute | solution.py:20
  11.4 5.8 %collective-permute-done.1 = f32[256,256]{0,1:T(8,128)S(1)} collective-permute-done((f32[256,256]{0,1:T(8,128)S(1)}, f32[256,256]{0,1:T(8,128)S(1)}, u32[]{:S(2)}, u32[]{:S(2)}) %collective-permute-start.1) | collective-permute-done | bytes 262176 | tf_op jit(solution)/shard_map/ppermute | solution.py:20
  17.3 1.3 collective-permute-start.3
  18.6 1.9 %collective-permute-start.2 = (f32[256]{0:T(256)S(1)}, f32[256]{0:T(256)S(1)}, u32[]{:S(2)}, u32[]{:S(2)}) collective-permute-start(f32[256]{0:T(256)S(1)} %bitcast.32), channel_id=1, source_target_pairs={{0,1},{1,2},{2,3},{3,4},{4,5},{5,6},{6,7},{8,9},{9,10},{10,11},{11... | collective-permute-start | bytes 3080 | tf_op jit(solution)/shard_map/ppermute | solution.py:20
  20.5 3.0 %collective-permute-done.2 = f32[256]{0:T(256)S(1)} collective-permute-done((f32[256]{0:T(256)S(1)}, f32[256]{0:T(256)S(1)}, u32[]{:S(2)}, u32[]{:S(2)}) %collective-permute-start.2) | collective-permute-done | bytes 1056 | tf_op jit(solution)/shard_map/ppermute | solution.py:20
  23.5 2.1 %collective-permute-done.3 = f32[256,256]{0,1:T(8,128)S(1)} collective-permute-done((f32[256,256]{0,1:T(8,128)S(1)}, f32[256,256]{0,1:T(8,128)S(1)}, u32[]{:S(2)}, u32[]{:S(2)}) %collective-permute-start.3) | collective-permute-done | bytes 262176 | tf_op jit(solution)/shard_map/ppermute | solution.py:20
  25.7 1.3 collective-permute-start.5
  27.0 1.3 collective-permute-start.4
  28.3 4.2 %collective-permute-done.4 = f32[256]{0:T(256)S(1)} collective-permute-done((f32[256]{0:T(256)S(1)}, f32[256]{0:T(256)S(1)}, u32[]{:S(2)}, u32[]{:S(2)}) %collective-permute-start.4) | collective-permute-done | bytes 1056 | tf_op jit(solution)/shard_map/ppermute | solution.py:20
  32.5 3.0 %collective-permute-done.5 = f32[256,256]{0,1:T(8,128)S(1)} collective-permute-done((f32[256,256]{0,1:T(8,128)S(1)}, f32[256,256]{0,1:T(8,128)S(1)}, u32[]{:S(2)}, u32[]{:S(2)}) %collective-permute-start.5) | collective-permute-done | bytes 262176 | tf_op jit(solution)/shard_map/ppermute | solution.py:20
  37.2 13.6 %all_to_all.31 = f32[4,1,49152]{2,1,0:T(1,128)S(1)} all-to-all(f32[4,1,49152]{2,1,0:T(1,128)S(1)} %all_to_all.26), channel_id=1, replica_groups=mesh['x'=4,'z'=16,'y'=4,'core'=2] {'x'}, dimensions={0} | all-to-all | bytes 1572864 | tf_op jit(solution)/shard_map/all_to_all | solution.py:50
  51.5 28.7 %all_to_all.32 = f32[16,1,3072]{2,1,0:T(1,128)S(1)} all-to-all(f32[16,1,3072]{2,1,0:T(1,128)S(1)} %bitcast.29), channel_id=1, replica_groups=mesh['x'=4,'z'=16,'y'=4,'core'=2] {'z'}, dimensions={0} | all-to-all | bytes 393216 | tf_op jit(solution)/shard_map/all_to_all | solution.py:50
  80.4 18.2 %all_to_all.33 = f32[16,1,3072]{2,1,0:T(1,128)S(1)} all-to-all(f32[16,1,3072]{2,1,0:T(1,128)S(1)} %broadcast_in_dim.29), channel_id=1, replica_groups=mesh['x'=4,'z'=16,'y'=4,'core'=2] {'z'}, dimensions={0} | all-to-all | bytes 393216 | tf_op jit(solution)/shard_map/all_to_all | solution.py:57
  99.0 11.9 %all_to_all.34 = f32[4,1,49152]{2,1,0:T(1,128)S(1)} all-to-all(f32[4,1,49152]{2,1,0:T(1,128)S(1)} %broadcast_in_dim.31), channel_id=1, replica_groups=mesh['x'=4,'z'=16,'y'=4,'core'=2] {'x'}, dimensions={0} | all-to-all | bytes 1572864 | tf_op jit(solution)/shard_map/all_to_all | solution.py:57
  110.9 2.3 %reduce.2 = f32[4,49152]{1,0:T(4,128)S(1)} reduce(f32[4,1,49152]{2,1,0:T(1,128)S(1)} %all_to_all.34, f32[]{:T(128)} %constant.23), dimensions={1}, to_apply=%all_to_all.25.reduce_sub_computation | reduce | bytes 1572868 | tf_op jit(solution)/shard_map/all_to_all | solution.py:57
  114.4 13.6 %shard_map.68 = f32[128,256]{1,0:T(8,128)} custom-call(f32[128,128]{1,0:T(8,128)} %slice.40.g_ref), custom_call_target="tpu_custom_call" | custom-call | tf_op jit(solution)/shard_map/pallas_call | solution.py:95
  128.0 1.2 fusion.44
  130.4 13.6 %shard_map.69 = f32[128,256]{1,0:T(8,128)} custom-call(f32[128,128]{1,0:T(8,128)} %convolution_subtract_fusion.g_ref), custom_call_target="tpu_custom_call" | custom-call | tf_op jit(solution)/shard_map/pallas_call | solution.py:95
  145.2 1.4 fusion
  146.6 1.3 fusion.1
  (37 shorter events, 10.7 us)
Async XLA Ops:
  0.6 8.6 %copy-start = (bf16[512,256]{1,0:T(8,128)(2,1)S(1)}, bf16[512,256]{1,0:T(8,128)(2,1)}, u32[]{:S(2)}) copy-start(bf16[512,256]{1,0:T(8,128)(2,1)} %param.6) | copy-start | bytes 786436
  0.6 7.5 %copy-start.4 = (bf16[256,512]{1,0:T(8,128)(2,1)S(1)}, bf16[256,512]{1,0:T(8,128)(2,1)}, u32[]{:S(2)}) copy-start(bf16[256,512]{1,0:T(8,128)(2,1)} %param.4) | copy-start | bytes 786436
  1.6 5.6 %collective-permute-start = (bf16[256,128]{1,0:T(8,128)(2,1)S(1)}, bf16[256,128]{1,0:T(8,128)(2,1)S(1)}, u32[]{:S(2)}, u32[]{:S(2)}) collective-permute-start(bf16[256,128]{1,0:T(8,128)(2,1)S(1)} %slice.31), channel_id=1, source_target_pairs={{0,1},{1,2},{2,3},{3,4},{4,5},{5,6},{6,7},{8,9},{9,10},{10,11},{11... | collective-permute-start | bytes 196616 | tf_op jit(solution)/shard_map/ppermute | solution.py:20
  7.1 1.0 copy-start.6
  8.1 0.8 copy-start.3
  9.5 7.7 %copy-start.5 = (f32[1,256]{1,0:T(1,128)S(1)}, f32[1,256]{1,0:T(1,128)}, u32[]{:S(2)}) copy-start(f32[1,256]{1,0:T(1,128)} %param.7) | copy-start | bytes 3076
  9.5 7.7 %collective-permute-start.1 = (f32[256,256]{0,1:T(8,128)S(1)}, f32[256,256]{0,1:T(8,128)S(1)}, u32[]{:S(2)}, u32[]{:S(2)}) collective-permute-start(f32[256,256]{0,1:T(8,128)S(1)} %fusion.47), channel_id=1, source_target_pairs={{0,1},{1,2},{2,3},{3,4},{4,5},{5,6},{6,7},{8,9},{9,10},{10,11},{11... | collective-permute-start | bytes 786440 | tf_op jit(solution)/shard_map/ppermute | solution.py:20
  17.3 8.3 %collective-permute-start.3 = (f32[256,256]{0,1:T(8,128)S(1)}, f32[256,256]{0,1:T(8,128)S(1)}, u32[]{:S(2)}, u32[]{:S(2)}) collective-permute-start(f32[256,256]{0,1:T(8,128)S(1)} %multiply_add_fusion.2), channel_id=1, source_target_pairs={{0,2},{1,3},{2,4},{3,5},{4,6},{5,7},{8,10},{9,11},{10,12},{11,13},... | collective-permute-start | bytes 786440 | tf_op jit(solution)/shard_map/ppermute | solution.py:20
  18.6 4.9 %collective-permute-start.2 = (f32[256]{0:T(256)S(1)}, f32[256]{0:T(256)S(1)}, u32[]{:S(2)}, u32[]{:S(2)}) collective-permute-start(f32[256]{0:T(256)S(1)} %bitcast.32), channel_id=1, source_target_pairs={{0,1},{1,2},{2,3},{3,4},{4,5},{5,6},{6,7},{8,9},{9,10},{10,11},{11... | collective-permute-start | bytes 3080 | tf_op jit(solution)/shard_map/ppermute | solution.py:20
  25.7 9.8 %collective-permute-start.5 = (f32[256,256]{0,1:T(8,128)S(1)}, f32[256,256]{0,1:T(8,128)S(1)}, u32[]{:S(2)}, u32[]{:S(2)}) collective-permute-start(f32[256,256]{0,1:T(8,128)S(1)} %multiply_add_fusion.1), channel_id=1, source_target_pairs={{0,4},{1,5},{2,6},{3,7},{8,12},{9,13},{10,14},{11,15},{16,20},{17,... | collective-permute-start | bytes 786440 | tf_op jit(solution)/shard_map/ppermute | solution.py:20
  27.0 5.5 %collective-permute-start.4 = (f32[256]{0:T(256)S(1)}, f32[256]{0:T(256)S(1)}, u32[]{:S(2)}, u32[]{:S(2)}) collective-permute-start(f32[256]{0:T(256)S(1)} %mul.44), channel_id=1, source_target_pairs={{0,2},{1,3},{2,4},{3,5},{4,6},{5,7},{8,10},{9,11},{10,12},{11,13},... | collective-permute-start | bytes 3080 | tf_op jit(solution)/shard_map/ppermute | solution.py:20
  128.0 1.2 copy-start.1
  144.0 1.0 copy-start.2

commit v10 on v9

--- a/solution.py
+++ b/solution.py
@@ -97,16 +97,6 @@
     return out[:, :n].T, out[:, n:]
 
 
-def factor_and_invert(gram):
-    h = gram.shape[0] // 2
-    l11, i11 = factor_block(gram[:h, :h])
-    l21 = jnp.dot(gram[h:, :h], i11.T, precision=HIGH)
-    l22, i22 = factor_block(gram[h:, h:] - jnp.dot(l21, l21.T, precision=HIGH))
-    x21 = -jnp.dot(i22, jnp.dot(l21, i11, precision=HIGH), precision=HIGH)
-    zero = jnp.zeros((h, h), jnp.float32)
-    return jnp.block([[l11, zero], [l21, l22]]), jnp.block([[i11, zero], [x21, i22]])
-
-
 def shards(frames, tap_table, sketch_matrix, decay_rates):
     rows_here, frame_count = frames.shape
     npoints = rows_here * math.prod(lax.axis_size(a) for a in ROWS)
@@ -146,7 +136,7 @@
     summed = reduce_rows(partial)
     gram = summed[:, :rank_count]
     cross = summed[:, rank_count:]
-    lower_one, inverse = factor_and_invert(gram)
+    lower_one, inverse = factor_block(gram)
     scaled = jnp.dot(weighted, inverse.T, precision=HIGH) * root_points
     projected = jnp.dot(inverse, cross, precision=HIGH) * (math.sqrt(rank_count) / root_points)
     upper = lower_one.T / root_points

time: 150 us -> 147 us (0.980)
  matrix products: 7.69 us -> 6.13 us
    dot_general x4 -> x0, matrix products: 2.58 us -> none  [the longest x1 1.17 us: factor_and_invert(): l21 = jnp.dot(gram[h:, :h], i11.T, precision=HIGH)]
    pallas_call x2 -> x1, Pallas kernels: 27.3 us -> 26.8 us  [factor_block(): pl.pallas_call(chol_kernel, out_shape=jax.ShapeDtypeStruct((n, 2 * n), jn...]
where the time goes in v10:
time: 147 us; the launch traced here: 146 us
  blocking collectives  72.3 us (49%)
  Pallas kernels  28.4 us (19%)
  waiting for transfers between devices  18.9 us (13%)
  starting transfers between devices  9.63 us (7%)
  matrix products  6.13 us (4%)
  other arithmetic  5.32 us (4%)
  local copies, waits for them, and re-layouts  4.24 us (3%)
    all_to_all x2, blocking collectives, scatter_sum(): got = lax.all_to_all(flat.reshape(count, -1), axis, 0, 0, tiled=True)  42.3 us
    all_to_all x2, blocking collectives, gather_back(): return lax.all_to_all(spread, axis, 0, 0, tiled=True).reshape(-1)  30.1 us
    pallas_call x1, Pallas kernels, factor_block(): pl.pallas_call(chol_kernel, out_shape=jax.ShapeDtypeStruct((n, 2 * n), jn...  26.8 us
    ppermute x6, waiting for transfers between devices, shifted(): return lax.ppermute(x, axis, pairs)  18.9 us
    ppermute x6, starting transfers between devices, shifted(): return lax.ppermute(x, axis, pairs)  9.63 us
  transfers between devices with their start and end apart: 6, of which 6 were waited for; matrix products, arithmetic and copies ran while one was open for 1% of the time, Pallas kernels for 1%

profile of v10, /device:TPU:24, one launch (start us, length us, event | category | flops | bytes accessed | tf_op | source)
XLA Modules:
  0.0 145.7 jit_solution(12682435960866869496)
XLA Ops:
  0.7 0.9 slice.15
  1.6 1.9 %collective-permute-start = (bf16[256,128]{1,0:T(8,128)(2,1)S(1)}, bf16[256,128]{1,0:T(8,128)(2,1)S(1)}, u32[]{:S(2)}, u32[]{:S(2)}) collective-permute-start(bf16[256,128]{1,0:T(8,128)(2,1)S(1)} %slice.15), channel_id=1, source_target_pairs={{0,1},{1,2},{2,3},{3,4},{4,5},{5,6},{6,7},{8,9},{9,10},{10,11},{11... | collective-permute-start | bytes 196616 | tf_op jit(solution)/shard_map/ppermute | solution.py:20
  3.5 1.2 convert_convert_fusion.coefs_ref
  4.7 1.6 %shard_map.67 = (bf16[128,128]{1,0:T(8,128)(2,1)}, bf16[128,128]{1,0:T(8,128)(2,1)}) custom-call(f32[63]{0:T(128)} %convert_convert_fusion.coefs_ref), custom_call_target="tpu_custom_call" | custom-call | tf_op jit(solution)/shard_map/pallas_call | solution.py:40
  6.2 0.9 collective-permute-done
  7.1 1.0 convolution_bitcast_fusion.1
  9.5 1.9 %collective-permute-start.1 = (f32[256,256]{0,1:T(8,128)S(1)}, f32[256,256]{0,1:T(8,128)S(1)}, u32[]{:S(2)}, u32[]{:S(2)}) collective-permute-start(f32[256,256]{0,1:T(8,128)S(1)} %fusion.42), channel_id=1, source_target_pairs={{0,1},{1,2},{2,3},{3,4},{4,5},{5,6},{6,7},{8,9},{9,10},{10,11},{11... | collective-permute-start | bytes 786440 | tf_op jit(solution)/shard_map/ppermute | solution.py:20
  11.4 5.8 %collective-permute-done.1 = f32[256,256]{0,1:T(8,128)S(1)} collective-permute-done((f32[256,256]{0,1:T(8,128)S(1)}, f32[256,256]{0,1:T(8,128)S(1)}, u32[]{:S(2)}, u32[]{:S(2)}) %collective-permute-start.1) | collective-permute-done | bytes 262176 | tf_op jit(solution)/shard_map/ppermute | solution.py:20
  17.3 1.3 collective-permute-start.3
  18.6 1.9 %collective-permute-start.2 = (f32[256]{0:T(256)S(1)}, f32[256]{0:T(256)S(1)}, u32[]{:S(2)}, u32[]{:S(2)}) collective-permute-start(f32[256]{0:T(256)S(1)} %bitcast.22), channel_id=1, source_target_pairs={{0,1},{1,2},{2,3},{3,4},{4,5},{5,6},{6,7},{8,9},{9,10},{10,11},{11... | collective-permute-start | bytes 3080 | tf_op jit(solution)/shard_map/ppermute | solution.py:20
  20.5 3.0 %collective-permute-done.2 = f32[256]{0:T(256)S(1)} collective-permute-done((f32[256]{0:T(256)S(1)}, f32[256]{0:T(256)S(1)}, u32[]{:S(2)}, u32[]{:S(2)}) %collective-permute-start.2) | collective-permute-done | bytes 1056 | tf_op jit(solution)/shard_map/ppermute | solution.py:20
  23.5 2.1 %collective-permute-done.3 = f32[256,256]{0,1:T(8,128)S(1)} collective-permute-done((f32[256,256]{0,1:T(8,128)S(1)}, f32[256,256]{0,1:T(8,128)S(1)}, u32[]{:S(2)}, u32[]{:S(2)}) %collective-permute-start.3) | collective-permute-done | bytes 262176 | tf_op jit(solution)/shard_map/ppermute | solution.py:20
  25.7 1.3 collective-permute-start.5
  27.0 1.3 collective-permute-start.4
  28.3 4.2 %collective-permute-done.4 = f32[256]{0:T(256)S(1)} collective-permute-done((f32[256]{0:T(256)S(1)}, f32[256]{0:T(256)S(1)}, u32[]{:S(2)}, u32[]{:S(2)}) %collective-permute-start.4) | collective-permute-done | bytes 1056 | tf_op jit(solution)/shard_map/ppermute | solution.py:20
  32.5 3.0 %collective-permute-done.5 = f32[256,256]{0,1:T(8,128)S(1)} collective-permute-done((f32[256,256]{0,1:T(8,128)S(1)}, f32[256,256]{0,1:T(8,128)S(1)}, u32[]{:S(2)}, u32[]{:S(2)}) %collective-permute-start.5) | collective-permute-done | bytes 262176 | tf_op jit(solution)/shard_map/ppermute | solution.py:20
  37.2 13.6 %all_to_all.31 = f32[4,1,49152]{2,1,0:T(1,128)S(1)} all-to-all(f32[4,1,49152]{2,1,0:T(1,128)S(1)} %all_to_all.26), channel_id=1, replica_groups=mesh['x'=4,'z'=16,'y'=4,'core'=2] {'x'}, dimensions={0} | all-to-all | bytes 1572864 | tf_op jit(solution)/shard_map/all_to_all | solution.py:50
  51.5 28.7 %all_to_all.32 = f32[16,1,3072]{2,1,0:T(1,128)S(1)} all-to-all(f32[16,1,3072]{2,1,0:T(1,128)S(1)} %bitcast.19), channel_id=1, replica_groups=mesh['x'=4,'z'=16,'y'=4,'core'=2] {'z'}, dimensions={0} | all-to-all | bytes 393216 | tf_op jit(solution)/shard_map/all_to_all | solution.py:50
  80.4 18.2 %all_to_all.33 = f32[16,1,3072]{2,1,0:T(1,128)S(1)} all-to-all(f32[16,1,3072]{2,1,0:T(1,128)S(1)} %broadcast_in_dim.28), channel_id=1, replica_groups=mesh['x'=4,'z'=16,'y'=4,'core'=2] {'z'}, dimensions={0} | all-to-all | bytes 393216 | tf_op jit(solution)/shard_map/all_to_all | solution.py:57
  99.0 11.9 %all_to_all.34 = f32[4,1,49152]{2,1,0:T(1,128)S(1)} all-to-all(f32[4,1,49152]{2,1,0:T(1,128)S(1)} %broadcast_in_dim.30), channel_id=1, replica_groups=mesh['x'=4,'z'=16,'y'=4,'core'=2] {'x'}, dimensions={0} | all-to-all | bytes 1572864 | tf_op jit(solution)/shard_map/all_to_all | solution.py:57
  110.9 2.3 %reduce.2 = f32[4,49152]{1,0:T(4,128)S(1)} reduce(f32[4,1,49152]{2,1,0:T(1,128)S(1)} %all_to_all.34, f32[]{:T(128)} %constant.18), dimensions={1}, to_apply=%all_to_all.25.reduce_sub_computation | reduce | bytes 1572868 | tf_op jit(solution)/shard_map/all_to_all | solution.py:57
  114.4 26.8 %shard_map.68 = f32[256,512]{1,0:T(8,128)} custom-call(f32[256,256]{1,0:T(8,128)} %slice.20.g_ref), custom_call_target="tpu_custom_call" | custom-call | tf_op jit(solution)/shard_map/pallas_call | solution.py:95
  141.3 2.4 %fusion = f32[1,256,512]{2,1,0:T(8,128)} fusion(f32[256,768]{1,0:T(8,128)S(1)} %reshape_reshape.4, f32[256,512]{1,0:T(8,128)} %shard_map.68), kind=kOutput, calls=%fused_computation.2 | convolution fusion | flops 402784256 | bytes 1310720 | tf_op jit(solution)/shard_map/dot_general | solution.py:141
  143.7 1.3 fusion.1
  (29 shorter events, 6.7 us)
Async XLA Ops:
  0.6 8.6 %copy-start = (bf16[512,256]{1,0:T(8,128)(2,1)S(1)}, bf16[512,256]{1,0:T(8,128)(2,1)}, u32[]{:S(2)}) copy-start(bf16[512,256]{1,0:T(8,128)(2,1)} %param.6) | copy-start | bytes 786436
  0.6 7.5 %copy-start.3 = (bf16[256,512]{1,0:T(8,128)(2,1)S(1)}, bf16[256,512]{1,0:T(8,128)(2,1)}, u32[]{:S(2)}) copy-start(bf16[256,512]{1,0:T(8,128)(2,1)} %param.4) | copy-start | bytes 786436
  1.6 5.6 %collective-permute-start = (bf16[256,128]{1,0:T(8,128)(2,1)S(1)}, bf16[256,128]{1,0:T(8,128)(2,1)S(1)}, u32[]{:S(2)}, u32[]{:S(2)}) collective-permute-start(bf16[256,128]{1,0:T(8,128)(2,1)S(1)} %slice.15), channel_id=1, source_target_pairs={{0,1},{1,2},{2,3},{3,4},{4,5},{5,6},{6,7},{8,9},{9,10},{10,11},{11... | collective-permute-start | bytes 196616 | tf_op jit(solution)/shard_map/ppermute | solution.py:20
  7.1 1.0 copy-start.5
  8.1 0.8 copy-start.2
  9.5 7.7 %copy-start.4 = (f32[1,256]{1,0:T(1,128)S(1)}, f32[1,256]{1,0:T(1,128)}, u32[]{:S(2)}) copy-start(f32[1,256]{1,0:T(1,128)} %param.7) | copy-start | bytes 3076
  9.5 7.7 %collective-permute-start.1 = (f32[256,256]{0,1:T(8,128)S(1)}, f32[256,256]{0,1:T(8,128)S(1)}, u32[]{:S(2)}, u32[]{:S(2)}) collective-permute-start(f32[256,256]{0,1:T(8,128)S(1)} %fusion.42), channel_id=1, source_target_pairs={{0,1},{1,2},{2,3},{3,4},{4,5},{5,6},{6,7},{8,9},{9,10},{10,11},{11... | collective-permute-start | bytes 786440 | tf_op jit(solution)/shard_map/ppermute | solution.py:20
  17.3 8.3 %collective-permute-start.3 = (f32[256,256]{0,1:T(8,128)S(1)}, f32[256,256]{0,1:T(8,128)S(1)}, u32[]{:S(2)}, u32[]{:S(2)}) collective-permute-start(f32[256,256]{0,1:T(8,128)S(1)} %multiply_add_fusion.2), channel_id=1, source_target_pairs={{0,2},{1,3},{2,4},{3,5},{4,6},{5,7},{8,10},{9,11},{10,12},{11,13},... | collective-permute-start | bytes 786440 | tf_op jit(solution)/shard_map/ppermute | solution.py:20
  18.6 4.9 %collective-permute-start.2 = (f32[256]{0:T(256)S(1)}, f32[256]{0:T(256)S(1)}, u32[]{:S(2)}, u32[]{:S(2)}) collective-permute-start(f32[256]{0:T(256)S(1)} %bitcast.22), channel_id=1, source_target_pairs={{0,1},{1,2},{2,3},{3,4},{4,5},{5,6},{6,7},{8,9},{9,10},{10,11},{11... | collective-permute-start | bytes 3080 | tf_op jit(solution)/shard_map/ppermute | solution.py:20
  25.7 9.8 %collective-permute-start.5 = (f32[256,256]{0,1:T(8,128)S(1)}, f32[256,256]{0,1:T(8,128)S(1)}, u32[]{:S(2)}, u32[]{:S(2)}) collective-permute-start(f32[256,256]{0,1:T(8,128)S(1)} %multiply_add_fusion.1), channel_id=1, source_target_pairs={{0,4},{1,5},{2,6},{3,7},{8,12},{9,13},{10,14},{11,15},{16,20},{17,... | collective-permute-start | bytes 786440 | tf_op jit(solution)/shard_map/ppermute | solution.py:20
  27.0 5.5 %collective-permute-start.4 = (f32[256]{0:T(256)S(1)}, f32[256]{0:T(256)S(1)}, u32[]{:S(2)}, u32[]{:S(2)}) collective-permute-start(f32[256]{0:T(256)S(1)} %mul.44), channel_id=1, source_target_pairs={{0,2},{1,3},{2,4},{3,5},{4,6},{5,7},{8,10},{9,11},{10,12},{11,13},... | collective-permute-start | bytes 3080 | tf_op jit(solution)/shard_map/ppermute | solution.py:20
  141.3 2.4 %copy-start.1 = (f32[256,512]{1,0:T(8,128)S(1)}, f32[256,512]{1,0:T(8,128)}, u32[]{:S(2)}) copy-start(f32[256,512]{1,0:T(8,128)} %shard_map.68) | copy-start | bytes 1572868

commit v11 on v10

--- a/solution.py
+++ b/solution.py
@@ -72,19 +72,30 @@
     cols = lax.broadcasted_iota(jnp.int32, (n, n), 1)
     whole = jnp.concatenate([g_ref[...], jnp.where(rows == cols, 1.0, 0.0).astype(jnp.float32)], axis=1)
     lane_row = lax.broadcasted_iota(jnp.int32, (1, 2 * n), 1)
-    for j in range(n):
+    for j in range(0, n, 2):
         lo = j - j % 8
         if j % 8 == 0 and j > 0:
             out_ref[lo - 8 : lo, :] = whole[:8]
             whole = whole[8:]
         r = j - lo
-        row = whole[r : r + 1]
-        inverse = 1.0 / row[:, j : j + 1]
-        kept = jnp.where(lane_row >= j, row, 0.0)
-        top = kept * jnp.sqrt(inverse)
+        first = jnp.where(lane_row >= j, whole[r : r + 1], 0.0)
+        inverse = 1.0 / first[:, j : j + 1]
+        first_scaled = first * inverse
+        second_row = whole[r + 1 : r + 2]
+        second = jnp.where(lane_row >= j + 1, second_row - second_row[:, j : j + 1] * first_scaled, 0.0)
+        inverse_2 = 1.0 / second[:, j + 1 : j + 2]
+        column = whole[:, j : j + 1]
+        column_2 = whole[:, j + 1 : j + 2] - column * first_scaled[:, j + 1 : j + 2]
         sub = lax.broadcasted_iota(jnp.int32, whole.shape, 0)
+        rest = whole - column * first_scaled - column_2 * (second * inverse_2)
         whole = jnp.where(
-            sub > r, whole - whole[:, j : j + 1] * (kept * inverse), jnp.where(sub == r, top, whole)
+            sub > r + 1,
+            rest,
+            jnp.where(
+                sub == r,
+                first * jnp.sqrt(inverse),
+                jnp.where(sub == r + 1, second * jnp.sqrt(inverse_2), whole),
+            ),
         )
     out_ref[n - 8 :, :] = whole
 

time: 147 us -> 160 us (1.088)
  Pallas kernels: 28.4 us -> 41.3 us
    pallas_call x1, Pallas kernels: 26.8 us -> 39.7 us  [factor_block(): pl.pallas_call(chol_kernel, out_shape=jax.ShapeDtypeStruct((n, 2 * n), jn...]
where the time goes in v11:
time: 160 us; the launch traced here: 159 us
  blocking collectives  72.3 us (45%)
  Pallas kernels  41.3 us (26%)
  waiting for transfers between devices  18.9 us (12%)
  starting transfers between devices  9.63 us (6%)
  matrix products  6.13 us (4%)
  other arithmetic  5.32 us (3%)
  local copies, waits for them, and re-layouts  4.24 us (3%)
    all_to_all x2, blocking collectives, scatter_sum(): got = lax.all_to_all(flat.reshape(count, -1), axis, 0, 0, tiled=True)  42.3 us
    pallas_call x1, Pallas kernels, factor_block(): pl.pallas_call(chol_kernel, out_shape=jax.ShapeDtypeStruct((n, 2 * n), jn...  39.7 us
    all_to_all x2, blocking collectives, gather_back(): return lax.all_to_all(spread, axis, 0, 0, tiled=True).reshape(-1)  30.1 us
    ppermute x6, waiting for transfers between devices, shifted(): return lax.ppermute(x, axis, pairs)  18.9 us
    ppermute x6, starting transfers between devices, shifted(): return lax.ppermute(x, axis, pairs)  9.63 us
  transfers between devices with their start and end apart: 6, of which 6 were waited for; matrix products, arithmetic and copies ran while one was open for 1% of the time, Pallas kernels for 1%

profile of v11, /device:TPU:24, one launch (start us, length us, event | category | flops | bytes accessed | tf_op | source)
XLA Modules:
  0.0 158.7 jit_solution(18010694129275733838)
XLA Ops:
  0.7 0.9 slice.15
  1.6 1.9 %collective-permute-start = (bf16[256,128]{1,0:T(8,128)(2,1)S(1)}, bf16[256,128]{1,0:T(8,128)(2,1)S(1)}, u32[]{:S(2)}, u32[]{:S(2)}) collective-permute-start(bf16[256,128]{1,0:T(8,128)(2,1)S(1)} %slice.15), channel_id=1, source_target_pairs={{0,1},{1,2},{2,3},{3,4},{4,5},{5,6},{6,7},{8,9},{9,10},{10,11},{11... | collective-permute-start | bytes 196616 | tf_op jit(solution)/shard_map/ppermute | solution.py:20
  3.5 1.2 convert_convert_fusion.coefs_ref
  4.7 1.6 shard_map.67
  6.2 0.9 collective-permute-done
  7.1 1.0 convolution_bitcast_fusion.1
  9.5 1.9 %collective-permute-start.1 = (f32[256,256]{0,1:T(8,128)S(1)}, f32[256,256]{0,1:T(8,128)S(1)}, u32[]{:S(2)}, u32[]{:S(2)}) collective-permute-start(f32[256,256]{0,1:T(8,128)S(1)} %fusion.42), channel_id=1, source_target_pairs={{0,1},{1,2},{2,3},{3,4},{4,5},{5,6},{6,7},{8,9},{9,10},{10,11},{11... | collective-permute-start | bytes 786440 | tf_op jit(solution)/shard_map/ppermute | solution.py:20
  11.4 5.8 %collective-permute-done.1 = f32[256,256]{0,1:T(8,128)S(1)} collective-permute-done((f32[256,256]{0,1:T(8,128)S(1)}, f32[256,256]{0,1:T(8,128)S(1)}, u32[]{:S(2)}, u32[]{:S(2)}) %collective-permute-start.1) | collective-permute-done | bytes 262176 | tf_op jit(solution)/shard_map/ppermute | solution.py:20
  17.3 1.3 collective-permute-start.3
  18.6 1.9 %collective-permute-start.2 = (f32[256]{0:T(256)S(1)}, f32[256]{0:T(256)S(1)}, u32[]{:S(2)}, u32[]{:S(2)}) collective-permute-start(f32[256]{0:T(256)S(1)} %bitcast.22), channel_id=1, source_target_pairs={{0,1},{1,2},{2,3},{3,4},{4,5},{5,6},{6,7},{8,9},{9,10},{10,11},{11... | collective-permute-start | bytes 3080 | tf_op jit(solution)/shard_map/ppermute | solution.py:20
  20.5 3.0 %collective-permute-done.2 = f32[256]{0:T(256)S(1)} collective-permute-done((f32[256]{0:T(256)S(1)}, f32[256]{0:T(256)S(1)}, u32[]{:S(2)}, u32[]{:S(2)}) %collective-permute-start.2) | collective-permute-done | bytes 1056 | tf_op jit(solution)/shard_map/ppermute | solution.py:20
  23.5 2.1 %collective-permute-done.3 = f32[256,256]{0,1:T(8,128)S(1)} collective-permute-done((f32[256,256]{0,1:T(8,128)S(1)}, f32[256,256]{0,1:T(8,128)S(1)}, u32[]{:S(2)}, u32[]{:S(2)}) %collective-permute-start.3) | collective-permute-done | bytes 262176 | tf_op jit(solution)/shard_map/ppermute | solution.py:20
  25.7 1.3 collective-permute-start.5
  27.0 1.3 collective-permute-start.4
  28.3 4.2 %collective-permute-done.4 = f32[256]{0:T(256)S(1)} collective-permute-done((f32[256]{0:T(256)S(1)}, f32[256]{0:T(256)S(1)}, u32[]{:S(2)}, u32[]{:S(2)}) %collective-permute-start.4) | collective-permute-done | bytes 1056 | tf_op jit(solution)/shard_map/ppermute | solution.py:20
  32.5 3.0 %collective-permute-done.5 = f32[256,256]{0,1:T(8,128)S(1)} collective-permute-done((f32[256,256]{0,1:T(8,128)S(1)}, f32[256,256]{0,1:T(8,128)S(1)}, u32[]{:S(2)}, u32[]{:S(2)}) %collective-permute-start.5) | collective-permute-done | bytes 262176 | tf_op jit(solution)/shard_map/ppermute | solution.py:20
  37.2 13.6 %all_to_all.31 = f32[4,1,49152]{2,1,0:T(1,128)S(1)} all-to-all(f32[4,1,49152]{2,1,0:T(1,128)S(1)} %all_to_all.26), channel_id=1, replica_groups=mesh['x'=4,'z'=16,'y'=4,'core'=2] {'x'}, dimensions={0} | all-to-all | bytes 1572864 | tf_op jit(solution)/shard_map/all_to_all | solution.py:50
  51.5 28.7 %all_to_all.32 = f32[16,1,3072]{2,1,0:T(1,128)S(1)} all-to-all(f32[16,1,3072]{2,1,0:T(1,128)S(1)} %bitcast.19), channel_id=1, replica_groups=mesh['x'=4,'z'=16,'y'=4,'core'=2] {'z'}, dimensions={0} | all-to-all | bytes 393216 | tf_op jit(solution)/shard_map/all_to_all | solution.py:50
  80.4 18.2 %all_to_all.33 = f32[16,1,3072]{2,1,0:T(1,128)S(1)} all-to-all(f32[16,1,3072]{2,1,0:T(1,128)S(1)} %broadcast_in_dim.28), channel_id=1, replica_groups=mesh['x'=4,'z'=16,'y'=4,'core'=2] {'z'}, dimensions={0} | all-to-all | bytes 393216 | tf_op jit(solution)/shard_map/all_to_all | solution.py:57
  99.0 11.9 %all_to_all.34 = f32[4,1,49152]{2,1,0:T(1,128)S(1)} all-to-all(f32[4,1,49152]{2,1,0:T(1,128)S(1)} %broadcast_in_dim.30), channel_id=1, replica_groups=mesh['x'=4,'z'=16,'y'=4,'core'=2] {'x'}, dimensions={0} | all-to-all | bytes 1572864 | tf_op jit(solution)/shard_map/all_to_all | solution.py:57
  110.9 2.3 %reduce.2 = f32[4,49152]{1,0:T(4,128)S(1)} reduce(f32[4,1,49152]{2,1,0:T(1,128)S(1)} %all_to_all.34, f32[]{:T(128)} %constant.18), dimensions={1}, to_apply=%all_to_all.25.reduce_sub_computation | reduce | bytes 1572868 | tf_op jit(solution)/shard_map/all_to_all | solution.py:57
  114.4 39.7 %shard_map.68 = f32[256,512]{1,0:T(8,128)} custom-call(f32[256,256]{1,0:T(8,128)} %slice.20.g_ref), custom_call_target="tpu_custom_call" | custom-call | tf_op jit(solution)/shard_map/pallas_call | solution.py:106
  154.2 2.4 %fusion = f32[1,256,512]{2,1,0:T(8,128)} fusion(f32[256,768]{1,0:T(8,128)S(1)} %reshape_reshape.4, f32[256,512]{1,0:T(8,128)} %shard_map.68), kind=kOutput, calls=%fused_computation.2 | convolution fusion | flops 402784256 | bytes 1310720 | tf_op jit(solution)/shard_map/dot_general | solution.py:152
  156.6 1.3 fusion.1
  (29 shorter events, 6.7 us)
Async XLA Ops:
  0.6 8.6 %copy-start = (bf16[512,256]{1,0:T(8,128)(2,1)S(1)}, bf16[512,256]{1,0:T(8,128)(2,1)}, u32[]{:S(2)}) copy-start(bf16[512,256]{1,0:T(8,128)(2,1)} %param.6) | copy-start | bytes 786436
  0.6 7.5 %copy-start.3 = (bf16[256,512]{1,0:T(8,128)(2,1)S(1)}, bf16[256,512]{1,0:T(8,128)(2,1)}, u32[]{:S(2)}) copy-start(bf16[256,512]{1,0:T(8,128)(2,1)} %param.4) | copy-start | bytes 786436
  1.6 5.6 %collective-permute-start = (bf16[256,128]{1,0:T(8,128)(2,1)S(1)}, bf16[256,128]{1,0:T(8,128)(2,1)S(1)}, u32[]{:S(2)}, u32[]{:S(2)}) collective-permute-start(bf16[256,128]{1,0:T(8,128)(2,1)S(1)} %slice.15), channel_id=1, source_target_pairs={{0,1},{1,2},{2,3},{3,4},{4,5},{5,6},{6,7},{8,9},{9,10},{10,11},{11... | collective-permute-start | bytes 196616 | tf_op jit(solution)/shard_map/ppermute | solution.py:20
  7.1 1.0 copy-start.5
  8.1 0.8 copy-start.2
  9.5 7.7 %copy-start.4 = (f32[1,256]{1,0:T(1,128)S(1)}, f32[1,256]{1,0:T(1,128)}, u32[]{:S(2)}) copy-start(f32[1,256]{1,0:T(1,128)} %param.7) | copy-start | bytes 3076
  9.5 7.7 %collective-permute-start.1 = (f32[256,256]{0,1:T(8,128)S(1)}, f32[256,256]{0,1:T(8,128)S(1)}, u32[]{:S(2)}, u32[]{:S(2)}) collective-permute-start(f32[256,256]{0,1:T(8,128)S(1)} %fusion.42), channel_id=1, source_target_pairs={{0,1},{1,2},{2,3},{3,4},{4,5},{5,6},{6,7},{8,9},{9,10},{10,11},{11... | collective-permute-start | bytes 786440 | tf_op jit(solution)/shard_map/ppermute | solution.py:20
  17.3 8.3 %collective-permute-start.3 = (f32[256,256]{0,1:T(8,128)S(1)}, f32[256,256]{0,1:T(8,128)S(1)}, u32[]{:S(2)}, u32[]{:S(2)}) collective-permute-start(f32[256,256]{0,1:T(8,128)S(1)} %multiply_add_fusion.2), channel_id=1, source_target_pairs={{0,2},{1,3},{2,4},{3,5},{4,6},{5,7},{8,10},{9,11},{10,12},{11,13},... | collective-permute-start | bytes 786440 | tf_op jit(solution)/shard_map/ppermute | solution.py:20
  18.6 4.9 %collective-permute-start.2 = (f32[256]{0:T(256)S(1)}, f32[256]{0:T(256)S(1)}, u32[]{:S(2)}, u32[]{:S(2)}) collective-permute-start(f32[256]{0:T(256)S(1)} %bitcast.22), channel_id=1, source_target_pairs={{0,1},{1,2},{2,3},{3,4},{4,5},{5,6},{6,7},{8,9},{9,10},{10,11},{11... | collective-permute-start | bytes 3080 | tf_op jit(solution)/shard_map/ppermute | solution.py:20
  25.7 9.8 %collective-permute-start.5 = (f32[256,256]{0,1:T(8,128)S(1)}, f32[256,256]{0,1:T(8,128)S(1)}, u32[]{:S(2)}, u32[]{:S(2)}) collective-permute-start(f32[256,256]{0,1:T(8,128)S(1)} %multiply_add_fusion.1), channel_id=1, source_target_pairs={{0,4},{1,5},{2,6},{3,7},{8,12},{9,13},{10,14},{11,15},{16,20},{17,... | collective-permute-start | bytes 786440 | tf_op jit(solution)/shard_map/ppermute | solution.py:20
  27.0 5.5 %collective-permute-start.4 = (f32[256]{0:T(256)S(1)}, f32[256]{0:T(256)S(1)}, u32[]{:S(2)}, u32[]{:S(2)}) collective-permute-start(f32[256]{0:T(256)S(1)} %mul.44), channel_id=1, source_target_pairs={{0,2},{1,3},{2,4},{3,5},{4,6},{5,7},{8,10},{9,11},{10,12},{11,13},... | collective-permute-start | bytes 3080 | tf_op jit(solution)/shard_map/ppermute | solution.py:20
  154.2 2.4 %copy-start.1 = (f32[256,512]{1,0:T(8,128)S(1)}, f32[256,512]{1,0:T(8,128)}, u32[]{:S(2)}) copy-start(f32[256,512]{1,0:T(8,128)} %shard_map.68) | copy-start | bytes 1572868

commit v12 on v10

--- a/solution.py
+++ b/solution.py
@@ -133,9 +133,13 @@
     partial = lax.dot_general(
         weighted, both, (((0,), (0,)), ((), ())), precision=HIGH, preferred_element_type=jnp.float32
     )
-    summed = reduce_rows(partial)
-    gram = summed[:, :rank_count]
-    cross = summed[:, rank_count:]
+    h = rank_count // 2
+    pieces = (partial[:h, :rank_count], partial[h:, h:rank_count], partial[:, rank_count:])
+    summed = reduce_rows(jnp.concatenate([p.reshape(-1) for p in pieces]))
+    upper_rows = summed[: h * rank_count].reshape(h, rank_count)
+    corner = summed[h * rank_count : h * rank_count + h * h].reshape(h, h)
+    cross = summed[h * rank_count + h * h :].reshape(rank_count, -1)
+    gram = jnp.concatenate([upper_rows, jnp.concatenate([upper_rows[:, h:].T, corner], axis=1)], axis=0)
     lower_one, inverse = factor_block(gram)
     scaled = jnp.dot(weighted, inverse.T, precision=HIGH) * root_points
     projected = jnp.dot(inverse, cross, precision=HIGH) * (math.sqrt(rank_count) / root_points)

time: 147 us -> 147 us (level)
  no operation moved by 1% of the time
where the time goes in v12:
time: 147 us; the launch traced here: 146 us
  blocking collectives  71.3 us (49%)
  Pallas kernels  28.4 us (19%)
  waiting for transfers between devices  18.9 us (13%)
  starting transfers between devices  9.63 us (7%)
  matrix products  6.14 us (4%)
  other arithmetic  5.82 us (4%)
  local copies, waits for them, and re-layouts  4.65 us (3%)
    all_to_all x2, blocking collectives, scatter_sum(): got = lax.all_to_all(flat.reshape(count, -1), axis, 0, 0, tiled=True)  41.8 us
    all_to_all x2, blocking collectives, gather_back(): return lax.all_to_all(spread, axis, 0, 0, tiled=True).reshape(-1)  29.5 us
    pallas_call x1, Pallas kernels, factor_block(): pl.pallas_call(chol_kernel, out_shape=jax.ShapeDtypeStruct((n, 2 * n), jn...  26.8 us
    ppermute x6, waiting for transfers between devices, shifted(): return lax.ppermute(x, axis, pairs)  18.9 us
    ppermute x6, starting transfers between devices, shifted(): return lax.ppermute(x, axis, pairs)  9.63 us
  transfers between devices with their start and end apart: 6, of which 6 were waited for; matrix products, arithmetic and copies ran while one was open for 1% of the time, Pallas kernels for 1%

profile of v12, /device:TPU:24, one launch (start us, length us, event | category | flops | bytes accessed | tf_op | source)
XLA Modules:
  0.0 145.7 jit_solution(478552644846147886)
XLA Ops:
  0.7 0.9 slice.40
  1.6 1.9 %collective-permute-start = (bf16[256,128]{1,0:T(8,128)(2,1)S(1)}, bf16[256,128]{1,0:T(8,128)(2,1)S(1)}, u32[]{:S(2)}, u32[]{:S(2)}) collective-permute-start(bf16[256,128]{1,0:T(8,128)(2,1)S(1)} %slice.40), channel_id=1, source_target_pairs={{0,1},{1,2},{2,3},{3,4},{4,5},{5,6},{6,7},{8,9},{9,10},{10,11},{11... | collective-permute-start | bytes 196616 | tf_op jit(solution)/shard_map/ppermute | solution.py:20
  3.5 1.2 convert_convert_fusion.coefs_ref
  4.7 1.6 %shard_map.67 = (bf16[128,128]{1,0:T(8,128)(2,1)}, bf16[128,128]{1,0:T(8,128)(2,1)}) custom-call(f32[63]{0:T(128)} %convert_convert_fusion.coefs_ref), custom_call_target="tpu_custom_call" | custom-call | tf_op jit(solution)/shard_map/pallas_call | solution.py:40
  6.2 0.9 collective-permute-done
  7.1 1.0 convolution_bitcast_fusion.1
  9.5 1.9 %collective-permute-start.1 = (f32[256,256]{0,1:T(8,128)S(1)}, f32[256,256]{0,1:T(8,128)S(1)}, u32[]{:S(2)}, u32[]{:S(2)}) collective-permute-start(f32[256,256]{0,1:T(8,128)S(1)} %fusion.42), channel_id=1, source_target_pairs={{0,1},{1,2},{2,3},{3,4},{4,5},{5,6},{6,7},{8,9},{9,10},{10,11},{11... | collective-permute-start | bytes 786440 | tf_op jit(solution)/shard_map/ppermute | solution.py:20
  11.4 5.8 %collective-permute-done.1 = f32[256,256]{0,1:T(8,128)S(1)} collective-permute-done((f32[256,256]{0,1:T(8,128)S(1)}, f32[256,256]{0,1:T(8,128)S(1)}, u32[]{:S(2)}, u32[]{:S(2)}) %collective-permute-start.1) | collective-permute-done | bytes 262176 | tf_op jit(solution)/shard_map/ppermute | solution.py:20
  17.3 1.3 collective-permute-start.3
  18.6 1.9 %collective-permute-start.2 = (f32[256]{0:T(256)S(1)}, f32[256]{0:T(256)S(1)}, u32[]{:S(2)}, u32[]{:S(2)}) collective-permute-start(f32[256]{0:T(256)S(1)} %bitcast.38), channel_id=1, source_target_pairs={{0,1},{1,2},{2,3},{3,4},{4,5},{5,6},{6,7},{8,9},{9,10},{10,11},{11... | collective-permute-start | bytes 3080 | tf_op jit(solution)/shard_map/ppermute | solution.py:20
  20.5 3.0 %collective-permute-done.2 = f32[256]{0:T(256)S(1)} collective-permute-done((f32[256]{0:T(256)S(1)}, f32[256]{0:T(256)S(1)}, u32[]{:S(2)}, u32[]{:S(2)}) %collective-permute-start.2) | collective-permute-done | bytes 1056 | tf_op jit(solution)/shard_map/ppermute | solution.py:20
  23.5 2.1 %collective-permute-done.3 = f32[256,256]{0,1:T(8,128)S(1)} collective-permute-done((f32[256,256]{0,1:T(8,128)S(1)}, f32[256,256]{0,1:T(8,128)S(1)}, u32[]{:S(2)}, u32[]{:S(2)}) %collective-permute-start.3) | collective-permute-done | bytes 262176 | tf_op jit(solution)/shard_map/ppermute | solution.py:20
  25.7 1.3 collective-permute-start.5
  27.0 1.3 collective-permute-start.4
  28.3 4.2 %collective-permute-done.4 = f32[256]{0:T(256)S(1)} collective-permute-done((f32[256]{0:T(256)S(1)}, f32[256]{0:T(256)S(1)}, u32[]{:S(2)}, u32[]{:S(2)}) %collective-permute-start.4) | collective-permute-done | bytes 1056 | tf_op jit(solution)/shard_map/ppermute | solution.py:20
  32.5 3.0 %collective-permute-done.5 = f32[256,256]{0,1:T(8,128)S(1)} collective-permute-done((f32[256,256]{0,1:T(8,128)S(1)}, f32[256,256]{0,1:T(8,128)S(1)}, u32[]{:S(2)}, u32[]{:S(2)}) %collective-permute-start.5) | collective-permute-done | bytes 262176 | tf_op jit(solution)/shard_map/ppermute | solution.py:20
  36.8 13.2 %all_to_all.30 = f32[4,1,45056]{2,1,0:T(1,128)S(1)} all-to-all(f32[4,1,45056]{2,1,0:T(1,128)S(1)} %bitcast.31), channel_id=1, replica_groups=mesh['x'=4,'z'=16,'y'=4,'core'=2] {'x'}, dimensions={0} | all-to-all | bytes 1441792 | tf_op jit(solution)/shard_map/all_to_all | solution.py:50
  50.7 28.5 %all_to_all.31 = f32[16,1,2816]{2,1,0:T(1,128)S(1)} all-to-all(f32[16,1,2816]{2,1,0:T(1,128)S(1)} %bitcast.34), channel_id=1, replica_groups=mesh['x'=4,'z'=16,'y'=4,'core'=2] {'z'}, dimensions={0} | all-to-all | bytes 360448 | tf_op jit(solution)/shard_map/all_to_all | solution.py:50
  79.4 18.0 %all_to_all.32 = f32[16,1,2816]{2,1,0:T(1,128)S(1)} all-to-all(f32[16,1,2816]{2,1,0:T(1,128)S(1)} %broadcast_in_dim.28), channel_id=1, replica_groups=mesh['x'=4,'z'=16,'y'=4,'core'=2] {'z'}, dimensions={0} | all-to-all | bytes 360448 | tf_op jit(solution)/shard_map/all_to_all | solution.py:57
  97.8 11.5 %all_to_all.33 = f32[4,1,45056]{2,1,0:T(1,128)S(1)} all-to-all(f32[4,1,45056]{2,1,0:T(1,128)S(1)} %broadcast_in_dim.30), channel_id=1, replica_groups=mesh['x'=4,'z'=16,'y'=4,'core'=2] {'x'}, dimensions={0} | all-to-all | bytes 1441792 | tf_op jit(solution)/shard_map/all_to_all | solution.py:57
  109.4 2.1 %reduce.2 = f32[4,45056]{1,0:T(4,128)S(1)} reduce(f32[4,1,45056]{2,1,0:T(1,128)S(1)} %all_to_all.33, f32[]{:T(128)} %constant.18), dimensions={1}, to_apply=%all_to_all.25.reduce_sub_computation | reduce | bytes 1441796 | tf_op jit(solution)/shard_map/all_to_all | solution.py:57
  114.4 26.8 %shard_map.68 = f32[256,512]{1,0:T(8,128)} custom-call(f32[256,256]{1,0:T(8,128)} %maximum_maximum_fusion.g_ref), custom_call_target="tpu_custom_call" | custom-call | tf_op jit(solution)/shard_map/pallas_call | solution.py:95
  141.3 2.3 %fusion.1 = f32[1,256,256]{2,1,0:T(8,128)} fusion(f32[256,256]{0,1:T(8,128)S(1)} %multiply_add_fusion, f32[256,512]{1,0:T(8,128)} %shard_map.68), kind=kOutput, calls=%fused_computation.4 | convolution fusion | flops 201392128 | bytes 786432 | tf_op jit(solution)/shard_map/dot_general | solution.py:144
  144.3 1.4 fusion
  (42 shorter events, 7.8 us)
Async XLA Ops:
  0.6 8.6 %copy-start = (bf16[512,256]{1,0:T(8,128)(2,1)S(1)}, bf16[512,256]{1,0:T(8,128)(2,1)}, u32[]{:S(2)}) copy-start(bf16[512,256]{1,0:T(8,128)(2,1)} %param.6) | copy-start | bytes 786436
  0.6 7.5 %copy-start.4 = (bf16[256,512]{1,0:T(8,128)(2,1)S(1)}, bf16[256,512]{1,0:T(8,128)(2,1)}, u32[]{:S(2)}) copy-start(bf16[256,512]{1,0:T(8,128)(2,1)} %param.4) | copy-start | bytes 786436
  1.6 5.6 %collective-permute-start = (bf16[256,128]{1,0:T(8,128)(2,1)S(1)}, bf16[256,128]{1,0:T(8,128)(2,1)S(1)}, u32[]{:S(2)}, u32[]{:S(2)}) collective-permute-start(bf16[256,128]{1,0:T(8,128)(2,1)S(1)} %slice.40), channel_id=1, source_target_pairs={{0,1},{1,2},{2,3},{3,4},{4,5},{5,6},{6,7},{8,9},{9,10},{10,11},{11... | collective-permute-start | bytes 196616 | tf_op jit(solution)/shard_map/ppermute | solution.py:20
  7.1 1.0 copy-start.6
  8.1 0.8 copy-start.3
  9.5 7.7 %copy-start.5 = (f32[1,256]{1,0:T(1,128)S(1)}, f32[1,256]{1,0:T(1,128)}, u32[]{:S(2)}) copy-start(f32[1,256]{1,0:T(1,128)} %param.7) | copy-start | bytes 3076
  9.5 7.7 %collective-permute-start.1 = (f32[256,256]{0,1:T(8,128)S(1)}, f32[256,256]{0,1:T(8,128)S(1)}, u32[]{:S(2)}, u32[]{:S(2)}) collective-permute-start(f32[256,256]{0,1:T(8,128)S(1)} %fusion.42), channel_id=1, source_target_pairs={{0,1},{1,2},{2,3},{3,4},{4,5},{5,6},{6,7},{8,9},{9,10},{10,11},{11... | collective-permute-start | bytes 786440 | tf_op jit(solution)/shard_map/ppermute | solution.py:20
  17.3 8.3 %collective-permute-start.3 = (f32[256,256]{0,1:T(8,128)S(1)}, f32[256,256]{0,1:T(8,128)S(1)}, u32[]{:S(2)}, u32[]{:S(2)}) collective-permute-start(f32[256,256]{0,1:T(8,128)S(1)} %multiply_add_fusion.2), channel_id=1, source_target_pairs={{0,2},{1,3},{2,4},{3,5},{4,6},{5,7},{8,10},{9,11},{10,12},{11,13},... | collective-permute-start | bytes 786440 | tf_op jit(solution)/shard_map/ppermute | solution.py:20
  18.6 4.9 %collective-permute-start.2 = (f32[256]{0:T(256)S(1)}, f32[256]{0:T(256)S(1)}, u32[]{:S(2)}, u32[]{:S(2)}) collective-permute-start(f32[256]{0:T(256)S(1)} %bitcast.38), channel_id=1, source_target_pairs={{0,1},{1,2},{2,3},{3,4},{4,5},{5,6},{6,7},{8,9},{9,10},{10,11},{11... | collective-permute-start | bytes 3080 | tf_op jit(solution)/shard_map/ppermute | solution.py:20
  25.7 9.8 %collective-permute-start.5 = (f32[256,256]{0,1:T(8,128)S(1)}, f32[256,256]{0,1:T(8,128)S(1)}, u32[]{:S(2)}, u32[]{:S(2)}) collective-permute-start(f32[256,256]{0,1:T(8,128)S(1)} %multiply_add_fusion.1), channel_id=1, source_target_pairs={{0,4},{1,5},{2,6},{3,7},{8,12},{9,13},{10,14},{11,15},{16,20},{17,... | collective-permute-start | bytes 786440 | tf_op jit(solution)/shard_map/ppermute | solution.py:20
  27.0 5.5 %collective-permute-start.4 = (f32[256]{0:T(256)S(1)}, f32[256]{0:T(256)S(1)}, u32[]{:S(2)}, u32[]{:S(2)}) collective-permute-start(f32[256]{0:T(256)S(1)} %mul.44), channel_id=1, source_target_pairs={{0,2},{1,3},{2,4},{3,5},{4,6},{5,7},{8,10},{9,11},{10,12},{11,13},... | collective-permute-start | bytes 3080 | tf_op jit(solution)/shard_map/ppermute | solution.py:20
  111.9 0.9 copy-start.2
  112.8 0.9 slice-start
  141.3 2.3 %copy-start.1 = (f32[256,512]{1,0:T(8,128)S(1)}, f32[256,512]{1,0:T(8,128)}, u32[]{:S(2)}) copy-start(f32[256,512]{1,0:T(8,128)} %shard_map.68) | copy-start | bytes 1572868

commit v13 on v10

--- a/solution.py
+++ b/solution.py
@@ -137,8 +137,8 @@
     gram = summed[:, :rank_count]
     cross = summed[:, rank_count:]
     lower_one, inverse = factor_block(gram)
-    scaled = jnp.dot(weighted, inverse.T, precision=HIGH) * root_points
-    projected = jnp.dot(inverse, cross, precision=HIGH) * (math.sqrt(rank_count) / root_points)
+    scaled = jnp.dot(weighted, inverse.T, precision=lax.Precision.HIGH) * root_points
+    projected = jnp.dot(inverse, cross, precision=lax.Precision.HIGH) * (math.sqrt(rank_count) / root_points)
     upper = lower_one.T / root_points
     return (scaled[None], upper[None], projected[None])
 

time: 147 us -> 147 us (level)
  no operation moved by 1% of the time
where the time goes in v13:
time: 147 us; the launch traced here: 145 us
  blocking collectives  72.3 us (49%)
  Pallas kernels  28.4 us (19%)
  waiting for transfers between devices  18.9 us (13%)
  starting transfers between devices  9.63 us (7%)
  matrix products  5.7 us (4%)
  other arithmetic  5.32 us (4%)
  local copies, waits for them, and re-layouts  4.24 us (3%)
    all_to_all x2, blocking collectives, scatter_sum(): got = lax.all_to_all(flat.reshape(count, -1), axis, 0, 0, tiled=True)  42.3 us
    all_to_all x2, blocking collectives, gather_back(): return lax.all_to_all(spread, axis, 0, 0, tiled=True).reshape(-1)  30.1 us
    pallas_call x1, Pallas kernels, factor_block(): pl.pallas_call(chol_kernel, out_shape=jax.ShapeDtypeStruct((n, 2 * n), jn...  26.8 us
    ppermute x6, waiting for transfers between devices, shifted(): return lax.ppermute(x, axis, pairs)  18.9 us
    ppermute x6, starting transfers between devices, shifted(): return lax.ppermute(x, axis, pairs)  9.63 us
  transfers between devices with their start and end apart: 6, of which 6 were waited for; matrix products, arithmetic and copies ran while one was open for 1% of the time, Pallas kernels for 1%

profile of v13, /device:TPU:24, one launch (start us, length us, event | category | flops | bytes accessed | tf_op | source)
XLA Modules:
  0.0 145.3 jit_solution(9832241471685570552)
XLA Ops:
  0.7 0.9 slice.15
  1.6 1.9 %collective-permute-start = (bf16[256,128]{1,0:T(8,128)(2,1)S(1)}, bf16[256,128]{1,0:T(8,128)(2,1)S(1)}, u32[]{:S(2)}, u32[]{:S(2)}) collective-permute-start(bf16[256,128]{1,0:T(8,128)(2,1)S(1)} %slice.15), channel_id=1, source_target_pairs={{0,1},{1,2},{2,3},{3,4},{4,5},{5,6},{6,7},{8,9},{9,10},{10,11},{11... | collective-permute-start | bytes 196616 | tf_op jit(solution)/shard_map/ppermute | solution.py:20
  3.5 1.2 convert_convert_fusion.coefs_ref
  4.7 1.6 %shard_map.67 = (bf16[128,128]{1,0:T(8,128)(2,1)}, bf16[128,128]{1,0:T(8,128)(2,1)}) custom-call(f32[63]{0:T(128)} %convert_convert_fusion.coefs_ref), custom_call_target="tpu_custom_call" | custom-call | tf_op jit(solution)/shard_map/pallas_call | solution.py:40
  6.2 0.9 collective-permute-done
  7.1 1.0 convolution_bitcast_fusion.1
  9.5 1.9 %collective-permute-start.1 = (f32[256,256]{0,1:T(8,128)S(1)}, f32[256,256]{0,1:T(8,128)S(1)}, u32[]{:S(2)}, u32[]{:S(2)}) collective-permute-start(f32[256,256]{0,1:T(8,128)S(1)} %fusion.42), channel_id=1, source_target_pairs={{0,1},{1,2},{2,3},{3,4},{4,5},{5,6},{6,7},{8,9},{9,10},{10,11},{11... | collective-permute-start | bytes 786440 | tf_op jit(solution)/shard_map/ppermute | solution.py:20
  11.4 5.8 %collective-permute-done.1 = f32[256,256]{0,1:T(8,128)S(1)} collective-permute-done((f32[256,256]{0,1:T(8,128)S(1)}, f32[256,256]{0,1:T(8,128)S(1)}, u32[]{:S(2)}, u32[]{:S(2)}) %collective-permute-start.1) | collective-permute-done | bytes 262176 | tf_op jit(solution)/shard_map/ppermute | solution.py:20
  17.3 1.3 collective-permute-start.3
  18.6 1.9 %collective-permute-start.2 = (f32[256]{0:T(256)S(1)}, f32[256]{0:T(256)S(1)}, u32[]{:S(2)}, u32[]{:S(2)}) collective-permute-start(f32[256]{0:T(256)S(1)} %bitcast.22), channel_id=1, source_target_pairs={{0,1},{1,2},{2,3},{3,4},{4,5},{5,6},{6,7},{8,9},{9,10},{10,11},{11... | collective-permute-start | bytes 3080 | tf_op jit(solution)/shard_map/ppermute | solution.py:20
  20.5 3.0 %collective-permute-done.2 = f32[256]{0:T(256)S(1)} collective-permute-done((f32[256]{0:T(256)S(1)}, f32[256]{0:T(256)S(1)}, u32[]{:S(2)}, u32[]{:S(2)}) %collective-permute-start.2) | collective-permute-done | bytes 1056 | tf_op jit(solution)/shard_map/ppermute | solution.py:20
  23.5 2.1 %collective-permute-done.3 = f32[256,256]{0,1:T(8,128)S(1)} collective-permute-done((f32[256,256]{0,1:T(8,128)S(1)}, f32[256,256]{0,1:T(8,128)S(1)}, u32[]{:S(2)}, u32[]{:S(2)}) %collective-permute-start.3) | collective-permute-done | bytes 262176 | tf_op jit(solution)/shard_map/ppermute | solution.py:20
  25.7 1.3 collective-permute-start.5
  27.0 1.3 collective-permute-start.4
  28.3 4.2 %collective-permute-done.4 = f32[256]{0:T(256)S(1)} collective-permute-done((f32[256]{0:T(256)S(1)}, f32[256]{0:T(256)S(1)}, u32[]{:S(2)}, u32[]{:S(2)}) %collective-permute-start.4) | collective-permute-done | bytes 1056 | tf_op jit(solution)/shard_map/ppermute | solution.py:20
  32.5 3.0 %collective-permute-done.5 = f32[256,256]{0,1:T(8,128)S(1)} collective-permute-done((f32[256,256]{0,1:T(8,128)S(1)}, f32[256,256]{0,1:T(8,128)S(1)}, u32[]{:S(2)}, u32[]{:S(2)}) %collective-permute-start.5) | collective-permute-done | bytes 262176 | tf_op jit(solution)/shard_map/ppermute | solution.py:20
  37.2 13.6 %all_to_all.31 = f32[4,1,49152]{2,1,0:T(1,128)S(1)} all-to-all(f32[4,1,49152]{2,1,0:T(1,128)S(1)} %all_to_all.26), channel_id=1, replica_groups=mesh['x'=4,'z'=16,'y'=4,'core'=2] {'x'}, dimensions={0} | all-to-all | bytes 1572864 | tf_op jit(solution)/shard_map/all_to_all | solution.py:50
  51.5 28.7 %all_to_all.32 = f32[16,1,3072]{2,1,0:T(1,128)S(1)} all-to-all(f32[16,1,3072]{2,1,0:T(1,128)S(1)} %bitcast.19), channel_id=1, replica_groups=mesh['x'=4,'z'=16,'y'=4,'core'=2] {'z'}, dimensions={0} | all-to-all | bytes 393216 | tf_op jit(solution)/shard_map/all_to_all | solution.py:50
  80.4 18.2 %all_to_all.33 = f32[16,1,3072]{2,1,0:T(1,128)S(1)} all-to-all(f32[16,1,3072]{2,1,0:T(1,128)S(1)} %broadcast_in_dim.28), channel_id=1, replica_groups=mesh['x'=4,'z'=16,'y'=4,'core'=2] {'z'}, dimensions={0} | all-to-all | bytes 393216 | tf_op jit(solution)/shard_map/all_to_all | solution.py:57
  99.0 11.9 %all_to_all.34 = f32[4,1,49152]{2,1,0:T(1,128)S(1)} all-to-all(f32[4,1,49152]{2,1,0:T(1,128)S(1)} %broadcast_in_dim.30), channel_id=1, replica_groups=mesh['x'=4,'z'=16,'y'=4,'core'=2] {'x'}, dimensions={0} | all-to-all | bytes 1572864 | tf_op jit(solution)/shard_map/all_to_all | solution.py:57
  110.9 2.3 %reduce.2 = f32[4,49152]{1,0:T(4,128)S(1)} reduce(f32[4,1,49152]{2,1,0:T(1,128)S(1)} %all_to_all.34, f32[]{:T(128)} %constant.18), dimensions={1}, to_apply=%all_to_all.25.reduce_sub_computation | reduce | bytes 1572868 | tf_op jit(solution)/shard_map/all_to_all | solution.py:57
  114.4 26.8 %shard_map.68 = f32[256,512]{1,0:T(8,128)} custom-call(f32[256,256]{1,0:T(8,128)} %slice.20.g_ref), custom_call_target="tpu_custom_call" | custom-call | tf_op jit(solution)/shard_map/pallas_call | solution.py:95
  141.3 2.2 %fusion = f32[1,256,512]{2,1,0:T(8,128)} fusion(f32[256,768]{1,0:T(8,128)S(1)} %reshape_reshape.4, f32[256,512]{1,0:T(8,128)} %shard_map.68), kind=kOutput, calls=%fused_computation.2 | convolution fusion | flops 201457664 | bytes 1310720 | tf_op jit(solution)/shard_map/dot_general | solution.py:141
  143.5 1.1 fusion.1
  (29 shorter events, 6.7 us)
Async XLA Ops:
  0.6 8.6 %copy-start = (bf16[512,256]{1,0:T(8,128)(2,1)S(1)}, bf16[512,256]{1,0:T(8,128)(2,1)}, u32[]{:S(2)}) copy-start(bf16[512,256]{1,0:T(8,128)(2,1)} %param.6) | copy-start | bytes 786436
  0.6 7.5 %copy-start.3 = (bf16[256,512]{1,0:T(8,128)(2,1)S(1)}, bf16[256,512]{1,0:T(8,128)(2,1)}, u32[]{:S(2)}) copy-start(bf16[256,512]{1,0:T(8,128)(2,1)} %param.4) | copy-start | bytes 786436
  1.6 5.6 %collective-permute-start = (bf16[256,128]{1,0:T(8,128)(2,1)S(1)}, bf16[256,128]{1,0:T(8,128)(2,1)S(1)}, u32[]{:S(2)}, u32[]{:S(2)}) collective-permute-start(bf16[256,128]{1,0:T(8,128)(2,1)S(1)} %slice.15), channel_id=1, source_target_pairs={{0,1},{1,2},{2,3},{3,4},{4,5},{5,6},{6,7},{8,9},{9,10},{10,11},{11... | collective-permute-start | bytes 196616 | tf_op jit(solution)/shard_map/ppermute | solution.py:20
  7.1 1.0 copy-start.5
  8.1 0.8 copy-start.2
  9.5 7.7 %copy-start.4 = (f32[1,256]{1,0:T(1,128)S(1)}, f32[1,256]{1,0:T(1,128)}, u32[]{:S(2)}) copy-start(f32[1,256]{1,0:T(1,128)} %param.7) | copy-start | bytes 3076
  9.5 7.7 %collective-permute-start.1 = (f32[256,256]{0,1:T(8,128)S(1)}, f32[256,256]{0,1:T(8,128)S(1)}, u32[]{:S(2)}, u32[]{:S(2)}) collective-permute-start(f32[256,256]{0,1:T(8,128)S(1)} %fusion.42), channel_id=1, source_target_pairs={{0,1},{1,2},{2,3},{3,4},{4,5},{5,6},{6,7},{8,9},{9,10},{10,11},{11... | collective-permute-start | bytes 786440 | tf_op jit(solution)/shard_map/ppermute | solution.py:20
  17.3 8.3 %collective-permute-start.3 = (f32[256,256]{0,1:T(8,128)S(1)}, f32[256,256]{0,1:T(8,128)S(1)}, u32[]{:S(2)}, u32[]{:S(2)}) collective-permute-start(f32[256,256]{0,1:T(8,128)S(1)} %multiply_add_fusion.2), channel_id=1, source_target_pairs={{0,2},{1,3},{2,4},{3,5},{4,6},{5,7},{8,10},{9,11},{10,12},{11,13},... | collective-permute-start | bytes 786440 | tf_op jit(solution)/shard_map/ppermute | solution.py:20
  18.6 4.9 %collective-permute-start.2 = (f32[256]{0:T(256)S(1)}, f32[256]{0:T(256)S(1)}, u32[]{:S(2)}, u32[]{:S(2)}) collective-permute-start(f32[256]{0:T(256)S(1)} %bitcast.22), channel_id=1, source_target_pairs={{0,1},{1,2},{2,3},{3,4},{4,5},{5,6},{6,7},{8,9},{9,10},{10,11},{11... | collective-permute-start | bytes 3080 | tf_op jit(solution)/shard_map/ppermute | solution.py:20
  25.7 9.8 %collective-permute-start.5 = (f32[256,256]{0,1:T(8,128)S(1)}, f32[256,256]{0,1:T(8,128)S(1)}, u32[]{:S(2)}, u32[]{:S(2)}) collective-permute-start(f32[256,256]{0,1:T(8,128)S(1)} %multiply_add_fusion.1), channel_id=1, source_target_pairs={{0,4},{1,5},{2,6},{3,7},{8,12},{9,13},{10,14},{11,15},{16,20},{17,... | collective-permute-start | bytes 786440 | tf_op jit(solution)/shard_map/ppermute | solution.py:20
  27.0 5.5 %collective-permute-start.4 = (f32[256]{0:T(256)S(1)}, f32[256]{0:T(256)S(1)}, u32[]{:S(2)}, u32[]{:S(2)}) collective-permute-start(f32[256]{0:T(256)S(1)} %mul.44), channel_id=1, source_target_pairs={{0,2},{1,3},{2,4},{3,5},{4,6},{5,7},{8,10},{9,11},{10,12},{11,13},... | collective-permute-start | bytes 3080 | tf_op jit(solution)/shard_map/ppermute | solution.py:20
  141.3 2.2 %copy-start.1 = (f32[256,512]{1,0:T(8,128)S(1)}, f32[256,512]{1,0:T(8,128)}, u32[]{:S(2)}) copy-start(f32[256,512]{1,0:T(8,128)} %shard_map.68) | copy-start | bytes 1572868

commit v14 on v10

--- a/solution.py
+++ b/solution.py
@@ -112,15 +112,17 @@
     main = jnp.dot(frames, main_band, preferred_element_type=jnp.float32)
     edge = jnp.dot(history, carry, preferred_element_type=jnp.float32)
     filtered = (main + jnp.pad(edge, ((0, 0), (0, frame_count - BLOCK)))).astype(jnp.bfloat16)
-    sketched = jnp.dot(filtered, sketch_matrix, preferred_element_type=jnp.float32)
-
     factors = []
     factor = decay_rates[0]
     d = 1
     while d < batch_count:
         factors.append(factor)
-        factor = factor * shifted(factor, BATCH, d)
+        if 2 * d < batch_count:
+            factor = factor * shifted(factor, BATCH, d)
         d *= 2
+    sketch_matrix, factors = lax.optimization_barrier((sketch_matrix, factors))
+    sketched = jnp.dot(filtered, sketch_matrix, preferred_element_type=jnp.float32)
+
     weighted = sketched
     d = 1
     for factor in factors:

time: 147 us -> 152 us (1.034)
  waiting for transfers between devices: 18.9 us -> 22.8 us
    ppermute x6, waiting for transfers between devices: 18.9 us -> 22.8 us  [shifted(): return lax.ppermute(x, axis, pairs)]
  transfers between devices with their start and end apart: 6 -> 6, of which waited for: 6 -> 5; matrix products, arithmetic and copies ran while one was open for 1% -> 1% of each run, Pallas kernels for 1% -> 1%
where the time goes in v14:
time: 152 us; the launch traced here: 150 us
  blocking collectives  72.5 us (48%)
  Pallas kernels  28.4 us (19%)
  waiting for transfers between devices  22.8 us (15%)
  starting transfers between devices  9.6 us (6%)
  matrix products  6.14 us (4%)
  other arithmetic  5.32 us (4%)
  local copies, waits for them, and re-layouts  4.87 us (3%)
    all_to_all x2, blocking collectives, scatter_sum(): got = lax.all_to_all(flat.reshape(count, -1), axis, 0, 0, tiled=True)  42.3 us
    all_to_all x2, blocking collectives, gather_back(): return lax.all_to_all(spread, axis, 0, 0, tiled=True).reshape(-1)  30.2 us
    pallas_call x1, Pallas kernels, factor_block(): pl.pallas_call(chol_kernel, out_shape=jax.ShapeDtypeStruct((n, 2 * n), jn...  26.8 us
    ppermute x6, waiting for transfers between devices, shifted(): return lax.ppermute(x, axis, pairs)  22.8 us
    ppermute x6, starting transfers between devices, shifted(): return lax.ppermute(x, axis, pairs)  9.6 us
  transfers between devices with their start and end apart: 6, of which 5 were waited for; matrix products, arithmetic and copies ran while one was open for 1% of the time, Pallas kernels for 1%

profile of v14, /device:TPU:24, one launch (start us, length us, event | category | flops | bytes accessed | tf_op | source)
XLA Modules:
  0.0 150.5 jit_solution(12722148651449086043)
XLA Ops:
  1.4 1.9 %collective-permute-start.1 = (f32[256]{0:T(256)S(1)}, f32[256]{0:T(256)S(1)}, u32[]{:S(2)}, u32[]{:S(2)}) collective-permute-start(f32[256]{0:T(256)S(1)} %bitcast.21), channel_id=1, source_target_pairs={{0,1},{1,2},{2,3},{3,4},{4,5},{5,6},{6,7},{8,9},{9,10},{10,11},{11... | collective-permute-start | bytes 3080 | tf_op jit(solution)/shard_map/ppermute | solution.py:20
  3.3 0.8 slice.15
  4.1 1.9 %collective-permute-start = (bf16[256,128]{1,0:T(8,128)(2,1)S(1)}, bf16[256,128]{1,0:T(8,128)(2,1)S(1)}, u32[]{:S(2)}, u32[]{:S(2)}) collective-permute-start(bf16[256,128]{1,0:T(8,128)(2,1)S(1)} %slice.15), channel_id=1, source_target_pairs={{0,1},{1,2},{2,3},{3,4},{4,5},{5,6},{6,7},{8,9},{9,10},{10,11},{11... | collective-permute-start | bytes 196616 | tf_op jit(solution)/shard_map/ppermute | solution.py:20
  6.3 1.3 collective-permute-start.2
  7.5 1.2 convert_convert_fusion.coefs_ref
  8.7 1.6 %shard_map.67 = (bf16[128,128]{1,0:T(8,128)(2,1)}, bf16[128,128]{1,0:T(8,128)(2,1)}) custom-call(f32[63]{0:T(128)} %convert_convert_fusion.coefs_ref), custom_call_target="tpu_custom_call" | custom-call | tf_op jit(solution)/shard_map/pallas_call | solution.py:40
  10.3 1.4 collective-permute-done.2
  11.7 1.0 convolution_bitcast_fusion.1
  14.1 1.9 %collective-permute-start.3 = (f32[256,256]{0,1:T(8,128)S(1)}, f32[256,256]{0,1:T(8,128)S(1)}, u32[]{:S(2)}, u32[]{:S(2)}) collective-permute-start(f32[256,256]{0,1:T(8,128)S(1)} %fusion.42), channel_id=1, source_target_pairs={{0,1},{1,2},{2,3},{3,4},{4,5},{5,6},{6,7},{8,9},{9,10},{10,11},{11... | collective-permute-start | bytes 786440 | tf_op jit(solution)/shard_map/ppermute | solution.py:20
  16.0 5.8 %collective-permute-done.3 = f32[256,256]{0,1:T(8,128)S(1)} collective-permute-done((f32[256,256]{0,1:T(8,128)S(1)}, f32[256,256]{0,1:T(8,128)S(1)}, u32[]{:S(2)}, u32[]{:S(2)}) %collective-permute-start.3) | collective-permute-done | bytes 262176 | tf_op jit(solution)/shard_map/ppermute | solution.py:20
  21.9 1.3 collective-permute-start.4
  23.2 7.0 %collective-permute-done.4 = f32[256,256]{0,1:T(8,128)S(1)} collective-permute-done((f32[256,256]{0,1:T(8,128)S(1)}, f32[256,256]{0,1:T(8,128)S(1)}, u32[]{:S(2)}, u32[]{:S(2)}) %collective-permute-start.4) | collective-permute-done | bytes 262176 | tf_op jit(solution)/shard_map/ppermute | solution.py:20
  30.3 1.3 collective-permute-start.5
  31.6 8.5 %collective-permute-done.5 = f32[256,256]{0,1:T(8,128)S(1)} collective-permute-done((f32[256,256]{0,1:T(8,128)S(1)}, f32[256,256]{0,1:T(8,128)S(1)}, u32[]{:S(2)}, u32[]{:S(2)}) %collective-permute-start.5) | collective-permute-done | bytes 262176 | tf_op jit(solution)/shard_map/ppermute | solution.py:20
  40.1 0.8 fusion.2
  41.0 0.8 all_to_all.26
  41.8 13.6 %all_to_all.31 = f32[4,1,49152]{2,1,0:T(1,128)S(1)} all-to-all(f32[4,1,49152]{2,1,0:T(1,128)S(1)} %all_to_all.26), channel_id=1, replica_groups=mesh['x'=4,'z'=16,'y'=4,'core'=2] {'x'}, dimensions={0} | all-to-all | bytes 1572864 | tf_op jit(solution)/shard_map/all_to_all | solution.py:50
  56.1 28.7 %all_to_all.32 = f32[16,1,3072]{2,1,0:T(1,128)S(1)} all-to-all(f32[16,1,3072]{2,1,0:T(1,128)S(1)} %bitcast.19), channel_id=1, replica_groups=mesh['x'=4,'z'=16,'y'=4,'core'=2] {'z'}, dimensions={0} | all-to-all | bytes 393216 | tf_op jit(solution)/shard_map/all_to_all | solution.py:50
  85.0 18.3 %all_to_all.33 = f32[16,1,3072]{2,1,0:T(1,128)S(1)} all-to-all(f32[16,1,3072]{2,1,0:T(1,128)S(1)} %broadcast_in_dim.29), channel_id=1, replica_groups=mesh['x'=4,'z'=16,'y'=4,'core'=2] {'z'}, dimensions={0} | all-to-all | bytes 393216 | tf_op jit(solution)/shard_map/all_to_all | solution.py:57
  103.7 11.9 %all_to_all.34 = f32[4,1,49152]{2,1,0:T(1,128)S(1)} all-to-all(f32[4,1,49152]{2,1,0:T(1,128)S(1)} %broadcast_in_dim.31), channel_id=1, replica_groups=mesh['x'=4,'z'=16,'y'=4,'core'=2] {'x'}, dimensions={0} | all-to-all | bytes 1572864 | tf_op jit(solution)/shard_map/all_to_all | solution.py:57
  115.6 2.3 %reduce.2 = f32[4,49152]{1,0:T(4,128)S(1)} reduce(f32[4,1,49152]{2,1,0:T(1,128)S(1)} %all_to_all.34, f32[]{:T(128)} %constant.18), dimensions={1}, to_apply=%all_to_all.25.reduce_sub_computation | reduce | bytes 1572868 | tf_op jit(solution)/shard_map/all_to_all | solution.py:57
  119.2 26.8 %shard_map.68 = f32[256,512]{1,0:T(8,128)} custom-call(f32[256,256]{1,0:T(8,128)} %slice.20.g_ref), custom_call_target="tpu_custom_call" | custom-call | tf_op jit(solution)/shard_map/pallas_call | solution.py:95
  146.0 2.4 %fusion = f32[1,256,512]{2,1,0:T(8,128)} fusion(f32[256,768]{1,0:T(8,128)S(1)} %reshape_reshape.4, f32[256,512]{1,0:T(8,128)} %shard_map.68), kind=kOutput, calls=%fused_computation.2 | convolution fusion | flops 402784256 | bytes 1310720 | tf_op jit(solution)/shard_map/dot_general | solution.py:143
  148.4 1.3 fusion.1
  (29 shorter events, 5.9 us)
Async XLA Ops:
  0.6 13.2 %copy-start = (bf16[512,256]{1,0:T(8,128)(2,1)S(1)}, bf16[512,256]{1,0:T(8,128)(2,1)}, u32[]{:S(2)}) copy-start(bf16[512,256]{1,0:T(8,128)(2,1)} %param.6) | copy-start | bytes 786436
  0.6 0.7 copy-start.4
  0.7 12.1 %copy-start.3 = (bf16[256,512]{1,0:T(8,128)(2,1)S(1)}, bf16[256,512]{1,0:T(8,128)(2,1)}, u32[]{:S(2)}) copy-start(bf16[256,512]{1,0:T(8,128)(2,1)} %param.4) | copy-start | bytes 786436
  1.4 4.9 %collective-permute-start.1 = (f32[256]{0:T(256)S(1)}, f32[256]{0:T(256)S(1)}, u32[]{:S(2)}, u32[]{:S(2)}) collective-permute-start(f32[256]{0:T(256)S(1)} %bitcast.21), channel_id=1, source_target_pairs={{0,1},{1,2},{2,3},{3,4},{4,5},{5,6},{6,7},{8,9},{9,10},{10,11},{11... | collective-permute-start | bytes 3080 | tf_op jit(solution)/shard_map/ppermute | solution.py:20
  4.1 7.6 %collective-permute-start = (bf16[256,128]{1,0:T(8,128)(2,1)S(1)}, bf16[256,128]{1,0:T(8,128)(2,1)S(1)}, u32[]{:S(2)}, u32[]{:S(2)}) collective-permute-start(bf16[256,128]{1,0:T(8,128)(2,1)S(1)} %slice.15), channel_id=1, source_target_pairs={{0,1},{1,2},{2,3},{3,4},{4,5},{5,6},{6,7},{8,9},{9,10},{10,11},{11... | collective-permute-start | bytes 196616 | tf_op jit(solution)/shard_map/ppermute | solution.py:20
  6.3 5.5 %collective-permute-start.2 = (f32[256]{0:T(256)S(1)}, f32[256]{0:T(256)S(1)}, u32[]{:S(2)}, u32[]{:S(2)}) collective-permute-start(f32[256]{0:T(256)S(1)} %mul.39), channel_id=1, source_target_pairs={{0,2},{1,3},{2,4},{3,5},{4,6},{5,7},{8,10},{9,11},{10,12},{11,13},... | collective-permute-start | bytes 3080 | tf_op jit(solution)/shard_map/ppermute | solution.py:20
  11.7 1.0 copy-start.5
  12.7 0.8 copy-start.2
  14.1 7.7 %collective-permute-start.3 = (f32[256,256]{0,1:T(8,128)S(1)}, f32[256,256]{0,1:T(8,128)S(1)}, u32[]{:S(2)}, u32[]{:S(2)}) collective-permute-start(f32[256,256]{0,1:T(8,128)S(1)} %fusion.42), channel_id=1, source_target_pairs={{0,1},{1,2},{2,3},{3,4},{4,5},{5,6},{6,7},{8,9},{9,10},{10,11},{11... | collective-permute-start | bytes 786440 | tf_op jit(solution)/shard_map/ppermute | solution.py:20
  21.9 8.3 %collective-permute-start.4 = (f32[256,256]{0,1:T(8,128)S(1)}, f32[256,256]{0,1:T(8,128)S(1)}, u32[]{:S(2)}, u32[]{:S(2)}) collective-permute-start(f32[256,256]{0,1:T(8,128)S(1)} %multiply_add_fusion.2), channel_id=1, source_target_pairs={{0,2},{1,3},{2,4},{3,5},{4,6},{5,7},{8,10},{9,11},{10,12},{11,13},... | collective-permute-start | bytes 786440 | tf_op jit(solution)/shard_map/ppermute | solution.py:20
  30.3 9.8 %collective-permute-start.5 = (f32[256,256]{0,1:T(8,128)S(1)}, f32[256,256]{0,1:T(8,128)S(1)}, u32[]{:S(2)}, u32[]{:S(2)}) collective-permute-start(f32[256,256]{0,1:T(8,128)S(1)} %multiply_add_fusion.1), channel_id=1, source_target_pairs={{0,4},{1,5},{2,6},{3,7},{8,12},{9,13},{10,14},{11,15},{16,20},{17,... | collective-permute-start | bytes 786440 | tf_op jit(solution)/shard_map/ppermute | solution.py:20
  146.0 2.4 %copy-start.1 = (f32[256,512]{1,0:T(8,128)S(1)}, f32[256,512]{1,0:T(8,128)}, u32[]{:S(2)}) copy-start(f32[256,512]{1,0:T(8,128)} %shard_map.68) | copy-start | bytes 1572868

commit v15 on v10

--- a/solution.py
+++ b/solution.py
@@ -105,13 +105,13 @@
     inner, carry = band_blocks(coefs)
     nblocks = frame_count // BLOCK
     zero = jnp.zeros((BLOCK, BLOCK), jnp.bfloat16)
-    main_band = jnp.block(
-        [[inner if j == i else (carry if j == i + 1 else zero) for j in range(nblocks)] for i in range(nblocks)]
+    band = jnp.block(
+        [[carry if j == 0 else zero for j in range(nblocks)]]
+        + [[inner if j == i else (carry if j == i + 1 else zero) for j in range(nblocks)] for i in range(nblocks)]
     )
     history = shifted(frames[:, frame_count - BLOCK :], BATCH, 1)
-    main = jnp.dot(frames, main_band, preferred_element_type=jnp.float32)
-    edge = jnp.dot(history, carry, preferred_element_type=jnp.float32)
-    filtered = (main + jnp.pad(edge, ((0, 0), (0, frame_count - BLOCK)))).astype(jnp.bfloat16)
+    extended = jnp.concatenate([history, frames], axis=1)
+    filtered = jnp.dot(extended, band, preferred_element_type=jnp.float32).astype(jnp.bfloat16)
     sketched = jnp.dot(filtered, sketch_matrix, preferred_element_type=jnp.float32)
 
     factors = []

time: 147 us -> 146 us (level)
  local copies, waits for them, and re-layouts: 4.24 us -> 5.87 us
    unnamed x12 -> x14, local copies, waits for them, and re-layouts: 0.75 us -> 2.41 us
  transfers between devices with their start and end apart: 6 -> 6, of which waited for: 6 -> 5; matrix products, arithmetic and copies ran while one was open for 1% -> 0% of each run, Pallas kernels for 1% -> 1%
where the time goes in v15:
time: 146 us; the launch traced here: 145 us
  blocking collectives  72.3 us (50%)
  Pallas kernels  28.4 us (19%)
  waiting for transfers between devices  18 us (12%)
  starting transfers between devices  9.63 us (7%)
  local copies, waits for them, and re-layouts  5.87 us (4%)
  matrix products  4.98 us (3%)
  other arithmetic  4.53 us (3%)
    all_to_all x2, blocking collectives, scatter_sum(): got = lax.all_to_all(flat.reshape(count, -1), axis, 0, 0, tiled=True)  42.3 us
    all_to_all x2, blocking collectives, gather_back(): return lax.all_to_all(spread, axis, 0, 0, tiled=True).reshape(-1)  30.1 us
    pallas_call x1, Pallas kernels, factor_block(): pl.pallas_call(chol_kernel, out_shape=jax.ShapeDtypeStruct((n, 2 * n), jn...  26.8 us
    ppermute x6, waiting for transfers between devices, shifted(): return lax.ppermute(x, axis, pairs)  18 us
    ppermute x6, starting transfers between devices, shifted(): return lax.ppermute(x, axis, pairs)  9.63 us
  transfers between devices with their start and end apart: 6, of which 5 were waited for; matrix products, arithmetic and copies ran while one was open for 0% of the time, Pallas kernels for 1%

profile of v15, /device:TPU:24, one launch (start us, length us, event | category | flops | bytes accessed | tf_op | source)
XLA Modules:
  0.0 144.6 jit_solution(10753784263038776875)
XLA Ops:
  0.7 0.9 slice.15
  1.5 1.9 %collective-permute-start = (bf16[256,128]{1,0:T(8,128)(2,1)S(1)}, bf16[256,128]{1,0:T(8,128)(2,1)S(1)}, u32[]{:S(2)}, u32[]{:S(2)}) collective-permute-start(bf16[256,128]{1,0:T(8,128)(2,1)S(1)} %slice.15), channel_id=1, source_target_pairs={{0,1},{1,2},{2,3},{3,4},{4,5},{5,6},{6,7},{8,9},{9,10},{10,11},{11... | collective-permute-start | bytes 196616 | tf_op jit(solution)/shard_map/ppermute | solution.py:20
  4.0 1.6 %shard_map.67 = (bf16[128,128]{1,0:T(8,128)(2,1)}, bf16[128,128]{1,0:T(8,128)(2,1)}) custom-call(f32[63]{0:T(128)} %convert_convert_fusion.coefs_ref), custom_call_target="tpu_custom_call" | custom-call | tf_op jit(solution)/shard_map/pallas_call | solution.py:40
  7.2 0.9 copy-done.4
  8.7 1.9 %collective-permute-start.1 = (f32[256,256]{1,0:T(8,128)S(1)}, f32[256,256]{1,0:T(8,128)S(1)}, u32[]{:S(2)}, u32[]{:S(2)}) collective-permute-start(f32[256,256]{1,0:T(8,128)S(1)} %fusion.25), channel_id=1, source_target_pairs={{0,1},{1,2},{2,3},{3,4},{4,5},{5,6},{6,7},{8,9},{9,10},{10,11},{11... | collective-permute-start | bytes 786440 | tf_op jit(solution)/shard_map/ppermute | solution.py:20
  10.6 5.8 %collective-permute-done.1 = f32[256,256]{1,0:T(8,128)S(1)} collective-permute-done((f32[256,256]{1,0:T(8,128)S(1)}, f32[256,256]{1,0:T(8,128)S(1)}, u32[]{:S(2)}, u32[]{:S(2)}) %collective-permute-start.1) | collective-permute-done | bytes 262176 | tf_op jit(solution)/shard_map/ppermute | solution.py:20
  16.4 1.3 collective-permute-start.3
  17.7 1.9 %collective-permute-start.2 = (f32[256]{0:T(256)S(1)}, f32[256]{0:T(256)S(1)}, u32[]{:S(2)}, u32[]{:S(2)}) collective-permute-start(f32[256]{0:T(256)S(1)} %bitcast.17), channel_id=1, source_target_pairs={{0,1},{1,2},{2,3},{3,4},{4,5},{5,6},{6,7},{8,9},{9,10},{10,11},{11... | collective-permute-start | bytes 3080 | tf_op jit(solution)/shard_map/ppermute | solution.py:20
  19.7 3.0 %collective-permute-done.2 = f32[256]{0:T(256)S(1)} collective-permute-done((f32[256]{0:T(256)S(1)}, f32[256]{0:T(256)S(1)}, u32[]{:S(2)}, u32[]{:S(2)}) %collective-permute-start.2) | collective-permute-done | bytes 1056 | tf_op jit(solution)/shard_map/ppermute | solution.py:20
  22.6 2.1 %collective-permute-done.3 = f32[256,256]{1,0:T(8,128)S(1)} collective-permute-done((f32[256,256]{1,0:T(8,128)S(1)}, f32[256,256]{1,0:T(8,128)S(1)}, u32[]{:S(2)}, u32[]{:S(2)}) %collective-permute-start.3) | collective-permute-done | bytes 262176 | tf_op jit(solution)/shard_map/ppermute | solution.py:20
  24.8 1.3 collective-permute-start.5
  26.1 1.3 collective-permute-start.4
  27.4 4.2 %collective-permute-done.4 = f32[256]{0:T(256)S(1)} collective-permute-done((f32[256]{0:T(256)S(1)}, f32[256]{0:T(256)S(1)}, u32[]{:S(2)}, u32[]{:S(2)}) %collective-permute-start.4) | collective-permute-done | bytes 1056 | tf_op jit(solution)/shard_map/ppermute | solution.py:20
  31.5 3.0 %collective-permute-done.5 = f32[256,256]{1,0:T(8,128)S(1)} collective-permute-done((f32[256,256]{1,0:T(8,128)S(1)}, f32[256,256]{1,0:T(8,128)S(1)}, u32[]{:S(2)}, u32[]{:S(2)}) %collective-permute-start.5) | collective-permute-done | bytes 262176 | tf_op jit(solution)/shard_map/ppermute | solution.py:20
  34.6 0.8 fusion.2
  35.4 0.8 all_to_all.26
  36.2 13.6 %all_to_all.31 = f32[4,1,49152]{2,1,0:T(1,128)S(1)} all-to-all(f32[4,1,49152]{2,1,0:T(1,128)S(1)} %all_to_all.26), channel_id=1, replica_groups=mesh['x'=4,'z'=16,'y'=4,'core'=2] {'x'}, dimensions={0} | all-to-all | bytes 1572864 | tf_op jit(solution)/shard_map/all_to_all | solution.py:50
  50.5 28.7 %all_to_all.32 = f32[16,1,3072]{2,1,0:T(1,128)S(1)} all-to-all(f32[16,1,3072]{2,1,0:T(1,128)S(1)} %bitcast.14), channel_id=1, replica_groups=mesh['x'=4,'z'=16,'y'=4,'core'=2] {'z'}, dimensions={0} | all-to-all | bytes 393216 | tf_op jit(solution)/shard_map/all_to_all | solution.py:50
  79.4 18.2 %all_to_all.33 = f32[16,1,3072]{2,1,0:T(1,128)S(1)} all-to-all(f32[16,1,3072]{2,1,0:T(1,128)S(1)} %broadcast_in_dim.28), channel_id=1, replica_groups=mesh['x'=4,'z'=16,'y'=4,'core'=2] {'z'}, dimensions={0} | all-to-all | bytes 393216 | tf_op jit(solution)/shard_map/all_to_all | solution.py:57
  98.0 11.9 %all_to_all.34 = f32[4,1,49152]{2,1,0:T(1,128)S(1)} all-to-all(f32[4,1,49152]{2,1,0:T(1,128)S(1)} %broadcast_in_dim.30), channel_id=1, replica_groups=mesh['x'=4,'z'=16,'y'=4,'core'=2] {'x'}, dimensions={0} | all-to-all | bytes 1572864 | tf_op jit(solution)/shard_map/all_to_all | solution.py:57
  109.9 2.3 %reduce.2 = f32[4,49152]{1,0:T(4,128)S(1)} reduce(f32[4,1,49152]{2,1,0:T(1,128)S(1)} %all_to_all.34, f32[]{:T(128)} %constant.14), dimensions={1}, to_apply=%all_to_all.25.reduce_sub_computation | reduce | bytes 1572868 | tf_op jit(solution)/shard_map/all_to_all | solution.py:57
  113.4 26.8 %shard_map.68 = f32[256,512]{1,0:T(8,128)} custom-call(f32[256,256]{1,0:T(8,128)} %slice.20.g_ref), custom_call_target="tpu_custom_call" | custom-call | tf_op jit(solution)/shard_map/pallas_call | solution.py:95
  140.3 2.4 %fusion = f32[1,256,512]{2,1,0:T(8,128)} fusion(f32[256,768]{1,0:T(8,128)S(1)} %reshape_reshape.4, f32[256,512]{1,0:T(8,128)} %shard_map.68), kind=kOutput, calls=%fused_computation.1 | convolution fusion | flops 402784256 | bytes 1310720 | tf_op jit(solution)/shard_map/dot_general | solution.py:141
  142.7 1.1 fusion.1
  (35 shorter events, 6.2 us)
Async XLA Ops:
  0.6 7.8 %copy-start = (bf16[512,256]{1,0:T(8,128)(2,1)S(1)}, bf16[512,256]{1,0:T(8,128)(2,1)}, u32[]{:S(2)}) copy-start(bf16[512,256]{1,0:T(8,128)(2,1)} %param.6) | copy-start | bytes 786436
  0.6 2.8 %copy-start.6 = (s32[63]{0:T(128)S(1)}, s32[63]{0:T(128)}, u32[]{:S(2)}) copy-start(s32[63]{0:T(128)} %param.5) | copy-start | bytes 760
  1.5 5.6 %collective-permute-start = (bf16[256,128]{1,0:T(8,128)(2,1)S(1)}, bf16[256,128]{1,0:T(8,128)(2,1)S(1)}, u32[]{:S(2)}, u32[]{:S(2)}) collective-permute-start(bf16[256,128]{1,0:T(8,128)(2,1)S(1)} %slice.15), channel_id=1, source_target_pairs={{0,1},{1,2},{2,3},{3,4},{4,5},{5,6},{6,7},{8,9},{9,10},{10,11},{11... | collective-permute-start | bytes 196616 | tf_op jit(solution)/shard_map/ppermute | solution.py:20
  5.6 0.8 copy-start.3
  6.3 0.8 copy-start.2
  7.1 1.0 copy-start.4
  8.7 7.7 %copy-start.5 = (f32[1,256]{1,0:T(1,128)S(1)}, f32[1,256]{1,0:T(1,128)}, u32[]{:S(2)}) copy-start(f32[1,256]{1,0:T(1,128)} %param.7) | copy-start | bytes 3076
  8.7 7.7 %collective-permute-start.1 = (f32[256,256]{1,0:T(8,128)S(1)}, f32[256,256]{1,0:T(8,128)S(1)}, u32[]{:S(2)}, u32[]{:S(2)}) collective-permute-start(f32[256,256]{1,0:T(8,128)S(1)} %fusion.25), channel_id=1, source_target_pairs={{0,1},{1,2},{2,3},{3,4},{4,5},{5,6},{6,7},{8,9},{9,10},{10,11},{11... | collective-permute-start | bytes 786440 | tf_op jit(solution)/shard_map/ppermute | solution.py:20
  16.4 8.3 %collective-permute-start.3 = (f32[256,256]{1,0:T(8,128)S(1)}, f32[256,256]{1,0:T(8,128)S(1)}, u32[]{:S(2)}, u32[]{:S(2)}) collective-permute-start(f32[256,256]{1,0:T(8,128)S(1)} %multiply_add_fusion.2), channel_id=1, source_target_pairs={{0,2},{1,3},{2,4},{3,5},{4,6},{5,7},{8,10},{9,11},{10,12},{11,13},... | collective-permute-start | bytes 786440 | tf_op jit(solution)/shard_map/ppermute | solution.py:20
  17.7 4.9 %collective-permute-start.2 = (f32[256]{0:T(256)S(1)}, f32[256]{0:T(256)S(1)}, u32[]{:S(2)}, u32[]{:S(2)}) collective-permute-start(f32[256]{0:T(256)S(1)} %bitcast.17), channel_id=1, source_target_pairs={{0,1},{1,2},{2,3},{3,4},{4,5},{5,6},{6,7},{8,9},{9,10},{10,11},{11... | collective-permute-start | bytes 3080 | tf_op jit(solution)/shard_map/ppermute | solution.py:20
  24.8 9.8 %collective-permute-start.5 = (f32[256,256]{1,0:T(8,128)S(1)}, f32[256,256]{1,0:T(8,128)S(1)}, u32[]{:S(2)}, u32[]{:S(2)}) collective-permute-start(f32[256,256]{1,0:T(8,128)S(1)} %multiply_add_fusion.1), channel_id=1, source_target_pairs={{0,4},{1,5},{2,6},{3,7},{8,12},{9,13},{10,14},{11,15},{16,20},{17,... | collective-permute-start | bytes 786440 | tf_op jit(solution)/shard_map/ppermute | solution.py:20
  26.1 5.5 %collective-permute-start.4 = (f32[256]{0:T(256)S(1)}, f32[256]{0:T(256)S(1)}, u32[]{:S(2)}, u32[]{:S(2)}) collective-permute-start(f32[256]{0:T(256)S(1)} %mul.44), channel_id=1, source_target_pairs={{0,2},{1,3},{2,4},{3,5},{4,6},{5,7},{8,10},{9,11},{10,12},{11,13},... | collective-permute-start | bytes 3080 | tf_op jit(solution)/shard_map/ppermute | solution.py:20
  140.3 2.4 %copy-start.1 = (f32[256,512]{1,0:T(8,128)S(1)}, f32[256,512]{1,0:T(8,128)}, u32[]{:S(2)}) copy-start(f32[256,512]{1,0:T(8,128)} %shard_map.68) | copy-start | bytes 1572868
